TPU v7x, 32 devices: a whole 2x2x4 slice. The times are simulated.
32 devices in a mesh: parts: 2 (over y), seq: 4 (over z), lat: 4 (over x, core).
Axes of the slice: x: 2, y: 2, z: 4, core: 2. Of those that a mesh axis runs over, the one named last changes fastest.
Arguments:
- layer_input: bfloat16 [8, 2048, 1024], P(('parts', 'lat'), 'seq'), parts along dimension 0, may hold values from -6 to 6
- query_rows: bfloat16 [8, 2048, 1024], P(('parts', 'lat'), 'seq'), parts along dimension 0, may hold values from -8 to 8, as said below
- key_rows: bfloat16 [8, 2048, 256], P(('parts', 'lat'), 'seq'), parts along dimension 0, may hold values from -8 to 8, as said below
- value_rows: bfloat16 [8, 2048, 256], P(('parts', 'lat'), 'seq'), parts along dimension 0, may hold values from -6 to 6
- saved_output: bfloat16 [8, 2048, 1024], P(('parts', 'lat'), 'seq'), parts along dimension 0, may hold values from -6 to 6
- output_grad: bfloat16 [8, 2048, 1024], P(('parts', 'lat'), 'seq'), parts along dimension 0, may hold values from -96 to 96
- weight_query: bfloat16 [1024, 1024], replicated, may hold values from -0.1875 to 0.1875
- weight_key: bfloat16 [1024, 256], replicated, may hold values from -0.1875 to 0.1875
- weight_value: bfloat16 [1024, 256], replicated, may hold values from -0.1875 to 0.1875
Outputs:
- input_grad: bfloat16 [8, 2048, 1024], P(('parts', 'lat'), 'seq'), parts along dimension 0
- query_weight_grad: float32 [2048, 1024], P(('parts', 'seq', 'lat')), parts along dimension 0
- key_weight_grad: float32 [2048, 256], P(('parts', 'seq', 'lat')), parts along dimension 0
- value_weight_grad: float32 [2048, 256], P(('parts', 'seq', 'lat')), parts along dimension 0
There are 2 independent parts, one for each index of `parts`. A program takes and returns all parts, laid end to end along the dimension named above; an argument that names none is the same for every part. Nothing has to cross between parts.
Inputs may be any that keep to these rules, and one draw needn't show every extreme that they name: `query_rows`: saved queries of the layer. `key_rows`: saved keys of the layer.
All inputs are finite; a program needn't handle non-finite values.
Results may differ from a plain program's by a relative error of at most 0.0055.
Values may be sent and summed in bfloat16 or wider, within the bound.
No kernel may reach another device: no remote copies, remote signals or barrier semaphores. Data moves between devices by JAX's collectives and lax.ppermute only.
A program may use at most 128 MiB of HBM per device.

v0:
```python
import jax
import jax.numpy as jnp
from jax import lax
from jax.sharding import PartitionSpec as P

HEADS = 16
HEAD_DIM = 64
KV_HEADS = 4
WINDOW = 512


def shifted(block, axis, distance):
    devices = range(lax.axis_size(axis))
    route = [((i - distance) % len(devices), i) for i in devices]
    return lax.ppermute(block, axis, route)


def group_terms(query_part, output_part, dout_part, key_part, value_part):
    rows = query_part.shape[0]
    span = key_part.shape[0]
    ratio = HEADS // KV_HEADS
    scale = HEAD_DIM ** (-0.5)
    queries3 = query_part.reshape(rows, ratio, HEAD_DIM)
    outputs3 = output_part.reshape(rows, ratio, HEAD_DIM)
    douts3 = dout_part.reshape(rows, ratio, HEAD_DIM)
    scores = (
        jnp.einsum("qrd,kd->rqk", queries3, key_part, preferred_element_type=jnp.float32) * scale
    )
    row_index = jnp.arange(rows, dtype=jnp.int32)[:, None]
    col_index = jnp.arange(span, dtype=jnp.int32)[None, :]
    linked = (col_index > row_index) & (col_index <= row_index + WINDOW)
    scores = jnp.where(linked[None], scores, -jnp.inf)
    peak = jnp.max(scores, axis=-1, keepdims=True)
    raised = jnp.exp(scores - peak)
    probs = raised / jnp.sum(raised, axis=-1, keepdims=True)
    probs_low = probs.astype(jnp.bfloat16)
    dprobs = jnp.einsum("qrd,kd->rqk", douts3, value_part, preferred_element_type=jnp.float32)
    delta = jnp.sum(douts3.astype(jnp.float32) * outputs3.astype(jnp.float32), axis=-1).T[
        :, :, None
    ]
    dscores = (probs * (dprobs - delta)).astype(jnp.bfloat16)
    query_grad = (
        jnp.einsum("rqk,kd->qrd", dscores, key_part, preferred_element_type=jnp.float32) * scale
    )
    key_grad = (
        jnp.einsum("rqk,qrd->kd", dscores, queries3, preferred_element_type=jnp.float32) * scale
    )
    value_grad = jnp.einsum("rqk,qrd->kd", probs_low, douts3, preferred_element_type=jnp.float32)
    return (query_grad.reshape(rows, ratio * HEAD_DIM), key_grad, value_grad)


def body(
    layer_input,
    query_rows,
    key_rows,
    value_rows,
    saved_output,
    output_grad,
    weight_query,
    weight_key,
    weight_value,
):
    inputs = layer_input[0]
    queries = query_rows[0]
    keys_own = key_rows[0]
    values_own = value_rows[0]
    outputs_own = saved_output[0]
    douts = output_grad[0]
    tokens = queries.shape[0]
    kv_width = keys_own.shape[1]
    width = HEADS // KV_HEADS * HEAD_DIM
    block = min(512, tokens)
    tail_pair = jnp.stack([keys_own, values_own])
    prior_pair = shifted(tail_pair, "seq", 1)
    ext_keys = jnp.concatenate([prior_pair[0], keys_own], axis=0)
    ext_values = jnp.concatenate([prior_pair[1], values_own], axis=0)
    key_acc = jnp.zeros((tokens + WINDOW, kv_width), jnp.float32)
    value_acc = jnp.zeros((tokens + WINDOW, kv_width), jnp.float32)
    query_list = []
    key_list = []
    value_list = []
    for group in range(KV_HEADS):
        cols = slice(group * width, (group + 1) * width)
        kv_cols = slice(group * HEAD_DIM, (group + 1) * HEAD_DIM)
        q_term, k_term, v_term = group_terms(
            queries[0:block, cols],
            outputs_own[0:block, cols],
            douts[0:block, cols],
            ext_keys[0 : block + WINDOW, kv_cols],
            ext_values[0 : block + WINDOW, kv_cols],
        )
        query_list.append(q_term)
        key_list.append(k_term)
        value_list.append(v_term)
    query_blocks = jnp.concatenate(query_list, 1).astype(jnp.bfloat16)
    key_acc = key_acc.at[0 : block + WINDOW].add(jnp.concatenate(key_list, 1))
    value_acc = value_acc.at[0 : block + WINDOW].add(jnp.concatenate(value_list, 1))
    front_pair = jnp.stack([key_acc[:WINDOW], value_acc[:WINDOW]])
    returned = shifted(front_pair, "seq", -1)
    key_grad = key_acc[WINDOW:].at[tokens - WINDOW :].add(returned[0]).astype(jnp.bfloat16)
    value_grad = value_acc[WINDOW:].at[tokens - WINDOW :].add(returned[1]).astype(jnp.bfloat16)
    contract_cols = (((1,), (1,)), ((), ()))
    summed = lax.dot_general(
        query_blocks, weight_query, contract_cols, preferred_element_type=jnp.float32
    )
    summed = summed + lax.dot_general(
        key_grad, weight_key, contract_cols, preferred_element_type=jnp.float32
    )
    summed = summed + lax.dot_general(
        value_grad, weight_value, contract_cols, preferred_element_type=jnp.float32
    )
    input_grad = summed.astype(jnp.bfloat16)[None]
    all_grads = jnp.concatenate([query_blocks, key_grad, value_grad], axis=1)
    owned = lax.psum_scatter(
        lax.dot_general(
            inputs, all_grads, (((0,), (0,)), ((), ())), preferred_element_type=jnp.float32
        ),
        ("seq", "lat"),
        scatter_dimension=0,
        tiled=True,
    )
    q_width = HEADS * HEAD_DIM
    query_weight_grad = owned[:, :q_width]
    key_weight_grad = owned[:, q_width : q_width + kv_width]
    value_weight_grad = owned[:, q_width + kv_width :]
    return (input_grad, query_weight_grad, key_weight_grad, value_weight_grad)


def solution(mesh):
    placed = (
        P(("parts", "lat"), "seq", None),
        P(("parts", "lat"), "seq", None),
        P(("parts", "lat"), "seq", None),
        P(("parts", "lat"), "seq", None),
        P(("parts", "lat"), "seq", None),
        P(("parts", "lat"), "seq", None),
        P(),
        P(),
        P(),
    )
    return jax.shard_map(
        body,
        mesh=mesh,
        in_specs=placed,
        out_specs=(
            P(("parts", "lat"), "seq", None),
            P(("parts", "seq", "lat"), None),
            P(("parts", "seq", "lat"), None),
            P(("parts", "seq", "lat"), None),
        ),
        check_vma=False,
    )
```

profile of v0, /device:TPU:0, one launch (start us, length us, event | category | flops | bytes accessed | tf_op | source)
XLA Modules:
  0.0 250.0 jit_solution(11327988300216209073)
XLA Ops:
  8.5 1.8 copy.45
  12.1 3.1 %collective-permute-start = (bf16[2,512,256]{1,2,0:T(8,128)(2,1)}, bf16[2,512,256]{1,2,0:T(8,128)(2,1)}, u32[]{:S(2)}, u32[]{:S(2)}) collective-permute-start(bf16[2,512,256]{1,2,0:T(8,128)(2,1)} %pad_maximum_fusion.3), channel_id=1, source_target_pairs={{12,0},{0,4},{4,8},{8,12},{13,1},{1,5},{5,9},{9,13},{14,2},{2,6},{... | collective-permute-start | bytes 1572872 | tf_op jit(solution)/shard_map/ppermute | solution.py:15
  15.2 2.2 fusion.128
  17.4 1.8 copy.60
  19.2 1.8 copy.56
  22.8 1.8 copy.47
  27.4 1.8 copy.57
  32.8 2.4 slice_convert_fusion
  36.6 2.0 copy.54
  38.7 2.0 copy.50
  48.7 6.7 %fusion.131 = (f32[4,512]{1,0:T(4,128)}, f32[4,512,1024]{1,2,0:T(8,128)}) fusion(pred[512,1024]{0,1:T(8,128)(4,1)} %fusion.36, bf16[512,4,64]{0,2,1:T(8,128)(2,1)S(1)} %bitcast.269, bf16[512,256]{0,1:T(8,128)(2,1)S(1)} %get-tuple-element.109, bf16[512,256]{0,1:T(8,128)(2,1)S(1)} %bitcast.248), kind=kOutput, calls=%fused_computation.165 | convolution fusion | flops 277087232 | bytes 9707520 | tf_op jit(solution)/shard_map/sub | solution.py:34
  55.4 5.6 %fusion.46 = f32[1024,64]{0,1:T(8,128)} fusion(bf16[512,4,64]{0,2,1:T(8,128)(2,1)S(1)} %bitcast.273, f32[4,512,1024]{1,2,0:T(8,128)} %get-tuple-element.113, f32[4,512]{1,0:T(4,128)} %get-tuple-element.112), kind=kOutput, calls=%fused_computation.74 | convolution fusion | flops 272629760 | bytes 8921088 | tf_op jit(solution)/shard_map/rqk,qrd->kd/dot_general | solution.py:48
  65.6 6.6 %fusion.136 = (f32[4,512]{1,0:T(4,128)}, f32[4,512,1024]{1,2,0:T(8,128)}) fusion(pred[512,1024]{0,1:T(8,128)(4,1)} %fusion.36, bf16[512,4,64]{0,2,1:T(8,128)(2,1)S(1)} %bitcast.265, bf16[512,256]{0,1:T(8,128)(2,1)S(1)} %get-tuple-element.109, bf16[512,256]{0,1:T(8,128)(2,1)S(1)} %bitcast.250), kind=kOutput, calls=%fused_computation.166 | convolution fusion | flops 277087232 | bytes 9707520 | tf_op jit(solution)/shard_map/sub | solution.py:34
  72.2 5.6 %fusion.49 = f32[1024,64]{0,1:T(8,128)} fusion(bf16[512,4,64]{0,2,1:T(8,128)(2,1)S(1)} %bitcast.271, f32[4,512,1024]{1,2,0:T(8,128)} %get-tuple-element.115, f32[4,512]{1,0:T(4,128)} %get-tuple-element.114), kind=kOutput, calls=%fused_computation.75 | convolution fusion | flops 272629760 | bytes 8921088 | tf_op jit(solution)/shard_map/rqk,qrd->kd/dot_general | solution.py:48
  82.4 6.5 %fusion.141 = (f32[4,512]{1,0:T(4,128)}, f32[4,512,1024]{1,2,0:T(8,128)}) fusion(pred[512,1024]{0,1:T(8,128)(4,1)} %fusion.36, bf16[512,4,64]{0,2,1:T(8,128)(2,1)S(1)} %bitcast.259, bf16[512,256]{0,1:T(8,128)(2,1)S(1)} %get-tuple-element.109, bf16[512,256]{0,1:T(8,128)(2,1)S(1)} %bitcast.252), kind=kOutput, calls=%fused_computation.167 | convolution fusion | flops 277087232 | bytes 9707520 | tf_op jit(solution)/shard_map/sub | solution.py:34
  89.0 5.6 %fusion.52 = f32[1024,64]{0,1:T(8,128)} fusion(bf16[512,4,64]{0,2,1:T(8,128)(2,1)} %bitcast.267, f32[4,512,1024]{1,2,0:T(8,128)} %get-tuple-element.117, f32[4,512]{1,0:T(4,128)} %get-tuple-element.116), kind=kOutput, calls=%fused_computation.76 | convolution fusion | flops 272629760 | bytes 8921088 | tf_op jit(solution)/shard_map/rqk,qrd->kd/dot_general | solution.py:48
  96.5 2.0 copy-done.1
  99.8 7.3 %fusion.146 = (f32[4,512]{1,0:T(4,128)S(1)}, f32[4,512,1024]{1,2,0:T(8,128)}) fusion(pred[512,1024]{0,1:T(8,128)(4,1)} %fusion.36, bf16[1024,64,1]{0,1,2:T(8,128)(2,1)S(1)} %fusion.97, bf16[512,4,64]{0,2,1:T(8,128)(2,1)} %bitcast.255), kind=kOutput, calls=%fused_computation.168 | convolution fusion | flops 276825088 | bytes 9314304 | tf_op jit(solution)/shard_map/sub | solution.py:34
  107.2 4.9 %fusion.55 = f32[1024,64]{0,1:T(8,128)S(1)} fusion(bf16[512,4,64]{0,2,1:T(8,128)(2,1)} %bitcast.263, f32[4,512,1024]{1,2,0:T(8,128)} %get-tuple-element.119, f32[4,512]{1,0:T(4,128)S(1)} %get-tuple-element.118), kind=kOutput, calls=%fused_computation.77 | convolution fusion | flops 272629760 | bytes 8921088 | tf_op jit(solution)/shard_map/rqk,qrd->kd/dot_general | solution.py:48
  116.4 2.1 collective-permute-start.1
  120.4 20.8 %collective-permute-done.1 = f32[2,512,256]{1,2,0:T(8,128)S(1)} collective-permute-done((f32[2,512,256]{1,2,0:T(8,128)S(1)}, f32[2,512,256]{1,2,0:T(8,128)S(1)}, u32[]{:S(2)}, u32[]{:S(2)}) %collective-permute-start.1) | collective-permute-done | bytes 1048608 | tf_op jit(solution)/shard_map/ppermute | solution.py:15
  142.0 4.5 %convolution_bitcast_fusion = f32[1024,1536]{0,1:T(8,128)} fusion(bf16[512,1536]{0,1:T(8,128)(2,1)S(1)} %get-tuple-element.92, bf16[1,512,1024]{2,1,0:T(8,128)(2,1)S(1)} %copy-done.35), kind=kOutput, calls=%fused_computation.28 | convolution fusion | flops 1610612736 | bytes 8912896 | tf_op jit(solution)/shard_map/dot_general | solution.py:115
  146.4 6.6 %copy.87 = f32[1024,1536]{1,0:T(8,128)} copy(f32[1024,1536]{0,1:T(8,128)} %convolution_bitcast_fusion) | data formatting | bytes 12582912
  157.4 82.6 %reduce-scatter.4.cloned.1.call-done = f32[64,1536]{1,0:T(8,128)} async-done(((f32[1024,1536]{1,0:T(8,128)}), f32[64,1536]{1,0:T(8,128)}) %reduce-scatter.4.cloned.1.call-update) | async-done | bytes 393232
  (132 shorter events, 47.3 us)
Async XLA Ops:
  7.2 145.9 %copy-start = (bf16[1024,1024]{1,0:T(8,128)(2,1)S(1)}, bf16[1024,1024]{1,0:T(8,128)(2,1)}, u32[]{:S(2)}) copy-start(bf16[1024,1024]{1,0:T(8,128)(2,1)} %param.31) | copy-start | bytes 6291460
  7.2 17.5 %copy-start.18 = (bf16[1,512,1024]{2,1,0:T(8,128)(2,1)S(1)}, bf16[1,512,1024]{2,1,0:T(8,128)(2,1)}, u32[]{:S(2)}) copy-start(bf16[1,512,1024]{2,1,0:T(8,128)(2,1)} %param.30) | copy-start | bytes 3145732
  7.2 232.8 %reduce-scatter.4.cloned.1.call-start = ((), (), s32[]{:S(2)}) async-start(), calls=%async_computation.1 | async-start | bytes 6684672
  12.1 35.4 %collective-permute-start = (bf16[2,512,256]{1,2,0:T(8,128)(2,1)}, bf16[2,512,256]{1,2,0:T(8,128)(2,1)}, u32[]{:S(2)}, u32[]{:S(2)}) collective-permute-start(bf16[2,512,256]{1,2,0:T(8,128)(2,1)} %pad_maximum_fusion.3), channel_id=1, source_target_pairs={{12,0},{0,4},{4,8},{8,12},{13,1},{1,5},{5,9},{9,13},{14,2},{2,6},{... | collective-permute-start | bytes 1572872 | tf_op jit(solution)/shard_map/ppermute | solution.py:15
  41.7 6.9 %copy-start.14 = (bf16[512,256]{0,1:T(8,128)(2,1)S(1)}, bf16[512,256]{0,1:T(8,128)(2,1)}, u32[]{:S(2)}) copy-start(bf16[512,256]{0,1:T(8,128)(2,1)} %copy.47) | copy-start | bytes 786436
  48.6 12.4 %copy-start.26 = (bf16[512,256]{0,1:T(8,128)(2,1)}, bf16[512,256]{0,1:T(8,128)(2,1)S(1)}, u32[]{:S(2)}) copy-start(bf16[512,256]{0,1:T(8,128)(2,1)S(1)} %get-tuple-element.108) | copy-start | bytes 786436
  48.7 6.7 %copy-start.17 = (bf16[512,256]{0,1:T(8,128)(2,1)S(1)}, bf16[512,256]{0,1:T(8,128)(2,1)}, u32[]{:S(2)}) copy-start(bf16[512,256]{0,1:T(8,128)(2,1)} %copy.49) | copy-start | bytes 786436
  55.4 5.7 %copy-start.34 = (f32[512,4]{0,1:T(4,128)S(1)}, f32[512,4]{0,1:T(4,128)}, u32[]{:S(2)}) copy-start(f32[512,4]{0,1:T(4,128)} %multiply_reduce_fusion.3) | copy-start | bytes 24580
  55.4 5.9 %copy-start.36 = (f32[4,512,1024]{1,2,0:T(8,128)S(1)}, f32[4,512,1024]{1,2,0:T(8,128)}, u32[]{:S(2)}) copy-start(f32[4,512,1024]{1,2,0:T(8,128)} %get-tuple-element.113) | copy-start | bytes 25165828
  55.4 5.9 %copy-start.40 = (f32[4,512]{1,0:T(4,128)S(1)}, f32[4,512]{1,0:T(4,128)}, u32[]{:S(2)}) copy-start(f32[4,512]{1,0:T(4,128)} %get-tuple-element.112) | copy-start | bytes 24580
  65.6 6.6 %copy-start.16 = (bf16[512,256]{0,1:T(8,128)(2,1)S(1)}, bf16[512,256]{0,1:T(8,128)(2,1)}, u32[]{:S(2)}) copy-start(bf16[512,256]{0,1:T(8,128)(2,1)} %copy.53) | copy-start | bytes 786436
  72.2 5.7 %copy-start.20 = (bf16[1,512,256]{1,2,0:T(8,128)(2,1)S(1)}, bf16[1,512,256]{1,2,0:T(8,128)(2,1)}, u32[]{:S(2)}) copy-start(bf16[1,512,256]{1,2,0:T(8,128)(2,1)} %copy.45) | copy-start | bytes 786436
  72.2 5.7 %copy-start.27 = (bf16[512,256]{0,1:T(8,128)(2,1)S(1)}, bf16[512,256]{0,1:T(8,128)(2,1)}, u32[]{:S(2)}) copy-start(bf16[512,256]{0,1:T(8,128)(2,1)} %copy-done.26) | copy-start | bytes 786436
  72.2 5.7 %copy-start.33 = (f32[512,4]{0,1:T(4,128)S(1)}, f32[512,4]{0,1:T(4,128)}, u32[]{:S(2)}) copy-start(f32[512,4]{0,1:T(4,128)} %multiply_reduce_fusion.2) | copy-start | bytes 24580
  72.2 6.0 %copy-start.37 = (f32[4,512,1024]{1,2,0:T(8,128)S(1)}, f32[4,512,1024]{1,2,0:T(8,128)}, u32[]{:S(2)}) copy-start(f32[4,512,1024]{1,2,0:T(8,128)} %get-tuple-element.115) | copy-start | bytes 25165828
  72.2 6.0 %copy-start.41 = (f32[4,512]{1,0:T(4,128)S(1)}, f32[4,512]{1,0:T(4,128)}, u32[]{:S(2)}) copy-start(f32[4,512]{1,0:T(4,128)} %get-tuple-element.114) | copy-start | bytes 24580
  89.0 5.7 %copy-start.13 = (bf16[512,256]{0,1:T(8,128)(2,1)S(1)}, bf16[512,256]{0,1:T(8,128)(2,1)}, u32[]{:S(2)}) copy-start(bf16[512,256]{0,1:T(8,128)(2,1)} %copy.57) | copy-start | bytes 786436
  89.0 5.7 %copy-start.21 = (bf16[1,512,256]{1,2,0:T(8,128)(2,1)S(1)}, bf16[1,512,256]{1,2,0:T(8,128)(2,1)}, u32[]{:S(2)}) copy-start(bf16[1,512,256]{1,2,0:T(8,128)(2,1)} %copy.45) | copy-start | bytes 786436
  89.0 5.7 %copy-start.28 = (bf16[512,256]{0,1:T(8,128)(2,1)S(1)}, bf16[512,256]{0,1:T(8,128)(2,1)}, u32[]{:S(2)}) copy-start(bf16[512,256]{0,1:T(8,128)(2,1)} %copy-done.26) | copy-start | bytes 786436
  89.0 6.2 %copy-start.38 = (f32[4,512,1024]{1,2,0:T(8,128)S(1)}, f32[4,512,1024]{1,2,0:T(8,128)}, u32[]{:S(2)}) copy-start(f32[4,512,1024]{1,2,0:T(8,128)} %get-tuple-element.117) | copy-start | bytes 25165828
  89.0 6.2 %copy-start.42 = (f32[4,512]{1,0:T(4,128)S(1)}, f32[4,512]{1,0:T(4,128)}, u32[]{:S(2)}) copy-start(f32[4,512]{1,0:T(4,128)} %get-tuple-element.116) | copy-start | bytes 24580
  107.2 6.1 %copy-start.39 = (f32[4,512,1024]{1,2,0:T(8,128)S(1)}, f32[4,512,1024]{1,2,0:T(8,128)}, u32[]{:S(2)}) copy-start(f32[4,512,1024]{1,2,0:T(8,128)} %get-tuple-element.119) | copy-start | bytes 25165828
  116.4 24.7 %collective-permute-start.1 = (f32[2,512,256]{1,2,0:T(8,128)S(1)}, f32[2,512,256]{1,2,0:T(8,128)S(1)}, u32[]{:S(2)}, u32[]{:S(2)}) collective-permute-start(f32[2,512,256]{1,2,0:T(8,128)S(1)} %pad_maximum_fusion.2), channel_id=1, source_target_pairs={{4,0},{8,4},{12,8},{0,12},{5,1},{9,5},{13,9},{1,13},{6,2},{10,6},{... | collective-permute-start | bytes 3145736 | tf_op jit(solution)/shard_map/ppermute | solution.py:15
  119.5 22.5 %copy-start.35 = (bf16[1,512,1024]{2,1,0:T(8,128)(2,1)S(1)}, bf16[1,512,1024]{2,1,0:T(8,128)(2,1)}, u32[]{:S(2)}) copy-start(bf16[1,512,1024]{2,1,0:T(8,128)(2,1)} %param.25) | copy-start | bytes 3145732
  (22 other events, 53.6 us)
Sparse Core Ops, SparseCore 0:
  153.2 86.7 reduce-scatter.3
where the time goes:
time: 251 us; the launch traced here: 250 us
  waiting for transfers between devices  103 us (41%)
  matrix products  72.3 us (29%)
  local copies, waits for them, and re-layouts  42.6 us (17%)
  between operations  14.5 us (6%)
  other arithmetic  12.1 us (5%)
  starting transfers between devices  5.16 us (2%)
    unnamed x2, waiting for transfers between devices  82.6 us
    sub x4, matrix products, group_terms(): raised = jnp.exp(scores - peak)  27.2 us
    dot_general x4, matrix products, group_terms(): jnp.einsum('rqk,qrd->kd', probs_low, douts3, preferred_element_type=jnp.f...  21.8 us
    ppermute x2, waiting for transfers between devices, shifted(): return lax.ppermute(block, axis, route)  20.8 us
    unnamed x93, local copies, waits for them, and re-layouts  15.1 us
    slice x5, local copies, waits for them, and re-layouts, body(): queries[0:block, cols]  9.44 us
    slice x5, local copies, waits for them, and re-layouts, body(): douts[0:block, cols]  8.17 us
    reduce_sum x4, other arithmetic, group_terms(): jnp.sum(douts3.astype(jnp.float32) * outputs3.astype(jnp.float32), axis=-1)  5.69 us
  transfers between devices with their start and end apart: 3, of which 2 were waited for; matrix products, arithmetic and copies ran while one was open for 15% of the time, Pallas kernels for 0%

commit v1 on v0

--- a/solution.py
+++ b/solution.py
@@ -111,14 +111,21 @@
     )
     input_grad = summed.astype(jnp.bfloat16)[None]
     all_grads = jnp.concatenate([query_blocks, key_grad, value_grad], axis=1)
-    owned = lax.psum_scatter(
-        lax.dot_general(
-            inputs, all_grads, (((0,), (0,)), ((), ())), preferred_element_type=jnp.float32
-        ),
-        ("seq", "lat"),
-        scatter_dimension=0,
-        tiled=True,
+    seq_n = lax.axis_size("seq")
+    lx_n = lax.axis_size("lx")
+    core_n = lax.axis_size("core")
+    model = inputs.shape[1]
+    rows = model // (seq_n * lx_n * core_n)
+    reordered = (
+        inputs.reshape(tokens, seq_n, lx_n, core_n, rows)
+        .transpose(0, 3, 1, 2, 4)
+        .reshape(tokens, model)
     )
+    partial = lax.dot_general(
+        reordered, all_grads, (((0,), (0,)), ((), ())), preferred_element_type=jnp.float32
+    )
+    in_chip = lax.psum_scatter(partial, "core", scatter_dimension=0, tiled=True)
+    owned = lax.psum_scatter(in_chip, ("seq", "lx"), scatter_dimension=0, tiled=True)
     q_width = HEADS * HEAD_DIM
     query_weight_grad = owned[:, :q_width]
     key_weight_grad = owned[:, q_width : q_width + kv_width]
@@ -127,26 +134,20 @@
 
 
 def solution(mesh):
-    placed = (
-        P(("parts", "lat"), "seq", None),
-        P(("parts", "lat"), "seq", None),
-        P(("parts", "lat"), "seq", None),
-        P(("parts", "lat"), "seq", None),
-        P(("parts", "lat"), "seq", None),
-        P(("parts", "lat"), "seq", None),
-        P(),
-        P(),
-        P(),
+    from jax.sharding import Mesh
+
+    grid = mesh.devices
+    split = Mesh(
+        grid.reshape(grid.shape[0], grid.shape[1], grid.shape[2] // 2, 2),
+        ("parts", "seq", "lx", "core"),
     )
+    rows_spec = P(("parts", "lx", "core"), "seq", None)
+    placed = (rows_spec,) * 6 + (P(), P(), P())
+    grads_spec = P(("parts", "seq", "lx", "core"), None)
     return jax.shard_map(
         body,
-        mesh=mesh,
+        mesh=split,
         in_specs=placed,
-        out_specs=(
-            P(("parts", "lat"), "seq", None),
-            P(("parts", "seq", "lat"), None),
-            P(("parts", "seq", "lat"), None),
-            P(("parts", "seq", "lat"), None),
-        ),
+        out_specs=(rows_spec, grads_spec, grads_spec, grads_spec),
         check_vma=False,
     )

time: 251 us -> 254 us (1.012)
  waiting for transfers between devices: 103 us -> 109 us
    reduce_scatter x0 -> x1, waiting for transfers between devices: none -> 15.7 us  [body(): in_chip = lax.psum_scatter(partial, 'core', scatter_dimension=0, tiled=True)]
    unnamed x2 -> x3, waiting for transfers between devices: 82.6 us -> 72.4 us
    unnamed x93 -> x96, local copies, waits for them, and re-layouts: 15.1 us -> 11.8 us
  transfers between devices with their start and end apart: 3 -> 4, of which waited for: 2 -> 3; matrix products, arithmetic and copies ran while one was open for 15% -> 16% of each run, Pallas kernels for 0% -> 0%
where the time goes in v1:
time: 254 us; the launch traced here: 253 us
  waiting for transfers between devices  109 us (43%)
  matrix products  72.3 us (28%)
  local copies, waits for them, and re-layouts  40.4 us (16%)
  between operations  14.6 us (6%)
  other arithmetic  11.3 us (4%)
  starting transfers between devices  5.22 us (2%)
    unnamed x3, waiting for transfers between devices  72.4 us
    sub x4, matrix products, group_terms(): raised = jnp.exp(scores - peak)  27.1 us
    dot_general x4, matrix products, group_terms(): jnp.einsum('rqk,qrd->kd', probs_low, douts3, preferred_element_type=jnp.f...  21.9 us
    ppermute x2, waiting for transfers between devices, shifted(): return lax.ppermute(block, axis, route)  20.7 us
    reduce_scatter x1, waiting for transfers between devices, body(): in_chip = lax.psum_scatter(partial, 'core', scatter_dimension=0, tiled=True)  15.7 us
    unnamed x96, local copies, waits for them, and re-layouts  11.8 us
    slice x5, local copies, waits for them, and re-layouts, body(): queries[0:block, cols]  9.5 us
    slice x5, local copies, waits for them, and re-layouts, body(): douts[0:block, cols]  8.16 us
  transfers between devices with their start and end apart: 4, of which 3 were waited for; matrix products, arithmetic and copies ran while one was open for 16% of the time, Pallas kernels for 0%

profile of v1, /device:TPU:0, one launch (start us, length us, event | category | flops | bytes accessed | tf_op | source)
XLA Modules:
  0.0 252.6 jit_solution(12382558785443468930)
XLA Ops:
  10.5 3.1 %collective-permute-start = (bf16[2,512,256]{1,2,0:T(8,128)(2,1)}, bf16[2,512,256]{1,2,0:T(8,128)(2,1)}, u32[]{:S(2)}, u32[]{:S(2)}) collective-permute-start(bf16[2,512,256]{1,2,0:T(8,128)(2,1)} %pad_maximum_fusion.3), channel_id=1, source_target_pairs={{12,0},{0,4},{4,8},{8,12},{13,1},{1,5},{5,9},{9,13},{14,2},{2,6},{... | collective-permute-start | bytes 1572872 | tf_op jit(solution)/shard_map/ppermute | solution.py:15
  16.1 2.3 fusion.127
  20.2 1.8 copy.89
  22.0 1.8 copy.85
  23.8 1.8 copy.80
  28.4 1.8 copy.90
  33.8 2.4 slice_convert_fusion
  37.6 2.1 copy.87
  39.7 2.0 copy.83
  49.7 6.6 %fusion.130 = (f32[4,512]{1,0:T(4,128)}, f32[4,512,1024]{1,2,0:T(8,128)}) fusion(pred[512,1024]{0,1:T(8,128)(4,1)} %fusion.36, bf16[512,4,64]{0,2,1:T(8,128)(2,1)S(1)} %bitcast.272, bf16[512,256]{0,1:T(8,128)(2,1)S(1)} %get-tuple-element.113, bf16[512,256]{0,1:T(8,128)(2,1)S(1)} %bitcast.250), kind=kOutput, calls=%fused_computation.164 | convolution fusion | flops 277087232 | bytes 9707520 | tf_op jit(solution)/shard_map/sub | solution.py:34
  56.4 5.6 %fusion.46 = f32[1024,64]{0,1:T(8,128)} fusion(bf16[512,4,64]{0,2,1:T(8,128)(2,1)S(1)} %bitcast.280, f32[4,512,1024]{1,2,0:T(8,128)} %get-tuple-element.117, f32[4,512]{1,0:T(4,128)} %get-tuple-element.116), kind=kOutput, calls=%fused_computation.74 | convolution fusion | flops 272629760 | bytes 8921088 | tf_op jit(solution)/shard_map/rqk,qrd->kd/dot_general | solution.py:48
  66.5 6.6 %fusion.135 = (f32[4,512]{1,0:T(4,128)}, f32[4,512,1024]{1,2,0:T(8,128)}) fusion(pred[512,1024]{0,1:T(8,128)(4,1)} %fusion.36, bf16[512,4,64]{0,2,1:T(8,128)(2,1)S(1)} %bitcast.268, bf16[512,256]{0,1:T(8,128)(2,1)S(1)} %get-tuple-element.113, bf16[512,256]{0,1:T(8,128)(2,1)S(1)} %bitcast.252), kind=kOutput, calls=%fused_computation.165 | convolution fusion | flops 277087232 | bytes 9707520 | tf_op jit(solution)/shard_map/sub | solution.py:34
  73.1 5.6 %fusion.49 = f32[1024,64]{0,1:T(8,128)} fusion(bf16[512,4,64]{0,2,1:T(8,128)(2,1)S(1)} %bitcast.274, f32[4,512,1024]{1,2,0:T(8,128)} %get-tuple-element.119, f32[4,512]{1,0:T(4,128)} %get-tuple-element.118), kind=kOutput, calls=%fused_computation.75 | convolution fusion | flops 272629760 | bytes 8921088 | tf_op jit(solution)/shard_map/rqk,qrd->kd/dot_general | solution.py:48
  83.4 6.5 %fusion.140 = (f32[4,512]{1,0:T(4,128)}, f32[4,512,1024]{1,2,0:T(8,128)}) fusion(pred[512,1024]{0,1:T(8,128)(4,1)} %fusion.36, bf16[512,4,64]{0,2,1:T(8,128)(2,1)S(1)} %bitcast.264, bf16[512,256]{0,1:T(8,128)(2,1)S(1)} %get-tuple-element.113, bf16[512,256]{0,1:T(8,128)(2,1)S(1)} %bitcast.254), kind=kOutput, calls=%fused_computation.166 | convolution fusion | flops 277087232 | bytes 9707520 | tf_op jit(solution)/shard_map/sub | solution.py:34
  89.9 5.7 %fusion.52 = f32[1024,64]{0,1:T(8,128)} fusion(bf16[512,4,64]{0,2,1:T(8,128)(2,1)} %bitcast.270, f32[4,512,1024]{1,2,0:T(8,128)} %get-tuple-element.121, f32[4,512]{1,0:T(4,128)} %get-tuple-element.120), kind=kOutput, calls=%fused_computation.76 | convolution fusion | flops 272629760 | bytes 8921088 | tf_op jit(solution)/shard_map/rqk,qrd->kd/dot_general | solution.py:48
  97.4 2.0 copy-done.1
  100.8 7.3 %fusion.145 = (f32[4,512]{1,0:T(4,128)S(1)}, f32[4,512,1024]{1,2,0:T(8,128)}) fusion(pred[512,1024]{0,1:T(8,128)(4,1)} %fusion.36, bf16[1024,64,1]{0,1,2:T(8,128)(2,1)S(1)} %fusion.96, bf16[512,4,64]{0,2,1:T(8,128)(2,1)} %bitcast.260), kind=kOutput, calls=%fused_computation.167 | convolution fusion | flops 276825088 | bytes 9314304 | tf_op jit(solution)/shard_map/sub | solution.py:34
  108.1 4.9 %fusion.55 = f32[1024,64]{0,1:T(8,128)S(1)} fusion(bf16[512,4,64]{0,2,1:T(8,128)(2,1)} %bitcast.266, f32[4,512,1024]{1,2,0:T(8,128)} %get-tuple-element.123, f32[4,512]{1,0:T(4,128)S(1)} %get-tuple-element.122), kind=kOutput, calls=%fused_computation.77 | convolution fusion | flops 272629760 | bytes 8921088 | tf_op jit(solution)/shard_map/rqk,qrd->kd/dot_general | solution.py:48
  117.4 2.1 collective-permute-start.1
  121.3 20.7 %collective-permute-done.1 = f32[2,512,256]{1,2,0:T(8,128)S(1)} collective-permute-done((f32[2,512,256]{1,2,0:T(8,128)S(1)}, f32[2,512,256]{1,2,0:T(8,128)S(1)}, u32[]{:S(2)}, u32[]{:S(2)}) %collective-permute-start.1) | collective-permute-done | bytes 1048608 | tf_op jit(solution)/shard_map/ppermute | solution.py:15
  142.9 4.6 %convolution_bitcast_fusion = f32[1024,1536]{0,1:T(8,128)} fusion(bf16[512,1536]{0,1:T(8,128)(2,1)S(1)} %get-tuple-element.96, bf16[512,1024]{0,1:T(8,128)(2,1)S(1)} %bitcast.284), kind=kOutput, calls=%fused_computation.28 | convolution fusion | flops 1610612736 | bytes 8912896 | tf_op jit(solution)/shard_map/dot_general | solution.py:124
  147.6 15.7 %reduce-scatter.5.cloned.1.call-done = f32[512,1536]{0,1:T(8,128)} async-done(((f32[1024,1536]{0,1:T(8,128)}), f32[512,1536]{0,1:T(8,128)}) %reduce-scatter.5.cloned.1.call-update) | async-done | bytes 3145744 | tf_op jit(solution)/shard_map/reduce_scatter | solution.py:127
  163.3 3.5 %copy.122 = f32[512,1536]{1,0:T(8,128)} copy(f32[512,1536]{0,1:T(8,128)} %reduce-scatter.5.cloned.1.call-done) | data formatting | bytes 6291456
  170.2 72.3 %reduce-scatter.7.cloned.1.call-done = f32[64,1536]{1,0:T(8,128)} async-done(((f32[512,1536]{1,0:T(8,128)}), f32[64,1536]{1,0:T(8,128)}) %reduce-scatter.7.cloned.1.call-update) | async-done | bytes 393232
  (139 shorter events, 49.1 us)
Async XLA Ops:
  7.2 159.7 %copy-start = (bf16[1024,1024]{1,0:T(8,128)(2,1)S(1)}, bf16[1024,1024]{1,0:T(8,128)(2,1)}, u32[]{:S(2)}) copy-start(bf16[1024,1024]{1,0:T(8,128)(2,1)} %param.31) | copy-start | bytes 6291460
  7.2 156.1 %reduce-scatter.5.cloned.1.call-start = ((), (), s32[]{:S(2)}) async-start(), calls=%async_computation.2 | async-start | bytes 9437184 | tf_op jit(solution)/shard_map/reduce_scatter | solution.py:127
  10.5 38.1 %collective-permute-start = (bf16[2,512,256]{1,2,0:T(8,128)(2,1)}, bf16[2,512,256]{1,2,0:T(8,128)(2,1)}, u32[]{:S(2)}, u32[]{:S(2)}) collective-permute-start(bf16[2,512,256]{1,2,0:T(8,128)(2,1)} %pad_maximum_fusion.3), channel_id=1, source_target_pairs={{12,0},{0,4},{4,8},{8,12},{13,1},{1,5},{5,9},{9,13},{14,2},{2,6},{... | collective-permute-start | bytes 1572872 | tf_op jit(solution)/shard_map/ppermute | solution.py:15
  16.1 9.5 %copy-start.18 = (bf16[1,512,1024]{2,1,0:T(8,128)(2,1)S(1)}, bf16[1,512,1024]{2,1,0:T(8,128)(2,1)}, u32[]{:S(2)}) copy-start(bf16[1,512,1024]{2,1,0:T(8,128)(2,1)} %param.30) | copy-start | bytes 3145732
  42.7 7.0 %copy-start.14 = (bf16[512,256]{0,1:T(8,128)(2,1)S(1)}, bf16[512,256]{0,1:T(8,128)(2,1)}, u32[]{:S(2)}) copy-start(bf16[512,256]{0,1:T(8,128)(2,1)} %copy.80) | copy-start | bytes 786436
  49.7 12.3 %copy-start.28 = (bf16[512,256]{0,1:T(8,128)(2,1)}, bf16[512,256]{0,1:T(8,128)(2,1)S(1)}, u32[]{:S(2)}) copy-start(bf16[512,256]{0,1:T(8,128)(2,1)S(1)} %get-tuple-element.112) | copy-start | bytes 786436
  49.7 6.6 %copy-start.17 = (bf16[512,256]{0,1:T(8,128)(2,1)S(1)}, bf16[512,256]{0,1:T(8,128)(2,1)}, u32[]{:S(2)}) copy-start(bf16[512,256]{0,1:T(8,128)(2,1)} %copy.82) | copy-start | bytes 786436
  56.4 5.7 %copy-start.36 = (f32[512,4]{0,1:T(4,128)S(1)}, f32[512,4]{0,1:T(4,128)}, u32[]{:S(2)}) copy-start(f32[512,4]{0,1:T(4,128)} %multiply_reduce_fusion.3) | copy-start | bytes 24580
  56.4 5.9 %copy-start.37 = (f32[4,512,1024]{1,2,0:T(8,128)S(1)}, f32[4,512,1024]{1,2,0:T(8,128)}, u32[]{:S(2)}) copy-start(f32[4,512,1024]{1,2,0:T(8,128)} %get-tuple-element.117) | copy-start | bytes 25165828
  56.4 5.9 %copy-start.41 = (f32[4,512]{1,0:T(4,128)S(1)}, f32[4,512]{1,0:T(4,128)}, u32[]{:S(2)}) copy-start(f32[4,512]{1,0:T(4,128)} %get-tuple-element.116) | copy-start | bytes 24580
  66.5 6.6 %copy-start.16 = (bf16[512,256]{0,1:T(8,128)(2,1)S(1)}, bf16[512,256]{0,1:T(8,128)(2,1)}, u32[]{:S(2)}) copy-start(bf16[512,256]{0,1:T(8,128)(2,1)} %copy.86) | copy-start | bytes 786436
  73.1 6.0 %copy-start.38 = (f32[4,512,1024]{1,2,0:T(8,128)S(1)}, f32[4,512,1024]{1,2,0:T(8,128)}, u32[]{:S(2)}) copy-start(f32[4,512,1024]{1,2,0:T(8,128)} %get-tuple-element.119) | copy-start | bytes 25165828
  73.1 6.0 %copy-start.42 = (f32[4,512]{1,0:T(4,128)S(1)}, f32[4,512]{1,0:T(4,128)}, u32[]{:S(2)}) copy-start(f32[4,512]{1,0:T(4,128)} %get-tuple-element.118) | copy-start | bytes 24580
  89.9 5.7 %copy-start.13 = (bf16[512,256]{0,1:T(8,128)(2,1)S(1)}, bf16[512,256]{0,1:T(8,128)(2,1)}, u32[]{:S(2)}) copy-start(bf16[512,256]{0,1:T(8,128)(2,1)} %copy.90) | copy-start | bytes 786436
  89.9 5.7 %copy-start.23 = (bf16[1,512,256]{1,2,0:T(8,128)(2,1)S(1)}, bf16[1,512,256]{1,2,0:T(8,128)(2,1)}, u32[]{:S(2)}) copy-start(bf16[1,512,256]{1,2,0:T(8,128)(2,1)} %copy-done.20) | copy-start | bytes 786436
  89.9 5.7 %copy-start.30 = (bf16[512,256]{0,1:T(8,128)(2,1)S(1)}, bf16[512,256]{0,1:T(8,128)(2,1)}, u32[]{:S(2)}) copy-start(bf16[512,256]{0,1:T(8,128)(2,1)} %copy-done.28) | copy-start | bytes 786436
  89.9 6.2 %copy-start.39 = (f32[4,512,1024]{1,2,0:T(8,128)S(1)}, f32[4,512,1024]{1,2,0:T(8,128)}, u32[]{:S(2)}) copy-start(f32[4,512,1024]{1,2,0:T(8,128)} %get-tuple-element.121) | copy-start | bytes 25165828
  89.9 6.2 %copy-start.43 = (f32[4,512]{1,0:T(4,128)S(1)}, f32[4,512]{1,0:T(4,128)}, u32[]{:S(2)}) copy-start(f32[4,512]{1,0:T(4,128)} %get-tuple-element.120) | copy-start | bytes 24580
  108.1 6.1 %copy-start.40 = (f32[4,512,1024]{1,2,0:T(8,128)S(1)}, f32[4,512,1024]{1,2,0:T(8,128)}, u32[]{:S(2)}) copy-start(f32[4,512,1024]{1,2,0:T(8,128)} %get-tuple-element.123) | copy-start | bytes 25165828
  117.4 24.7 %collective-permute-start.1 = (f32[2,512,256]{1,2,0:T(8,128)S(1)}, f32[2,512,256]{1,2,0:T(8,128)S(1)}, u32[]{:S(2)}, u32[]{:S(2)}) collective-permute-start(f32[2,512,256]{1,2,0:T(8,128)S(1)} %pad_maximum_fusion.2), channel_id=1, source_target_pairs={{4,0},{8,4},{12,8},{0,12},{5,1},{9,5},{13,9},{1,13},{6,2},{10,6},{... | collective-permute-start | bytes 3145736 | tf_op jit(solution)/shard_map/ppermute | solution.py:15
  120.4 22.5 %copy-start.19 = (bf16[512,2,4,2,64]{0,4,3,2,1:T(8,128)(2,1)S(1)}, bf16[512,2,4,2,64]{0,4,3,2,1:T(8,128)(2,1)}, u32[]{:S(2)}) copy-start(bf16[512,2,4,2,64]{0,4,3,2,1:T(8,128)(2,1)} %copy.106) | copy-start | bytes 3145732
  147.5 19.3 %copy-start.4 = (bf16[64,4,512]{2,0,1:T(8,128)(2,1)S(1)}, bf16[64,4,512]{2,0,1:T(8,128)(2,1)}, u32[]{:S(2)}) copy-start(bf16[64,4,512]{2,0,1:T(8,128)(2,1)} %fusion.38) | copy-start | bytes 786436
  147.5 19.3 %copy-start.7 = (bf16[64,4,512]{2,0,1:T(8,128)(2,1)S(1)}, bf16[64,4,512]{2,0,1:T(8,128)(2,1)}, u32[]{:S(2)}) copy-start(bf16[64,4,512]{2,0,1:T(8,128)(2,1)} %fusion.39) | copy-start | bytes 786436
  147.5 95.0 %reduce-scatter.7.cloned.1.call-start = ((), (), s32[]{:S(2)}) async-start(), calls=%async_computation.3 | async-start | bytes 3538944
  (24 other events, 72.8 us)
Sparse Core Ops, SparseCore 0:
  147.6 15.5 reduce-scatter.4
  166.9 75.5 reduce-scatter.6

commit v2 on v0

--- a/solution.py
+++ b/solution.py
@@ -74,11 +74,10 @@
     prior_pair = shifted(tail_pair, "seq", 1)
     ext_keys = jnp.concatenate([prior_pair[0], keys_own], axis=0)
     ext_values = jnp.concatenate([prior_pair[1], values_own], axis=0)
-    key_acc = jnp.zeros((tokens + WINDOW, kv_width), jnp.float32)
-    value_acc = jnp.zeros((tokens + WINDOW, kv_width), jnp.float32)
+    fronts = []
+    owns = []
     query_list = []
-    key_list = []
-    value_list = []
+    wq_list = []
     for group in range(KV_HEADS):
         cols = slice(group * width, (group + 1) * width)
         kv_cols = slice(group * HEAD_DIM, (group + 1) * HEAD_DIM)
@@ -89,16 +88,23 @@
             ext_keys[0 : block + WINDOW, kv_cols],
             ext_values[0 : block + WINDOW, kv_cols],
         )
-        query_list.append(q_term)
-        key_list.append(k_term)
-        value_list.append(v_term)
-    query_blocks = jnp.concatenate(query_list, 1).astype(jnp.bfloat16)
-    key_acc = key_acc.at[0 : block + WINDOW].add(jnp.concatenate(key_list, 1))
-    value_acc = value_acc.at[0 : block + WINDOW].add(jnp.concatenate(value_list, 1))
-    front_pair = jnp.stack([key_acc[:WINDOW], value_acc[:WINDOW]])
-    returned = shifted(front_pair, "seq", -1)
-    key_grad = key_acc[WINDOW:].at[tokens - WINDOW :].add(returned[0]).astype(jnp.bfloat16)
-    value_grad = value_acc[WINDOW:].at[tokens - WINDOW :].add(returned[1]).astype(jnp.bfloat16)
+        q_low = q_term.astype(jnp.bfloat16)
+        query_list.append(q_low)
+        wq_part = lax.dot_general(
+            inputs, q_low, (((0,), (0,)), ((), ())), preferred_element_type=jnp.float32
+        )
+        wq_list.append(
+            lax.psum_scatter(wq_part, ("seq", "lat"), scatter_dimension=0, tiled=True)
+        )
+        fronts.append(shifted(jnp.stack([k_term[:WINDOW], v_term[:WINDOW]]), "seq", -1))
+        owns.append((k_term[WINDOW:], v_term[WINDOW:]))
+    query_blocks = jnp.concatenate(query_list, 1)
+    key_grad = jnp.concatenate(
+        [own[0].at[tokens - WINDOW :].add(back[0]) for own, back in zip(owns, fronts)], 1
+    ).astype(jnp.bfloat16)
+    value_grad = jnp.concatenate(
+        [own[1].at[tokens - WINDOW :].add(back[1]) for own, back in zip(owns, fronts)], 1
+    ).astype(jnp.bfloat16)
     contract_cols = (((1,), (1,)), ((), ()))
     summed = lax.dot_general(
         query_blocks, weight_query, contract_cols, preferred_element_type=jnp.float32
@@ -110,19 +116,18 @@
         value_grad, weight_value, contract_cols, preferred_element_type=jnp.float32
     )
     input_grad = summed.astype(jnp.bfloat16)[None]
-    all_grads = jnp.concatenate([query_blocks, key_grad, value_grad], axis=1)
-    owned = lax.psum_scatter(
+    kv_grads = jnp.concatenate([key_grad, value_grad], axis=1)
+    kv_owned = lax.psum_scatter(
         lax.dot_general(
-            inputs, all_grads, (((0,), (0,)), ((), ())), preferred_element_type=jnp.float32
+            inputs, kv_grads, (((0,), (0,)), ((), ())), preferred_element_type=jnp.float32
         ),
         ("seq", "lat"),
         scatter_dimension=0,
         tiled=True,
     )
-    q_width = HEADS * HEAD_DIM
-    query_weight_grad = owned[:, :q_width]
-    key_weight_grad = owned[:, q_width : q_width + kv_width]
-    value_weight_grad = owned[:, q_width + kv_width :]
+    query_weight_grad = jnp.concatenate(wq_list, 1)
+    key_weight_grad = kv_owned[:, :kv_width]
+    value_weight_grad = kv_owned[:, kv_width:]
     return (input_grad, query_weight_grad, key_weight_grad, value_weight_grad)
 
 

time: 251 us -> 378 us (1.51)
  waiting for transfers between devices: 103 us -> 188 us
  matrix products: 72.3 us -> 88.8 us
  other arithmetic: 12.1 us -> 23.9 us
  local copies, waits for them, and re-layouts: 42.6 us -> 52.8 us
    unnamed x2 -> x10, waiting for transfers between devices: 82.6 us -> 187 us
    ppermute x2 -> x5, waiting for transfers between devices: 20.8 us -> 0.93 us  [shifted(): return lax.ppermute(block, axis, route)]
    unnamed x93 -> x102, local copies, waits for them, and re-layouts: 15.1 us -> 30.3 us
    unnamed x1 -> x7, other arithmetic: 0.77 us -> 10.1 us
    dot_general x4, matrix products: 5.24 us -> 10.7 us  [group_terms(): jnp.einsum('qrd,kd->rqk', douts3, value_part, preferred_element_type=jnp....]
    sub x4, matrix products: 27.2 us -> 31.1 us  [group_terms(): raised = jnp.exp(scores - peak)]
    dot_general x1 -> x5, matrix products: 4.48 us -> 7.74 us  [the longest x4 5.7 us: body(): lax.dot_general(inputs, q_low, (((0,), (0,)), ((), ())), preferred_elemen...]
    ppermute x2 -> x5, starting transfers between devices: 5.12 us -> 7.92 us  [shifted(): return lax.ppermute(block, axis, route)]
  transfers between devices with their start and end apart: 3 -> 10, of which waited for: 2 -> 5; matrix products, arithmetic and copies ran while one was open for 15% -> 35% of each run, Pallas kernels for 0% -> 0%
where the time goes in v2:
time: 378 us; the launch traced here: 377 us
  waiting for transfers between devices  188 us (50%)
  matrix products  88.8 us (23%)
  local copies, waits for them, and re-layouts  52.8 us (14%)
  other arithmetic  23.9 us (6%)
  between operations  14.4 us (4%)
  starting transfers between devices  8.78 us (2%)
    unnamed x10, waiting for transfers between devices  187 us
    sub x4, matrix products, group_terms(): raised = jnp.exp(scores - peak)  31.1 us
    unnamed x102, local copies, waits for them, and re-layouts  30.3 us
    dot_general x4, matrix products, group_terms(): jnp.einsum('rqk,qrd->kd', probs_low, douts3, preferred_element_type=jnp.f...  20.7 us
    dot_general x4, matrix products, group_terms(): jnp.einsum('qrd,kd->rqk', douts3, value_part, preferred_element_type=jnp....  10.7 us
    unnamed x7, other arithmetic  10.1 us
    ppermute x5, starting transfers between devices, shifted(): return lax.ppermute(block, axis, route)  7.92 us
    dot_general x4, matrix products, group_terms(): jnp.einsum('rqk,qrd->kd', dscores, queries3, preferred_element_type=jnp.f...  7.73 us
  transfers between devices with their start and end apart: 10, of which 5 were waited for; matrix products, arithmetic and copies ran while one was open for 35% of the time, Pallas kernels for 0%

profile of v2, /device:TPU:0, one launch (start us, length us, event | category | flops | bytes accessed | tf_op | source)
XLA Modules:
  0.0 377.0 jit_solution(15074287905044157750)
XLA Ops:
  10.4 3.1 collective-permute-start
  26.1 2.4 slice_convert_fusion.3
  42.0 7.8 %fusion.176 = (f32[4,512]{1,0:T(4,128)}, f32[4,512,1024]{1,2,0:T(8,128)}) fusion(pred[512,1024]{0,1:T(8,128)(4,1)S(1)} %fusion.36, bf16[512,4,64]{0,2,1:T(8,128)(2,1)} %bitcast.351, bf16[512,256]{0,1:T(8,128)(2,1)S(1)} %get-tuple-element.201, bf16[512,256]{0,1:T(8,128)(2,1)S(1)} %bitcast.324), kind=kOutput, calls=%fused_computation.220 | convolution fusion | flops 277087232 | bytes 9707520 | tf_op jit(solution)/shard_map/sub | solution.py:34
  49.9 4.9 %fusion.49 = f32[1024,64]{0,1:T(8,128)S(1)} fusion(bf16[512,4,64]{0,2,1:T(8,128)(2,1)S(1)} %bitcast.353, f32[4,512,1024]{1,2,0:T(8,128)} %get-tuple-element.209, f32[4,512]{1,0:T(4,128)} %get-tuple-element.208), kind=kOutput, calls=%fused_computation.79 | convolution fusion | flops 272629760 | bytes 8921088 | tf_op jit(solution)/shard_map/rqk,qrd->kd/dot_general | solution.py:48
  63.7 2.6 copy.89
  66.6 8.0 %fusion.171 = (f32[4,512]{1,0:T(4,128)}, f32[4,512,1024]{1,2,0:T(8,128)}) fusion(pred[512,1024]{0,1:T(8,128)(4,1)} %copy-done.28, bf16[512,4,64]{0,2,1:T(8,128)(2,1)} %bitcast.347, bf16[512,256]{0,1:T(8,128)(2,1)} %copy-done.4, bf16[512,256]{0,1:T(8,128)(2,1)S(1)} %bitcast.326), kind=kOutput, calls=%fused_computation.219 | convolution fusion | flops 277087232 | bytes 9707520 | tf_op jit(solution)/shard_map/sub | solution.py:34
  74.5 5.1 %fusion.52 = f32[1024,64]{0,1:T(8,128)S(1)} fusion(bf16[512,4,64]{0,2,1:T(8,128)(2,1)} %bitcast.349, f32[4,512,1024]{1,2,0:T(8,128)} %get-tuple-element.207, f32[4,512]{1,0:T(4,128)} %get-tuple-element.206), kind=kOutput, calls=%fused_computation.80 | convolution fusion | flops 272629760 | bytes 8921088 | tf_op jit(solution)/shard_map/rqk,qrd->kd/dot_general | solution.py:48
  89.2 7.9 %fusion.170 = (f32[4,512]{1,0:T(4,128)}, f32[4,512,1024]{1,2,0:T(8,128)}) fusion(pred[512,1024]{0,1:T(8,128)(4,1)} %copy-done.28, bf16[1024,64,1]{0,1,2:T(8,128)(2,1)S(1)} %fusion.128, bf16[512,4,64]{0,2,1:T(8,128)(2,1)} %bitcast.343), kind=kOutput, calls=%fused_computation.218 | convolution fusion | flops 276825088 | bytes 9314304 | tf_op jit(solution)/shard_map/sub | solution.py:34
  97.1 5.7 %fusion.55 = f32[1024,64]{0,1:T(8,128)} fusion(bf16[512,4,64]{0,2,1:T(8,128)(2,1)} %bitcast.345, f32[4,512,1024]{1,2,0:T(8,128)} %get-tuple-element.205, f32[4,512]{1,0:T(4,128)} %get-tuple-element.204), kind=kOutput, calls=%fused_computation.81 | convolution fusion | flops 272629760 | bytes 8921088 | tf_op jit(solution)/shard_map/rqk,qrd->kd/dot_general | solution.py:48
  105.8 2.5 copy.91
  108.3 6.7 %fusion.5 = bf16[4,512,1024]{1,2,0:T(8,128)(2,1)} fusion(f32[4,512]{1,0:T(4,128)S(1)} %bitcast.362, f32[4,512,1024]{1,2,0:T(8,128)} %get-tuple-element.205, f32[4,512]{1,0:T(4,128)} %get-tuple-element.204, bf16[512,4,64]{0,2,1:T(8,128)(2,1)} %bitcast.346, bf16[512,256]{0,1:T(8,128)(2,1)} %bitcast.357, bf16[512,256]{0,1:T(8,128)(2,1)} %get-tuple-element.200), kind=kOutput, calls=%fused_computation.6 | convolution fusion | flops 277086208 | bytes 13385728 | tf_op jit(solution)/shard_map/qrd,kd->rqk/dot_general | solution.py:37
  115.4 3.6 fusion.42
  121.7 3.0 fusion.41
  126.9 2.6 copy.93
  129.5 7.3 %fusion.181 = (f32[4,512]{1,0:T(4,128)S(1)}, f32[4,512,1024]{1,2,0:T(8,128)}) fusion(pred[512,1024]{0,1:T(8,128)(4,1)} %copy-done.28, bf16[512,4,64]{0,2,1:T(8,128)(2,1)} %bitcast.339, bf16[512,256]{0,1:T(8,128)(2,1)} %copy-done.4, bf16[512,256]{0,1:T(8,128)(2,1)S(1)} %bitcast.328), kind=kOutput, calls=%fused_computation.221 | convolution fusion | flops 277087232 | bytes 9707520 | tf_op jit(solution)/shard_map/sub | solution.py:34
  136.9 5.0 %fusion.46 = f32[1024,64]{0,1:T(8,128)S(1)} fusion(bf16[512,4,64]{0,2,1:T(8,128)(2,1)} %bitcast.341, f32[4,512,1024]{1,2,0:T(8,128)} %get-tuple-element.211, f32[4,512]{1,0:T(4,128)S(1)} %get-tuple-element.210), kind=kOutput, calls=%fused_computation.78 | convolution fusion | flops 272629760 | bytes 8921088 | tf_op jit(solution)/shard_map/rqk,qrd->kd/dot_general | solution.py:48
  151.0 2.6 copy.87
  166.5 2.0 convolution_bitcast_fusion
  168.6 3.0 copy.95
  171.6 2.4 fusion.58
  177.9 6.1 %reduce-scatter.20.cloned.1.call-done = f32[64,256]{1,0:T(8,128)} async-done(((f32[1024,256]{1,0:T(8,128)}), f32[64,256]{1,0:T(8,128)}) %reduce-scatter.20.cloned.1.call-update) | async-done | bytes 65552
  185.0 59.4 %reduce-scatter.22.cloned.1.call-done = f32[64,256]{1,0:T(8,128)} async-done(((f32[1024,256]{1,0:T(8,128)}), f32[64,256]{1,0:T(8,128)}) %reduce-scatter.22.cloned.1.call-update) | async-done | bytes 65552
  245.3 59.2 %reduce-scatter.16.cloned.1.call-done = f32[64,256]{1,0:T(8,128)} async-done(((f32[1024,256]{1,0:T(8,128)}), f32[64,256]{1,0:T(8,128)}) %reduce-scatter.16.cloned.1.call-update) | async-done | bytes 65552
  306.3 62.6 %reduce-scatter.24.cloned.1.call-done = f32[64,512]{1,0:T(8,128)} async-done(((f32[1024,512]{1,0:T(8,128)}), f32[64,512]{1,0:T(8,128)}) %reduce-scatter.24.cloned.1.call-update) | async-done | bytes 131088
  (173 shorter events, 86.9 us)
Async XLA Ops:
  7.2 164.4 %copy-start = (bf16[1024,1024]{1,0:T(8,128)(2,1)S(1)}, bf16[1024,1024]{1,0:T(8,128)(2,1)}, u32[]{:S(2)}) copy-start(bf16[1024,1024]{1,0:T(8,128)(2,1)} %param.47) | copy-start | bytes 6291460
  7.2 169.8 %reduce-scatter.18.cloned.1.call-start = ((), (), s32[]{:S(2)}) async-start(), calls=%async_computation.6 | async-start | bytes 1114112
  9.6 18.9 %copy-start.23 = (bf16[1,512,256]{1,2,0:T(8,128)(2,1)}, bf16[1,512,256]{1,2,0:T(8,128)(2,1)S(1)}, u32[]{:S(2)}) copy-start(bf16[1,512,256]{1,2,0:T(8,128)(2,1)S(1)} %copy.45) | copy-start | bytes 786436
  10.4 29.6 %collective-permute-start = (bf16[2,512,256]{1,2,0:T(8,128)(2,1)}, bf16[2,512,256]{1,2,0:T(8,128)(2,1)}, u32[]{:S(2)}, u32[]{:S(2)}) collective-permute-start(bf16[2,512,256]{1,2,0:T(8,128)(2,1)} %pad_maximum_fusion), channel_id=1, source_target_pairs={{12,0},{0,4},{4,8},{8,12},{13,1},{1,5},{5,9},{9,13},{14,2},{2,6},{... | collective-permute-start | bytes 1572872 | tf_op jit(solution)/shard_map/ppermute | solution.py:15
  40.0 9.9 %copy-start.28 = (pred[512,1024]{0,1:T(8,128)(4,1)}, pred[512,1024]{0,1:T(8,128)(4,1)S(1)}, u32[]{:S(2)}) copy-start(pred[512,1024]{0,1:T(8,128)(4,1)S(1)} %fusion.36) | copy-start | bytes 1572868
  40.0 9.8 %copy-start.22 = (bf16[512,256]{0,1:T(8,128)(2,1)S(1)}, bf16[512,256]{0,1:T(8,128)(2,1)}, u32[]{:S(2)}) copy-start(bf16[512,256]{0,1:T(8,128)(2,1)} %copy.53) | copy-start | bytes 786436
  42.0 12.8 %copy-start.4 = (bf16[512,256]{0,1:T(8,128)(2,1)}, bf16[512,256]{0,1:T(8,128)(2,1)S(1)}, u32[]{:S(2)}) copy-start(bf16[512,256]{0,1:T(8,128)(2,1)S(1)} %get-tuple-element.201) | copy-start | bytes 786436
  49.9 6.0 %copy-start.41 = (f32[4,512,1024]{1,2,0:T(8,128)S(1)}, f32[4,512,1024]{1,2,0:T(8,128)}, u32[]{:S(2)}) copy-start(f32[4,512,1024]{1,2,0:T(8,128)} %get-tuple-element.209) | copy-start | bytes 25165828
  49.9 6.0 %copy-start.43 = (f32[4,512]{1,0:T(4,128)S(1)}, f32[4,512]{1,0:T(4,128)}, u32[]{:S(2)}) copy-start(f32[4,512]{1,0:T(4,128)} %get-tuple-element.208) | copy-start | bytes 24580
  60.3 96.2 %collective-permute-start.2 = (f32[2,512,64]{1,2,0:T(8,128)}, f32[2,512,64]{1,2,0:T(8,128)}, u32[]{:S(2)}, u32[]{:S(2)}) collective-permute-start(f32[2,512,64]{1,2,0:T(8,128)} %pad_maximum_fusion.3), channel_id=1, source_target_pairs={{4,0},{8,4},{12,8},{0,12},{5,1},{9,5},{13,9},{1,13},{6,2},{10,6},{... | collective-permute-start | bytes 786440 | tf_op jit(solution)/shard_map/ppermute | solution.py:15
  66.3 117.8 %reduce-scatter.20.cloned.1.call-start = ((), (), s32[]{:S(2)}) async-start(), calls=%async_computation.7 | async-start | bytes 1114112
  74.5 6.5 %copy-start.42 = (f32[4,512,1024]{1,2,0:T(8,128)S(1)}, f32[4,512,1024]{1,2,0:T(8,128)}, u32[]{:S(2)}) copy-start(f32[4,512,1024]{1,2,0:T(8,128)} %get-tuple-element.207) | copy-start | bytes 25165828
  74.5 6.5 %copy-start.44 = (f32[4,512]{1,0:T(4,128)S(1)}, f32[4,512]{1,0:T(4,128)}, u32[]{:S(2)}) copy-start(f32[4,512]{1,0:T(4,128)} %get-tuple-element.206) | copy-start | bytes 24580
  79.6 6.1 %copy-start.33 = (f32[1024,64]{0,1:T(8,128)}, f32[1024,64]{0,1:T(8,128)S(1)}, u32[]{:S(2)}) copy-start(f32[1024,64]{0,1:T(8,128)S(1)} %fusion.52) | copy-start | bytes 786436
  87.2 70.9 %collective-permute-start.3 = (f32[2,512,64]{1,2,0:T(8,128)}, f32[2,512,64]{1,2,0:T(8,128)}, u32[]{:S(2)}, u32[]{:S(2)}) collective-permute-start(f32[2,512,64]{1,2,0:T(8,128)} %pad_maximum_fusion.4), channel_id=1, source_target_pairs={{4,0},{8,4},{12,8},{0,12},{5,1},{9,5},{13,9},{1,13},{6,2},{10,6},{... | collective-permute-start | bytes 786440 | tf_op jit(solution)/shard_map/ppermute | solution.py:15
  97.1 5.7 %copy-start.6 = (bf16[512,256]{0,1:T(8,128)(2,1)S(1)}, bf16[512,256]{0,1:T(8,128)(2,1)}, u32[]{:S(2)}) copy-start(bf16[512,256]{0,1:T(8,128)(2,1)} %copy-done.4) | copy-start | bytes 786436
  115.1 129.3 %reduce-scatter.22.cloned.1.call-start = ((), (), s32[]{:S(2)}) async-start(), calls=%async_computation.8 | async-start | bytes 1114112
  121.3 38.3 %collective-permute-start.4 = (f32[2,512,64]{1,2,0:T(8,128)}, f32[2,512,64]{1,2,0:T(8,128)}, u32[]{:S(2)}, u32[]{:S(2)}) collective-permute-start(f32[2,512,64]{1,2,0:T(8,128)} %pad_maximum_fusion.5), channel_id=1, source_target_pairs={{4,0},{8,4},{12,8},{0,12},{5,1},{9,5},{13,9},{1,13},{6,2},{10,6},{... | collective-permute-start | bytes 786440 | tf_op jit(solution)/shard_map/ppermute | solution.py:15
  136.8 167.6 %reduce-scatter.16.cloned.1.call-start = ((), (), s32[]{:S(2)}) async-start(), calls=%async_computation.5 | async-start | bytes 1114112
  136.9 6.5 %copy-start.40 = (f32[4,512,1024]{1,2,0:T(8,128)S(1)}, f32[4,512,1024]{1,2,0:T(8,128)}, u32[]{:S(2)}) copy-start(f32[4,512,1024]{1,2,0:T(8,128)} %get-tuple-element.211) | copy-start | bytes 25165828
  147.5 7.3 %collective-permute-start.1 = (f32[2,512,64]{1,2,0:T(8,128)}, f32[2,512,64]{1,2,0:T(8,128)}, u32[]{:S(2)}, u32[]{:S(2)}) collective-permute-start(f32[2,512,64]{1,2,0:T(8,128)} %pad_maximum_fusion.2), channel_id=1, source_target_pairs={{4,0},{8,4},{12,8},{0,12},{5,1},{9,5},{13,9},{1,13},{6,2},{10,6},{... | collective-permute-start | bytes 786440 | tf_op jit(solution)/shard_map/ppermute | solution.py:15
  151.0 20.6 %copy-start.13 = (bf16[64,4,512]{2,0,1:T(8,128)(2,1)S(1)}, bf16[64,4,512]{2,0,1:T(8,128)(2,1)}, u32[]{:S(2)}) copy-start(bf16[64,4,512]{2,0,1:T(8,128)(2,1)} %copy-done.12) | copy-start | bytes 786436
  153.6 215.4 %reduce-scatter.24.cloned.1.call-start = ((), (), s32[]{:S(2)}) async-start(), calls=%async_computation.9 | async-start | bytes 2228224
  168.6 6.9 %copy-start.27 = (bf16[1024,256]{1,0:T(8,128)(2,1)S(1)}, bf16[1024,256]{1,0:T(8,128)(2,1)}, u32[]{:S(2)}) copy-start(bf16[1024,256]{1,0:T(8,128)(2,1)} %param.49) | copy-start | bytes 1572868
  (31 other events, 106.9 us)
Sparse Core Ops, SparseCore 0:
  66.4 57.2 reduce-scatter.17
  127.4 56.6 reduce-scatter.19
  187.7 56.6 reduce-scatter.21
  247.9 56.5 reduce-scatter.15
  308.1 60.8 reduce-scatter.23

commit v3 on v0

--- a/solution.py
+++ b/solution.py
@@ -72,6 +72,7 @@
     block = min(512, tokens)
     tail_pair = jnp.stack([keys_own, values_own])
     prior_pair = shifted(tail_pair, "seq", 1)
+    prior_inputs = shifted(inputs, "seq", 1)
     ext_keys = jnp.concatenate([prior_pair[0], keys_own], axis=0)
     ext_values = jnp.concatenate([prior_pair[1], values_own], axis=0)
     key_acc = jnp.zeros((tokens + WINDOW, kv_width), jnp.float32)
@@ -110,15 +111,21 @@
         value_grad, weight_value, contract_cols, preferred_element_type=jnp.float32
     )
     input_grad = summed.astype(jnp.bfloat16)[None]
-    all_grads = jnp.concatenate([query_blocks, key_grad, value_grad], axis=1)
-    owned = lax.psum_scatter(
-        lax.dot_general(
-            inputs, all_grads, (((0,), (0,)), ((), ())), preferred_element_type=jnp.float32
-        ),
-        ("seq", "lat"),
-        scatter_dimension=0,
-        tiled=True,
+    own_grads = jnp.concatenate(
+        [query_blocks, key_acc[WINDOW:].astype(jnp.bfloat16), value_acc[WINDOW:].astype(jnp.bfloat16)],
+        axis=1,
     )
+    front_grads = jnp.concatenate(
+        [key_acc[:WINDOW].astype(jnp.bfloat16), value_acc[:WINDOW].astype(jnp.bfloat16)], axis=1
+    )
+    by_tokens = (((0,), (0,)), ((), ()))
+    partial = lax.dot_general(inputs, own_grads, by_tokens, preferred_element_type=jnp.float32)
+    front_part = lax.dot_general(
+        prior_inputs[tokens - WINDOW :], front_grads, by_tokens, preferred_element_type=jnp.float32
+    )
+    q_span = query_blocks.shape[1]
+    partial = partial.at[:, q_span:].add(front_part)
+    owned = lax.psum_scatter(partial, ("seq", "lat"), scatter_dimension=0, tiled=True)
     q_width = HEADS * HEAD_DIM
     query_weight_grad = owned[:, :q_width]
     key_weight_grad = owned[:, q_width : q_width + kv_width]

time: 251 us -> 231 us (0.920)
  waiting for transfers between devices: 103 us -> 77.1 us
  matrix products: 72.3 us -> 75.2 us
  local copies, waits for them, and re-layouts: 42.6 us -> 45.4 us
    unnamed x2, waiting for transfers between devices: 82.6 us -> 57.4 us
    ppermute x2 -> x3, starting transfers between devices: 5.12 us -> 6.93 us  [shifted(): return lax.ppermute(block, axis, route)]
    ppermute x2 -> x3, waiting for transfers between devices: 20.8 us -> 19.7 us  [shifted(): return lax.ppermute(block, axis, route)]
    unnamed x93 -> x98, local copies, waits for them, and re-layouts: 15.1 us -> 15.8 us
    dot_general x1 -> x2, matrix products: 4.48 us -> 5.1 us  [the longest x1 3.31 us: body(): lax.dot_general(prior_inputs[tokens - WINDOW:], front_grads, by_tokens, p...]
  transfers between devices with their start and end apart: 3 -> 4, of which waited for: 2 -> 2; matrix products, arithmetic and copies ran while one was open for 15% -> 48% of each run, Pallas kernels for 0% -> 0%
where the time goes in v3:
time: 231 us; the launch traced here: 230 us
  waiting for transfers between devices  77.1 us (33%)
  matrix products  75.2 us (33%)
  local copies, waits for them, and re-layouts  45.4 us (20%)
  between operations  14.6 us (6%)
  other arithmetic  10.5 us (5%)
  starting transfers between devices  6.97 us (3%)
    unnamed x2, waiting for transfers between devices  57.4 us
    sub x4, matrix products, group_terms(): raised = jnp.exp(scores - peak)  27 us
    dot_general x4, matrix products, group_terms(): jnp.einsum('rqk,qrd->kd', probs_low, douts3, preferred_element_type=jnp.f...  21.9 us
    ppermute x3, waiting for transfers between devices, shifted(): return lax.ppermute(block, axis, route)  19.7 us
    unnamed x98, local copies, waits for them, and re-layouts  15.8 us
    slice x5, local copies, waits for them, and re-layouts, body(): queries[0:block, cols]  9.38 us
    slice x5, local copies, waits for them, and re-layouts, body(): douts[0:block, cols]  8.2 us
    ppermute x3, starting transfers between devices, shifted(): return lax.ppermute(block, axis, route)  6.93 us
  transfers between devices with their start and end apart: 4, of which 2 were waited for; matrix products, arithmetic and copies ran while one was open for 48% of the time, Pallas kernels for 0%

profile of v3, /device:TPU:0, one launch (start us, length us, event | category | flops | bytes accessed | tf_op | source)
XLA Modules:
  0.0 229.8 jit_solution(13736442957761807373)
XLA Ops:
  12.1 3.1 %collective-permute-start = (bf16[2,512,256]{1,2,0:T(8,128)(2,1)}, bf16[2,512,256]{1,2,0:T(8,128)(2,1)}, u32[]{:S(2)}, u32[]{:S(2)}) collective-permute-start(bf16[2,512,256]{1,2,0:T(8,128)(2,1)} %pad_maximum_fusion.3), channel_id=1, source_target_pairs={{12,0},{0,4},{4,8},{8,12},{13,1},{1,5},{5,9},{9,13},{14,2},{2,6},{... | collective-permute-start | bytes 1572872 | tf_op jit(solution)/shard_map/ppermute | solution.py:15
  16.7 2.2 fusion.140
  28.9 1.8 copy.61
  34.3 2.4 %slice_convert_fusion.7 = (f32[512,256]{1,0:T(8,128)S(1)}, f32[512,256]{1,0:T(8,128)}, f32[512,256]{1,0:T(8,128)}, f32[512,256]{1,0:T(8,128)}) fusion(bf16[512,1024]{1,0:T(8,128)(2,1)} %bitcast.257), kind=kLoop, calls=%fused_computation.133 | loop fusion | flops 524288 | bytes 3145728 | tf_op jit(solution)/shard_map/convert_element_type | solution.py:38
  38.2 2.0 copy.58
  40.2 2.0 copy.54
  48.3 2.0 slice_bitcast_fusion.4
  50.3 7.7 %fusion.149 = (f32[4,512]{1,0:T(4,128)}, f32[4,512,1024]{1,2,0:T(8,128)}) fusion(pred[512,1024]{0,1:T(8,128)(4,1)S(1)} %fusion.38, bf16[512,4,64]{0,2,1:T(8,128)(2,1)} %bitcast.276, bf16[512,256]{0,1:T(8,128)(2,1)S(1)} %get-tuple-element.121, bf16[512,256]{0,1:T(8,128)(2,1)S(1)} %bitcast.251), kind=kOutput, calls=%fused_computation.181 | convolution fusion | flops 277087232 | bytes 9707520 | tf_op jit(solution)/shard_map/sub | solution.py:34
  58.0 5.6 %fusion.51 = f32[1024,64]{0,1:T(8,128)} fusion(bf16[512,4,64]{0,2,1:T(8,128)(2,1)S(1)} %bitcast.280, f32[4,512,1024]{1,2,0:T(8,128)} %get-tuple-element.129, f32[4,512]{1,0:T(4,128)} %get-tuple-element.128), kind=kOutput, calls=%fused_computation.77 | convolution fusion | flops 272629760 | bytes 8921088 | tf_op jit(solution)/shard_map/rqk,qrd->kd/dot_general | solution.py:48
  67.6 6.7 %fusion.144 = (f32[4,512]{1,0:T(4,128)}, f32[4,512,1024]{1,2,0:T(8,128)}) fusion(pred[512,1024]{0,1:T(8,128)(4,1)} %copy-done.26, bf16[512,4,64]{0,2,1:T(8,128)(2,1)S(1)} %bitcast.270, bf16[512,256]{0,1:T(8,128)(2,1)S(1)} %get-tuple-element.121, bf16[512,256]{0,1:T(8,128)(2,1)S(1)} %bitcast.253), kind=kOutput, calls=%fused_computation.180 | convolution fusion | flops 277087232 | bytes 9707520 | tf_op jit(solution)/shard_map/sub | solution.py:34
  74.4 5.7 %fusion.54 = f32[1024,64]{0,1:T(8,128)} fusion(bf16[512,4,64]{0,2,1:T(8,128)(2,1)} %bitcast.278, f32[4,512,1024]{1,2,0:T(8,128)} %get-tuple-element.127, f32[4,512]{1,0:T(4,128)} %get-tuple-element.126), kind=kOutput, calls=%fused_computation.78 | convolution fusion | flops 272629760 | bytes 8921088 | tf_op jit(solution)/shard_map/rqk,qrd->kd/dot_general | solution.py:48
  81.9 2.1 fusion.45
  85.5 6.5 %fusion.143 = (f32[4,512]{1,0:T(4,128)}, f32[4,512,1024]{1,2,0:T(8,128)}) fusion(pred[512,1024]{0,1:T(8,128)(4,1)} %copy-done.26, bf16[1024,64,1]{0,1,2:T(8,128)(2,1)S(1)} %fusion.106, bf16[512,4,64]{0,2,1:T(8,128)(2,1)S(1)} %bitcast.264), kind=kOutput, calls=%fused_computation.179 | convolution fusion | flops 276825088 | bytes 9314304 | tf_op jit(solution)/shard_map/sub | solution.py:34
  92.1 5.7 %fusion.57 = f32[1024,64]{0,1:T(8,128)} fusion(bf16[512,4,64]{0,2,1:T(8,128)(2,1)} %bitcast.272, f32[4,512,1024]{1,2,0:T(8,128)} %get-tuple-element.125, f32[4,512]{1,0:T(4,128)} %get-tuple-element.124), kind=kOutput, calls=%fused_computation.79 | convolution fusion | flops 272629760 | bytes 8921088 | tf_op jit(solution)/shard_map/rqk,qrd->kd/dot_general | solution.py:48
  99.6 2.1 fusion.44
  103.3 5.9 %fusion.154 = (f32[4,512]{1,0:T(4,128)S(1)}, f32[4,512,1024]{1,2,0:T(8,128)}) fusion(pred[512,1024]{0,1:T(8,128)(4,1)} %copy-done.26, bf16[512,4,64]{0,2,1:T(8,128)(2,1)S(1)} %bitcast.258, bf16[512,256]{0,1:T(8,128)(2,1)S(1)} %get-tuple-element.121, bf16[512,256]{0,1:T(8,128)(2,1)S(1)} %bitcast.255), kind=kOutput, calls=%fused_computation.182 | convolution fusion | flops 277087232 | bytes 9707520 | tf_op jit(solution)/shard_map/sub | solution.py:34
  109.2 4.9 %fusion.48 = f32[1024,64]{0,1:T(8,128)S(1)} fusion(bf16[512,4,64]{0,2,1:T(8,128)(2,1)} %bitcast.266, f32[4,512,1024]{1,2,0:T(8,128)} %get-tuple-element.131, f32[4,512]{1,0:T(4,128)S(1)} %get-tuple-element.130), kind=kOutput, calls=%fused_computation.76 | convolution fusion | flops 272629760 | bytes 8921088 | tf_op jit(solution)/shard_map/rqk,qrd->kd/dot_general | solution.py:48
  122.1 2.6 %copy.97 = f32[1024,1536]{0,1:T(8,128)} copy(f32[1024,1536]{0,1:T(8,128)S(1)} %bitcast.249) | data formatting | bytes 12582912
  124.7 3.3 %fusion.37 = f32[1024,1536]{0,1:T(8,128)} fusion(f32[1024,1536]{0,1:T(8,128)} %copy.97, f32[1536,1024]{1,0:T(8,128)S(1)} %fusion.117, bf16[512,1024]{1,0:T(8,128)(2,1)} %collective-permute-done.2, bf16[512,256]{0,1:T(8,128)(2,1)S(1)} %get-tuple-element.106, bf16[512,256]{0,1:T(8,128)(2,1)S(1)} %get-tuple-element.104), kind=kOutput, calls=%fused_computation.54 | convolution fusion | flops 538443776 | bytes 5767168 | tf_op jit(solution)/shard_map/dot_general | solution.py:123
  128.0 6.6 %copy.87 = f32[1024,1536]{1,0:T(8,128)} copy(f32[1024,1536]{0,1:T(8,128)} %fusion.37) | data formatting | bytes 12582912
  135.9 2.3 %collective-permute-start.1 = (f32[2,512,256]{1,2,0:T(8,128)S(1)}, f32[2,512,256]{1,2,0:T(8,128)S(1)}, u32[]{:S(2)}, u32[]{:S(2)}) collective-permute-start(f32[2,512,256]{1,2,0:T(8,128)S(1)} %pad_maximum_fusion.2), channel_id=1, source_target_pairs={{4,0},{8,4},{12,8},{0,12},{5,1},{9,5},{13,9},{1,13},{6,2},{10,6},{... | collective-permute-start | bytes 3145736 | tf_op jit(solution)/shard_map/ppermute | solution.py:15
  138.2 2.4 %fusion.60 = f32[512,1024]{1,0:T(8,128)S(1)} fusion(bf16[1024,1024]{1,0:T(8,128)(2,1)S(1)} %copy-done, bf16[512,256]{0,1:T(8,128)(2,1)} %bitcast.268, bf16[512,256]{0,1:T(8,128)(2,1)} %bitcast.262, bf16[512,256]{0,1:T(8,128)(2,1)S(1)} %bitcast.261, bf16[512,256]{0,1:T(8,128)(2,1)} %bitcast.275), kind=kOutput, calls=%fused_computation.80 | convolution fusion | flops 1077936128 | bytes 5242880 | tf_op jit(solution)/shard_map/dot_general | solution.py:104
  140.7 19.7 %collective-permute-done.1 = f32[2,512,256]{1,2,0:T(8,128)S(1)} collective-permute-done((f32[2,512,256]{1,2,0:T(8,128)S(1)}, f32[2,512,256]{1,2,0:T(8,128)S(1)}, u32[]{:S(2)}, u32[]{:S(2)}) %collective-permute-start.1) | collective-permute-done | bytes 1048608 | tf_op jit(solution)/shard_map/ppermute | solution.py:15
  162.3 57.4 %reduce-scatter.4.cloned.1.call-done = f32[64,1536]{1,0:T(8,128)} async-done(((f32[1024,1536]{1,0:T(8,128)}), f32[64,1536]{1,0:T(8,128)}) %reduce-scatter.4.cloned.1.call-update) | async-done | bytes 393232
  (140 shorter events, 52.4 us)
Async XLA Ops:
  7.2 131.1 %copy-start = (bf16[1024,1024]{1,0:T(8,128)(2,1)S(1)}, bf16[1024,1024]{1,0:T(8,128)(2,1)}, u32[]{:S(2)}) copy-start(bf16[1024,1024]{1,0:T(8,128)(2,1)} %param.33) | copy-start | bytes 6291460
  7.2 18.9 %copy-start.20 = (bf16[1,512,1024]{2,1,0:T(8,128)(2,1)S(1)}, bf16[1,512,1024]{2,1,0:T(8,128)(2,1)}, u32[]{:S(2)}) copy-start(bf16[1,512,1024]{2,1,0:T(8,128)(2,1)} %param.32) | copy-start | bytes 3145732
  7.2 212.5 %reduce-scatter.4.cloned.1.call-start = ((), (), s32[]{:S(2)}) async-start(), calls=%async_computation.1 | async-start | bytes 6684672
  12.1 36.2 %collective-permute-start = (bf16[2,512,256]{1,2,0:T(8,128)(2,1)}, bf16[2,512,256]{1,2,0:T(8,128)(2,1)}, u32[]{:S(2)}, u32[]{:S(2)}) collective-permute-start(bf16[2,512,256]{1,2,0:T(8,128)(2,1)} %pad_maximum_fusion.3), channel_id=1, source_target_pairs={{12,0},{0,4},{4,8},{8,12},{13,1},{1,5},{5,9},{9,13},{14,2},{2,6},{... | collective-permute-start | bytes 1572872 | tf_op jit(solution)/shard_map/ppermute | solution.py:15
  15.2 109.5 %collective-permute-start.2 = (bf16[512,1024]{1,0:T(8,128)(2,1)}, bf16[512,1024]{1,0:T(8,128)(2,1)}, u32[]{:S(2)}, u32[]{:S(2)}) collective-permute-start(bf16[512,1024]{1,0:T(8,128)(2,1)} %bitcast.292), channel_id=1, source_target_pairs={{12,0},{0,4},{4,8},{8,12},{13,1},{1,5},{5,9},{9,13},{14,2},{2,6},{... | collective-permute-start | bytes 3145736 | tf_op jit(solution)/shard_map/ppermute | solution.py:15
  48.3 9.7 %copy-start.26 = (pred[512,1024]{0,1:T(8,128)(4,1)}, pred[512,1024]{0,1:T(8,128)(4,1)S(1)}, u32[]{:S(2)}) copy-start(pred[512,1024]{0,1:T(8,128)(4,1)S(1)} %fusion.38) | copy-start | bytes 1572868
  50.2 7.8 %copy-start.19 = (bf16[512,256]{0,1:T(8,128)(2,1)S(1)}, bf16[512,256]{0,1:T(8,128)(2,1)}, u32[]{:S(2)}) copy-start(bf16[512,256]{0,1:T(8,128)(2,1)} %copy.53) | copy-start | bytes 786436
  58.0 5.7 %copy-start.28 = (bf16[512,256]{0,1:T(8,128)(2,1)S(1)}, bf16[512,256]{0,1:T(8,128)(2,1)}, u32[]{:S(2)}) copy-start(bf16[512,256]{0,1:T(8,128)(2,1)} %get-tuple-element.120) | copy-start | bytes 786436
  58.0 6.0 %copy-start.39 = (f32[4,512,1024]{1,2,0:T(8,128)S(1)}, f32[4,512,1024]{1,2,0:T(8,128)}, u32[]{:S(2)}) copy-start(f32[4,512,1024]{1,2,0:T(8,128)} %get-tuple-element.129) | copy-start | bytes 25165828
  58.0 6.0 %copy-start.42 = (f32[4,512]{1,0:T(4,128)S(1)}, f32[4,512]{1,0:T(4,128)}, u32[]{:S(2)}) copy-start(f32[4,512]{1,0:T(4,128)} %get-tuple-element.128) | copy-start | bytes 24580
  67.6 51.4 %copy-start.6 = (bf16[64,4,512]{2,0,1:T(8,128)(2,1)}, bf16[64,4,512]{2,0,1:T(8,128)(2,1)S(1)}, u32[]{:S(2)}) copy-start(bf16[64,4,512]{2,0,1:T(8,128)(2,1)S(1)} %fusion.41) | copy-start | bytes 786436
  74.3 5.7 %copy-start.18 = (bf16[512,256]{0,1:T(8,128)(2,1)S(1)}, bf16[512,256]{0,1:T(8,128)(2,1)}, u32[]{:S(2)}) copy-start(bf16[512,256]{0,1:T(8,128)(2,1)} %copy.57) | copy-start | bytes 786436
  74.3 5.7 %copy-start.22 = (bf16[1,512,256]{1,2,0:T(8,128)(2,1)S(1)}, bf16[1,512,256]{1,2,0:T(8,128)(2,1)}, u32[]{:S(2)}) copy-start(bf16[1,512,256]{1,2,0:T(8,128)(2,1)} %copy.45) | copy-start | bytes 786436
  74.3 5.7 %copy-start.29 = (bf16[512,256]{0,1:T(8,128)(2,1)S(1)}, bf16[512,256]{0,1:T(8,128)(2,1)}, u32[]{:S(2)}) copy-start(bf16[512,256]{0,1:T(8,128)(2,1)} %get-tuple-element.120) | copy-start | bytes 786436
  74.3 5.7 %copy-start.35 = (f32[512,4]{0,1:T(4,128)S(1)}, f32[512,4]{0,1:T(4,128)}, u32[]{:S(2)}) copy-start(f32[512,4]{0,1:T(4,128)} %multiply_reduce_fusion.1) | copy-start | bytes 24580
  74.3 6.2 %copy-start.40 = (f32[4,512,1024]{1,2,0:T(8,128)S(1)}, f32[4,512,1024]{1,2,0:T(8,128)}, u32[]{:S(2)}) copy-start(f32[4,512,1024]{1,2,0:T(8,128)} %get-tuple-element.127) | copy-start | bytes 25165828
  74.4 6.2 %copy-start.43 = (f32[4,512]{1,0:T(4,128)S(1)}, f32[4,512]{1,0:T(4,128)}, u32[]{:S(2)}) copy-start(f32[4,512]{1,0:T(4,128)} %get-tuple-element.126) | copy-start | bytes 24580
  92.1 6.2 %copy-start.41 = (f32[4,512,1024]{1,2,0:T(8,128)S(1)}, f32[4,512,1024]{1,2,0:T(8,128)}, u32[]{:S(2)}) copy-start(f32[4,512,1024]{1,2,0:T(8,128)} %get-tuple-element.125) | copy-start | bytes 25165828
  92.1 6.2 %copy-start.44 = (f32[4,512]{1,0:T(4,128)S(1)}, f32[4,512]{1,0:T(4,128)}, u32[]{:S(2)}) copy-start(f32[4,512]{1,0:T(4,128)} %get-tuple-element.124) | copy-start | bytes 24580
  109.2 6.1 %copy-start.38 = (f32[4,512,1024]{1,2,0:T(8,128)S(1)}, f32[4,512,1024]{1,2,0:T(8,128)}, u32[]{:S(2)}) copy-start(f32[4,512,1024]{1,2,0:T(8,128)} %get-tuple-element.131) | copy-start | bytes 25165828
  134.6 25.7 %copy-start.25 = (bf16[1024,256]{1,0:T(8,128)(2,1)S(1)}, bf16[1024,256]{1,0:T(8,128)(2,1)}, u32[]{:S(2)}) copy-start(bf16[1024,256]{1,0:T(8,128)(2,1)} %param.34) | copy-start | bytes 1572868
  135.9 24.9 %copy-start.2 = (f32[1024,256]{0,1:T(8,128)S(1)}, f32[1024,256]{0,1:T(8,128)}, u32[]{:S(2)}) copy-start(f32[1024,256]{0,1:T(8,128)} %copy-done.1) | copy-start | bytes 3145732
  135.9 24.9 %copy-start.27 = (bf16[1024,256]{1,0:T(8,128)(2,1)S(1)}, bf16[1024,256]{1,0:T(8,128)(2,1)}, u32[]{:S(2)}) copy-start(bf16[1024,256]{1,0:T(8,128)(2,1)} %param.35) | copy-start | bytes 1572868
  135.9 24.4 %collective-permute-start.1 = (f32[2,512,256]{1,2,0:T(8,128)S(1)}, f32[2,512,256]{1,2,0:T(8,128)S(1)}, u32[]{:S(2)}, u32[]{:S(2)}) collective-permute-start(f32[2,512,256]{1,2,0:T(8,128)S(1)} %pad_maximum_fusion.2), channel_id=1, source_target_pairs={{4,0},{8,4},{12,8},{0,12},{5,1},{9,5},{13,9},{1,13},{6,2},{10,6},{... | collective-permute-start | bytes 3145736 | tf_op jit(solution)/shard_map/ppermute | solution.py:15
  (25 other events, 82.5 us)
Sparse Core Ops, SparseCore 0:
  134.7 84.9 reduce-scatter.3

commit v4 on v3

--- a/solution.py
+++ b/solution.py
@@ -1,6 +1,7 @@
 import jax
 import jax.numpy as jnp
 from jax import lax
+from jax.experimental import pallas as pl
 from jax.sharding import PartitionSpec as P
 
 HEADS = 16
@@ -15,38 +16,67 @@
     return lax.ppermute(block, axis, route)
 
 
-def group_terms(query_part, output_part, dout_part, key_part, value_part):
-    rows = query_part.shape[0]
-    span = key_part.shape[0]
+def attn_kernel(q_ref, o_ref, do_ref, k_ref, v_ref, dq_ref, dk_ref, dv_ref):
+    rows = q_ref.shape[0]
+    span = k_ref.shape[1]
     ratio = HEADS // KV_HEADS
     scale = HEAD_DIM ** (-0.5)
-    queries3 = query_part.reshape(rows, ratio, HEAD_DIM)
-    outputs3 = output_part.reshape(rows, ratio, HEAD_DIM)
-    douts3 = dout_part.reshape(rows, ratio, HEAD_DIM)
-    scores = (
-        jnp.einsum("qrd,kd->rqk", queries3, key_part, preferred_element_type=jnp.float32) * scale
-    )
-    row_index = jnp.arange(rows, dtype=jnp.int32)[:, None]
-    col_index = jnp.arange(span, dtype=jnp.int32)[None, :]
-    linked = (col_index > row_index) & (col_index <= row_index + WINDOW)
-    scores = jnp.where(linked[None], scores, -jnp.inf)
-    peak = jnp.max(scores, axis=-1, keepdims=True)
-    raised = jnp.exp(scores - peak)
-    probs = raised / jnp.sum(raised, axis=-1, keepdims=True)
-    probs_low = probs.astype(jnp.bfloat16)
-    dprobs = jnp.einsum("qrd,kd->rqk", douts3, value_part, preferred_element_type=jnp.float32)
-    delta = jnp.sum(douts3.astype(jnp.float32) * outputs3.astype(jnp.float32), axis=-1).T[
-        :, :, None
-    ]
-    dscores = (probs * (dprobs - delta)).astype(jnp.bfloat16)
-    query_grad = (
-        jnp.einsum("rqk,kd->qrd", dscores, key_part, preferred_element_type=jnp.float32) * scale
-    )
-    key_grad = (
-        jnp.einsum("rqk,qrd->kd", dscores, queries3, preferred_element_type=jnp.float32) * scale
-    )
-    value_grad = jnp.einsum("rqk,qrd->kd", probs_low, douts3, preferred_element_type=jnp.float32)
-    return (query_grad.reshape(rows, ratio * HEAD_DIM), key_grad, value_grad)
+    keys = k_ref[0]
+    values = v_ref[0]
+    row = lax.broadcasted_iota(jnp.int32, (rows, span), 0)
+    col = lax.broadcasted_iota(jnp.int32, (rows, span), 1)
+    linked = (col > row) & (col <= row + WINDOW)
+    by_rows = (((0,), (0,)), ((), ()))
+    by_cols = (((1,), (1,)), ((), ()))
+    dk = jnp.zeros((span, HEAD_DIM), jnp.float32)
+    dv = jnp.zeros((span, HEAD_DIM), jnp.float32)
+    for r in range(ratio):
+        sl = slice(r * HEAD_DIM, (r + 1) * HEAD_DIM)
+        q = q_ref[:, sl]
+        dout = do_ref[:, sl]
+        out = o_ref[:, sl]
+        s = lax.dot_general(q, keys, by_cols, preferred_element_type=jnp.float32) * scale
+        s = jnp.where(linked, s, -jnp.inf)
+        peak = jnp.max(s, axis=1, keepdims=True)
+        raised = jnp.exp(s - peak)
+        probs = raised / jnp.sum(raised, axis=1, keepdims=True)
+        dp = lax.dot_general(dout, values, by_cols, preferred_element_type=jnp.float32)
+        delta = jnp.sum(dout.astype(jnp.float32) * out.astype(jnp.float32), axis=1, keepdims=True)
+        ds = (probs * (dp - delta)).astype(jnp.bfloat16)
+        dq = jnp.dot(ds, keys, preferred_element_type=jnp.float32) * scale
+        dq_ref[:, sl] = dq.astype(dq_ref.dtype)
+        dk = dk + lax.dot_general(ds, q, by_rows, preferred_element_type=jnp.float32)
+        dv = dv + lax.dot_general(
+            probs.astype(jnp.bfloat16), dout, by_rows, preferred_element_type=jnp.float32
+        )
+    dk_ref[0] = dk * scale
+    dv_ref[0] = dv
+
+
+def attention_grads(queries, outputs, douts, ext_keys, ext_values, interpret=False):
+    rows, width_all = queries.shape
+    span, kv_width = ext_keys.shape
+    groups = kv_width // HEAD_DIM
+    width = width_all // groups
+    keys4 = ext_keys.reshape(span, groups, HEAD_DIM).transpose(1, 0, 2)
+    values4 = ext_values.reshape(span, groups, HEAD_DIM).transpose(1, 0, 2)
+    row_block = pl.BlockSpec((rows, width), lambda c: (0, c))
+    kv_block = pl.BlockSpec((1, span, HEAD_DIM), lambda c: (c, 0, 0))
+    dq, dk4, dv4 = pl.pallas_call(
+        attn_kernel,
+        grid=(groups,),
+        in_specs=[row_block, row_block, row_block, kv_block, kv_block],
+        out_specs=[row_block, kv_block, kv_block],
+        out_shape=[
+            jax.ShapeDtypeStruct((rows, width_all), jnp.bfloat16),
+            jax.ShapeDtypeStruct((groups, span, HEAD_DIM), jnp.float32),
+            jax.ShapeDtypeStruct((groups, span, HEAD_DIM), jnp.float32),
+        ],
+        interpret=interpret,
+    )(queries, outputs, douts, keys4, values4)
+    key_acc = dk4.transpose(1, 0, 2).reshape(span, kv_width)
+    value_acc = dv4.transpose(1, 0, 2).reshape(span, kv_width)
+    return dq, key_acc, value_acc
 
 
 def body(
@@ -75,27 +105,10 @@
     prior_inputs = shifted(inputs, "seq", 1)
     ext_keys = jnp.concatenate([prior_pair[0], keys_own], axis=0)
     ext_values = jnp.concatenate([prior_pair[1], values_own], axis=0)
-    key_acc = jnp.zeros((tokens + WINDOW, kv_width), jnp.float32)
-    value_acc = jnp.zeros((tokens + WINDOW, kv_width), jnp.float32)
-    query_list = []
-    key_list = []
-    value_list = []
-    for group in range(KV_HEADS):
-        cols = slice(group * width, (group + 1) * width)
-        kv_cols = slice(group * HEAD_DIM, (group + 1) * HEAD_DIM)
-        q_term, k_term, v_term = group_terms(
-            queries[0:block, cols],
-            outputs_own[0:block, cols],
-            douts[0:block, cols],
-            ext_keys[0 : block + WINDOW, kv_cols],
-            ext_values[0 : block + WINDOW, kv_cols],
-        )
-        query_list.append(q_term)
-        key_list.append(k_term)
-        value_list.append(v_term)
-    query_blocks = jnp.concatenate(query_list, 1).astype(jnp.bfloat16)
-    key_acc = key_acc.at[0 : block + WINDOW].add(jnp.concatenate(key_list, 1))
-    value_acc = value_acc.at[0 : block + WINDOW].add(jnp.concatenate(value_list, 1))
+    query_blocks, key_acc, value_acc = attention_grads(
+        queries[0:block], outputs_own[0:block], douts[0:block],
+        ext_keys[0 : block + WINDOW], ext_values[0 : block + WINDOW],
+    )
     front_pair = jnp.stack([key_acc[:WINDOW], value_acc[:WINDOW]])
     returned = shifted(front_pair, "seq", -1)
     key_grad = key_acc[WINDOW:].at[tokens - WINDOW :].add(returned[0]).astype(jnp.bfloat16)

time: 231 us -> 193 us (0.84)
  matrix products: 75.2 us -> 10.1 us
  Pallas kernels: 0 us -> 30.5 us
  waiting for transfers between devices: 77.1 us -> 85.7 us
  local copies, waits for them, and re-layouts: 45.4 us -> 39.9 us
  other arithmetic: 10.5 us -> 5.2 us
    dot_general x16 -> x0, matrix products: 38.8 us -> none  [the longest x4 21.9 us: group_terms(): jnp.einsum('rqk,qrd->kd', probs_low, douts3, preferred_element_type=jnp.f...]
    pallas_call x0 -> x1, Pallas kernels: none -> 30.5 us  [attention_grads(): pl.pallas_call(attn_kernel, grid=(groups,), in_specs=[row_block, row_bloc...]
    sub x4 -> x0, matrix products: 27 us -> none  [group_terms(): raised = jnp.exp(scores - peak)]
    ppermute x3, waiting for transfers between devices: 19.7 us -> 32.4 us  [shifted(): return lax.ppermute(block, axis, route)]
    slice x2 -> x5, local copies, waits for them, and re-layouts: 0.14 us -> 10.3 us  [body(): front_pair = jnp.stack([key_acc[:WINDOW], value_acc[:WINDOW]])]
    slice x10 -> x6, local copies, waits for them, and re-layouts: 17.6 us -> 9.52 us  [the longest x3 5.38 us: body(): value_acc[WINDOW:].at[tokens - WINDOW:].add(returned[1])]
    reduce_sum x4 -> x0, other arithmetic: 5.65 us -> none  [group_terms(): jnp.sum(douts3.astype(jnp.float32) * outputs3.astype(jnp.float32), axis=-1)]
    convert_element_type x4 -> x2, local copies, waits for them, and re-layouts: 5.51 us -> 1.1 us  [the longest x1 0.91 us: body(): key_acc[:WINDOW].astype(jnp.bfloat16)]
  transfers between devices with their start and end apart: 4 -> 4, of which waited for: 2 -> 3; matrix products, arithmetic and copies ran while one was open for 48% -> 20% of each run, Pallas kernels for 0% -> 16%
where the time goes in v4:
time: 193 us; the launch traced here: 192 us
  waiting for transfers between devices  85.7 us (44%)
  local copies, waits for them, and re-layouts  39.9 us (21%)
  Pallas kernels  30.5 us (16%)
  between operations  14.1 us (7%)
  matrix products  10.1 us (5%)
  starting transfers between devices  6.69 us (3%)
  other arithmetic  5.2 us (3%)
    unnamed x2, waiting for transfers between devices  53.3 us
    ppermute x3, waiting for transfers between devices, shifted(): return lax.ppermute(block, axis, route)  32.4 us
    pallas_call x1, Pallas kernels, attention_grads(): pl.pallas_call(attn_kernel, grid=(groups,), in_specs=[row_block, row_bloc...  30.5 us
    unnamed x16, local copies, waits for them, and re-layouts  11.6 us
    slice x5, local copies, waits for them, and re-layouts, body(): front_pair = jnp.stack([key_acc[:WINDOW], value_acc[:WINDOW]])  10.3 us
    ppermute x3, starting transfers between devices, shifted(): return lax.ppermute(block, axis, route)  6.65 us
    slice x3, local copies, waits for them, and re-layouts, body(): value_acc[WINDOW:].at[tokens - WINDOW:].add(returned[1])  5.38 us
  transfers between devices with their start and end apart: 4, of which 3 were waited for; matrix products, arithmetic and copies ran while one was open for 20% of the time, Pallas kernels for 16%

profile of v4, /device:TPU:0, one launch (start us, length us, event | category | flops | bytes accessed | tf_op | source)
XLA Modules:
  0.0 192.2 jit_solution(2937673754585673064)
XLA Ops:
  10.4 3.1 %collective-permute-start = (bf16[2,512,256]{1,2,0:T(8,128)(2,1)}, bf16[2,512,256]{1,2,0:T(8,128)(2,1)}, u32[]{:S(2)}, u32[]{:S(2)}) collective-permute-start(bf16[2,512,256]{1,2,0:T(8,128)(2,1)} %pad_maximum_fusion.1), channel_id=1, source_target_pairs={{12,0},{0,4},{4,8},{8,12},{13,1},{1,5},{5,9},{9,13},{14,2},{2,6},{... | collective-permute-start | bytes 1572872 | tf_op jit(solution)/shard_map/ppermute | solution.py:16
  13.5 1.6 collective-permute-start.2
  16.3 12.2 %collective-permute-done = bf16[2,512,256]{1,2,0:T(8,128)(2,1)} collective-permute-done((bf16[2,512,256]{1,2,0:T(8,128)(2,1)}, bf16[2,512,256]{1,2,0:T(8,128)(2,1)}, u32[]{:S(2)}, u32[]{:S(2)}) %collective-permute-start) | collective-permute-done | bytes 524320 | tf_op jit(solution)/shard_map/ppermute | solution.py:16
  28.6 1.8 fusion.24
  30.3 1.9 %copy.57 = bf16[512,4,64]{2,0,1:T(8,128)(2,1)} copy(bf16[512,4,64]{0,2,1:T(8,128)(2,1)} %bitcast.68) | data formatting | bytes 524288 | tf_op jit(solution)/shard_map/concatenate | solution.py:106
  33.3 3.0 %maximum_bitcast_fusion = (bf16[4,1024,64]{2,1,0:T(8,128)(2,1)}, bf16[4,1024,64]{2,1,0:T(8,128)(2,1)}) fusion(bf16[512,4,64]{2,0,1:T(8,128)(2,1)S(1)} %copy-done.1, bf16[512,4,64]{2,0,1:T(8,128)(2,1)} %copy.57, bf16[512,4,64]{2,0,1:T(8,128)(2,1)S(1)} %copy.61, bf16[512,4,64]{2,0,1:T(8,128)(2,1)} %copy.60), kind=kLoop, calls=%fused_computation.11 | loop fusion | flops 2097152 | bytes 2097152 | tf_op jit(solution)/shard_map/transpose | solution.py:61
  36.2 30.5 %shard_map.130 = (bf16[512,1024]{1,0:T(8,128)(2,1)}, f32[4,1024,64]{2,1,0:T(8,128)}, f32[4,1024,64]{2,1,0:T(8,128)}) custom-call(bf16[512,1024]{1,0:T(8,128)(2,1)} %bitcast.62, bf16[512,1024]{1,0:T(8,128)(2,1)} %bitcast.63, bf16[512,1024]{1,0:T(8,128)(2,1)} %bitcast.64, bf16[4,1024,64]{2,1,0:T(8,128)(2,1)} %get-tuple-element.86.k_ref, ...), custom_call_target="tpu_custom_call" | custom-call | tf_op jit(solution)/shard_map/pallas_call | solution.py:65
  68.2 3.0 %fusion.22 = (f32[512,4,64]{2,0,1:T(8,128)}, f32[512,4,64]{2,0,1:T(8,128)}) fusion(f32[1024,4,64]{2,0,1:T(8,128)} %bitcast.57), kind=kLoop, calls=%fused_computation.30 | loop fusion | bytes 2097152 | tf_op jit(solution)/shard_map/slice | solution.py:115
  71.2 1.5 copy.65
  75.8 3.0 %fusion.23 = (f32[512,4,64]{2,0,1:T(8,128)}, f32[512,4,64]{2,0,1:T(8,128)}) fusion(f32[1024,4,64]{2,0,1:T(8,128)} %bitcast.55), kind=kLoop, calls=%fused_computation.31 | loop fusion | bytes 2097152 | tf_op jit(solution)/shard_map/slice | solution.py:112
  78.8 1.5 copy.62
  81.2 3.6 %fusion.2 = f32[1536,1024]{1,0:T(8,128)S(1)} fusion(bf16[512,256]{1,0:T(8,128)(2,1)} %copy.67, bf16[512,256]{1,0:T(8,128)(2,1)} %copy.66, bf16[512,1024]{1,0:T(8,128)(2,1)} %get-tuple-element.59, bf16[1,512,1024]{2,1,0:T(8,128)(2,1)} %param.19), kind=kOutput, calls=%fused_computation.4 | convolution fusion | flops 1615331328 | bytes 8912896 | tf_op jit(solution)/shard_map/dot_general | solution.py:135
  84.8 2.6 %copy.78 = f32[1024,1536]{0,1:T(8,128)} copy(f32[1024,1536]{0,1:T(8,128)S(1)} %bitcast.49) | data formatting | bytes 12582912
  87.4 3.3 %fusion.1 = f32[1024,1536]{0,1:T(8,128)} fusion(f32[1024,1536]{0,1:T(8,128)} %copy.78, f32[1536,1024]{1,0:T(8,128)S(1)} %fusion.2, bf16[512,1024]{1,0:T(8,128)(2,1)} %collective-permute-done.2, bf16[512,256]{0,1:T(8,128)(2,1)S(1)} %bitcast.65, bf16[512,256]{0,1:T(8,128)(2,1)S(1)} %bitcast.66), kind=kOutput, calls=%fused_computation.2 | convolution fusion | flops 538443776 | bytes 5767168 | tf_op jit(solution)/shard_map/dot_general | solution.py:136
  90.7 6.6 %copy.73 = f32[1024,1536]{1,0:T(8,128)} copy(f32[1024,1536]{0,1:T(8,128)} %fusion.1) | data formatting | bytes 12582912
  97.3 2.3 %copy.64 = f32[512,4,64]{0,2,1:T(8,128)} copy(f32[512,4,64]{2,0,1:T(8,128)} %get-tuple-element.79) | data formatting | bytes 1048576 | tf_op jit(solution)/shard_map/slice | solution.py:112
  99.7 2.3 %copy.63 = f32[512,4,64]{0,2,1:T(8,128)} copy(f32[512,4,64]{2,0,1:T(8,128)} %get-tuple-element.80) | data formatting | bytes 1048576 | tf_op jit(solution)/shard_map/slice | solution.py:112
  102.0 1.4 pad_maximum_fusion
  103.4 2.0 %collective-permute-start.1 = (f32[2,512,256]{1,2,0:T(8,128)S(1)}, f32[2,512,256]{1,2,0:T(8,128)S(1)}, u32[]{:S(2)}, u32[]{:S(2)}) collective-permute-start(f32[2,512,256]{1,2,0:T(8,128)S(1)} %pad_maximum_fusion), channel_id=1, source_target_pairs={{4,0},{8,4},{12,8},{0,12},{5,1},{9,5},{13,9},{1,13},{6,2},{10,6},{... | collective-permute-start | bytes 3145736 | tf_op jit(solution)/shard_map/ppermute | solution.py:16
  106.8 20.1 %collective-permute-done.1 = f32[2,512,256]{1,2,0:T(8,128)S(1)} collective-permute-done((f32[2,512,256]{1,2,0:T(8,128)S(1)}, f32[2,512,256]{1,2,0:T(8,128)S(1)}, u32[]{:S(2)}, u32[]{:S(2)}) %collective-permute-start.1) | collective-permute-done | bytes 1048608 | tf_op jit(solution)/shard_map/ppermute | solution.py:16
  127.4 1.5 fusion.8
  128.9 53.3 %reduce-scatter.4.cloned.1.call-done = f32[64,1536]{1,0:T(8,128)} async-done(((f32[1024,1536]{1,0:T(8,128)}), f32[64,1536]{1,0:T(8,128)}) %reduce-scatter.4.cloned.1.call-update) | async-done | bytes 393232
  182.2 1.5 fusion.25
  183.7 1.7 slice.115
  (29 shorter events, 12.7 us)
Async XLA Ops:
  7.2 98.3 %copy-start = (bf16[1024,1024]{1,0:T(8,128)(2,1)S(1)}, bf16[1024,1024]{1,0:T(8,128)(2,1)}, u32[]{:S(2)}) copy-start(bf16[1024,1024]{1,0:T(8,128)(2,1)} %param.25) | copy-start | bytes 6291460
  7.2 175.0 %reduce-scatter.4.cloned.1.call-start = ((), (), s32[]{:S(2)}) async-start(), calls=%async_computation.1 | async-start | bytes 6684672
  10.4 18.2 %collective-permute-start = (bf16[2,512,256]{1,2,0:T(8,128)(2,1)}, bf16[2,512,256]{1,2,0:T(8,128)(2,1)}, u32[]{:S(2)}, u32[]{:S(2)}) collective-permute-start(bf16[2,512,256]{1,2,0:T(8,128)(2,1)} %pad_maximum_fusion.1), channel_id=1, source_target_pairs={{12,0},{0,4},{4,8},{8,12},{13,1},{1,5},{5,9},{9,13},{14,2},{2,6},{... | collective-permute-start | bytes 1572872 | tf_op jit(solution)/shard_map/ppermute | solution.py:16
  13.5 74.0 %collective-permute-start.2 = (bf16[512,1024]{1,0:T(8,128)(2,1)}, bf16[512,1024]{1,0:T(8,128)(2,1)}, u32[]{:S(2)}, u32[]{:S(2)}) collective-permute-start(bf16[512,1024]{1,0:T(8,128)(2,1)} %bitcast.69), channel_id=1, source_target_pairs={{12,0},{0,4},{4,8},{8,12},{13,1},{1,5},{5,9},{9,13},{14,2},{2,6},{... | collective-permute-start | bytes 3145736 | tf_op jit(solution)/shard_map/ppermute | solution.py:16
  16.3 17.0 %copy-start.1 = (bf16[512,4,64]{2,0,1:T(8,128)(2,1)S(1)}, bf16[512,4,64]{2,0,1:T(8,128)(2,1)}, u32[]{:S(2)}) copy-start(bf16[512,4,64]{2,0,1:T(8,128)(2,1)} %copy.58) | copy-start | bytes 786436
  84.8 2.7 %copy-start.2 = (bf16[512,4,64]{0,2,1:T(8,128)(2,1)S(1)}, bf16[512,4,64]{0,2,1:T(8,128)(2,1)}, u32[]{:S(2)}) copy-start(bf16[512,4,64]{0,2,1:T(8,128)(2,1)} %copy.68) | copy-start | bytes 786436
  102.0 3.4 %copy-start.5 = (bf16[512,1024]{1,0:T(8,128)(2,1)S(1)}, bf16[512,1024]{1,0:T(8,128)(2,1)}, u32[]{:S(2)}) copy-start(bf16[512,1024]{1,0:T(8,128)(2,1)} %get-tuple-element.59) | copy-start | bytes 3145732
  103.4 23.5 %copy-start.3 = (bf16[1024,256]{1,0:T(8,128)(2,1)S(1)}, bf16[1024,256]{1,0:T(8,128)(2,1)}, u32[]{:S(2)}) copy-start(bf16[1024,256]{1,0:T(8,128)(2,1)} %param.26) | copy-start | bytes 1572868
  103.4 23.5 %collective-permute-start.1 = (f32[2,512,256]{1,2,0:T(8,128)S(1)}, f32[2,512,256]{1,2,0:T(8,128)S(1)}, u32[]{:S(2)}, u32[]{:S(2)}) collective-permute-start(f32[2,512,256]{1,2,0:T(8,128)S(1)} %pad_maximum_fusion), channel_id=1, source_target_pairs={{4,0},{8,4},{12,8},{0,12},{5,1},{9,5},{13,9},{1,13},{6,2},{10,6},{... | collective-permute-start | bytes 3145736 | tf_op jit(solution)/shard_map/ppermute | solution.py:16
  106.7 20.7 %copy-start.4 = (bf16[1024,256]{1,0:T(8,128)(2,1)S(1)}, bf16[1024,256]{1,0:T(8,128)(2,1)}, u32[]{:S(2)}) copy-start(bf16[1024,256]{1,0:T(8,128)(2,1)} %param.27) | copy-start | bytes 1572868
Sparse Core Ops, SparseCore 0:
  97.4 84.6 reduce-scatter.3

commit v5 on v4

v5 whole, which is shorter than its diff:
```python
import jax
import jax.numpy as jnp
from jax import lax
from jax.experimental import pallas as pl
from jax.experimental.pallas import tpu as pltpu
from jax.sharding import PartitionSpec as P

HEADS = 16
HEAD_DIM = 64
KV_HEADS = 4
WINDOW = 512
ROW_BLOCK = 256


def shifted(block, axis, distance):
    devices = range(lax.axis_size(axis))
    route = [((i - distance) % len(devices), i) for i in devices]
    return lax.ppermute(block, axis, route)


def attn_kernel(q_ref, o_ref, do_ref, k_ref, v_ref, own_ref, front_ref, own32_ref, front32_ref,
                dk_scr, dv_scr):
    rows = q_ref.shape[0]
    ratio = HEADS // KV_HEADS
    scale = HEAD_DIM ** (-0.5)
    span = ROW_BLOCK + WINDOW
    q_width = HEADS * HEAD_DIM
    kv_width = KV_HEADS * HEAD_DIM
    row = lax.broadcasted_iota(jnp.int32, (ROW_BLOCK, span), 0)
    col = lax.broadcasted_iota(jnp.int32, (ROW_BLOCK, span), 1)
    linked = (col > row) & (col <= row + WINDOW)
    by_rows = (((0,), (0,)), ((), ()))
    by_cols = (((1,), (1,)), ((), ()))
    for c in range(KV_HEADS):
        kv_cols = slice(c * HEAD_DIM, (c + 1) * HEAD_DIM)
        dk_scr[...] = jnp.zeros(dk_scr.shape, jnp.float32)
        dv_scr[...] = jnp.zeros(dv_scr.shape, jnp.float32)

        def row_step(a, carry):
            top = a * ROW_BLOCK
            keys = k_ref[c, pl.ds(top, span), :]
            values = v_ref[c, pl.ds(top, span), :]
            dk = jnp.zeros((HEAD_DIM, span), jnp.float32)
            dv = jnp.zeros((HEAD_DIM, span), jnp.float32)
            for r in range(ratio):
                sl = slice((c * ratio + r) * HEAD_DIM, (c * ratio + r + 1) * HEAD_DIM)
                q = q_ref[pl.ds(top, ROW_BLOCK), sl]
                q_scaled = q * jnp.asarray(scale, q.dtype)
                dout = do_ref[pl.ds(top, ROW_BLOCK), sl]
                out = o_ref[pl.ds(top, ROW_BLOCK), sl]
                s = lax.dot_general(q_scaled, keys, by_cols, preferred_element_type=jnp.float32)
                s = jnp.where(linked, s, -jnp.inf)
                peak = jnp.max(s, axis=1, keepdims=True)
                raised = jnp.exp(s - peak)
                probs = raised * (1.0 / jnp.sum(raised, axis=1, keepdims=True))
                dp = lax.dot_general(dout, values, by_cols, preferred_element_type=jnp.float32)
                delta = jnp.sum(
                    dout.astype(jnp.float32) * out.astype(jnp.float32), axis=1, keepdims=True
                )
                ds = (probs * (dp - delta)).astype(jnp.bfloat16)
                dq = jnp.dot(ds, keys, preferred_element_type=jnp.float32) * scale
                own_ref[pl.ds(top, ROW_BLOCK), sl] = dq.astype(own_ref.dtype)
                dk = dk + lax.dot_general(q, ds, by_rows, preferred_element_type=jnp.float32)
                dv = dv + lax.dot_general(
                    dout, probs.astype(jnp.bfloat16), by_rows, preferred_element_type=jnp.float32
                )
            dk_scr[:, top : top + span] += dk
            dv_scr[:, top : top + span] += dv
            return carry

        for a in range(rows // ROW_BLOCK):
            row_step(a, 0)
        dk_all = dk_scr[...].T * scale
        dv_all = dv_scr[...].T
        k_cols = slice(q_width + c * HEAD_DIM, q_width + (c + 1) * HEAD_DIM)
        v_cols = slice(q_width + kv_width + c * HEAD_DIM, q_width + kv_width + (c + 1) * HEAD_DIM)
        own_ref[:, k_cols] = dk_all[WINDOW:].astype(own_ref.dtype)
        own_ref[:, v_cols] = dv_all[WINDOW:].astype(own_ref.dtype)
        front_ref[:, kv_cols] = dk_all[:WINDOW].astype(front_ref.dtype)
        front_ref[:, slice(kv_width + c * HEAD_DIM, kv_width + (c + 1) * HEAD_DIM)] = (
            dv_all[:WINDOW].astype(front_ref.dtype)
        )
        own32_ref[0, :, kv_cols] = dk_all[WINDOW:]
        own32_ref[1, :, kv_cols] = dv_all[WINDOW:]
        front32_ref[0, :, kv_cols] = dk_all[:WINDOW]
        front32_ref[1, :, kv_cols] = dv_all[:WINDOW]


def attention_grads(queries, outputs, douts, ext_keys, ext_values):
    rows, q_width = queries.shape
    span, kv_width = ext_keys.shape
    ext_keys = ext_keys.reshape(span, KV_HEADS, HEAD_DIM).transpose(1, 0, 2)
    ext_values = ext_values.reshape(span, KV_HEADS, HEAD_DIM).transpose(1, 0, 2)
    vmem = pltpu.MemorySpace.VMEM if hasattr(pltpu, "MemorySpace") else pltpu.VMEM
    return pl.pallas_call(
        attn_kernel,
        out_shape=[
            jax.ShapeDtypeStruct((rows, q_width + 2 * kv_width), jnp.bfloat16),
            jax.ShapeDtypeStruct((span - rows, 2 * kv_width), jnp.bfloat16),
            jax.ShapeDtypeStruct((2, rows, kv_width), jnp.float32),
            jax.ShapeDtypeStruct((2, span - rows, kv_width), jnp.float32),
        ],
        scratch_shapes=[
            pltpu.VMEM((HEAD_DIM, span), jnp.float32),
            pltpu.VMEM((HEAD_DIM, span), jnp.float32),
        ],
    )(queries, outputs, douts, ext_keys, ext_values)


def body(
    layer_input,
    query_rows,
    key_rows,
    value_rows,
    saved_output,
    output_grad,
    weight_query,
    weight_key,
    weight_value,
):
    inputs = layer_input[0]
    queries = query_rows[0]
    keys_own = key_rows[0]
    values_own = value_rows[0]
    outputs_own = saved_output[0]
    douts = output_grad[0]
    tokens = queries.shape[0]
    kv_width = keys_own.shape[1]
    width = HEADS // KV_HEADS * HEAD_DIM
    block = min(512, tokens)
    prior_keys = shifted(keys_own, "seq", 1)
    prior_values = shifted(values_own, "seq", 1)
    prior_inputs = shifted(inputs, "seq", 1)
    ext_keys = jnp.concatenate([prior_keys, keys_own], axis=0)
    ext_values = jnp.concatenate([prior_values, values_own], axis=0)
    own_grads, front_grads, own32, front32 = attention_grads(
        queries, outputs_own, douts, ext_keys, ext_values
    )
    q_span = HEADS * HEAD_DIM
    query_blocks = own_grads[:, :q_span]
    returned = shifted(front32, "seq", -1)
    key_grad = own32[0].at[tokens - WINDOW :].add(returned[0]).astype(jnp.bfloat16)
    value_grad = own32[1].at[tokens - WINDOW :].add(returned[1]).astype(jnp.bfloat16)
    contract_cols = (((1,), (1,)), ((), ()))
    summed = lax.dot_general(
        query_blocks, weight_query, contract_cols, preferred_element_type=jnp.float32
    )
    summed = summed + lax.dot_general(
        key_grad, weight_key, contract_cols, preferred_element_type=jnp.float32
    )
    summed = summed + lax.dot_general(
        value_grad, weight_value, contract_cols, preferred_element_type=jnp.float32
    )
    input_grad = summed.astype(jnp.bfloat16)[None]
    by_tokens = (((0,), (0,)), ((), ()))
    partial = lax.dot_general(inputs, own_grads, by_tokens, preferred_element_type=jnp.float32)
    front_part = lax.dot_general(
        prior_inputs[tokens - WINDOW :], front_grads, by_tokens, preferred_element_type=jnp.float32
    )
    partial = partial.at[:, q_span:].add(front_part)
    owned = lax.psum_scatter(partial, ("seq", "lat"), scatter_dimension=0, tiled=True)
    q_width = HEADS * HEAD_DIM
    query_weight_grad = owned[:, :q_width]
    key_weight_grad = owned[:, q_width : q_width + kv_width]
    value_weight_grad = owned[:, q_width + kv_width :]
    return (input_grad, query_weight_grad, key_weight_grad, value_weight_grad)


def solution(mesh):
    placed = (
        P(("parts", "lat"), "seq", None),
        P(("parts", "lat"), "seq", None),
        P(("parts", "lat"), "seq", None),
        P(("parts", "lat"), "seq", None),
        P(("parts", "lat"), "seq", None),
        P(("parts", "lat"), "seq", None),
        P(),
        P(),
        P(),
    )
    return jax.shard_map(
        body,
        mesh=mesh,
        in_specs=placed,
        out_specs=(
            P(("parts", "lat"), "seq", None),
            P(("parts", "seq", "lat"), None),
            P(("parts", "seq", "lat"), None),
            P(("parts", "seq", "lat"), None),
        ),
        check_vma=False,
    )
```

time: 193 us -> 195 us (1.010)
  waiting for transfers between devices: 85.7 us -> 104 us
  local copies, waits for them, and re-layouts: 39.9 us -> 21.9 us
  other arithmetic: 5.2 us -> 2.95 us
    slice x11 -> x0, local copies, waits for them, and re-layouts: 19.8 us -> none  [the longest x5 10.3 us: body(): front_pair = jnp.stack([key_acc[:WINDOW], value_acc[:WINDOW]])]
    ppermute x3 -> x4, waiting for transfers between devices: 32.4 us -> 47.2 us  [shifted(): return lax.ppermute(block, axis, route)]
    unnamed x2, waiting for transfers between devices: 53.3 us -> 57.1 us
    another operation x2 -> x0, other arithmetic: 2.24 us -> none  [the longest x1 1.4 us: body(): front_pair = jnp.stack([key_acc[:WINDOW], value_acc[:WINDOW]])]
    unnamed x16 -> x18, local copies, waits for them, and re-layouts: 11.6 us -> 13.3 us
    ppermute x3 -> x4, starting transfers between devices: 6.65 us -> 8.05 us  [shifted(): return lax.ppermute(block, axis, route)]
  transfers between devices with their start and end apart: 4 -> 5, of which waited for: 3 -> 4; matrix products, arithmetic and copies ran while one was open for 20% -> 11% of each run, Pallas kernels for 16% -> 17%
where the time goes in v5:
time: 195 us
  waiting for transfers between devices  104 us (53%)
  Pallas kernels  32.1 us (16%)
  local copies, waits for them, and re-layouts  21.9 us (11%)
  between operations  14.1 us (7%)
  matrix products  11 us (6%)
  starting transfers between devices  8.08 us (4%)
  other arithmetic  2.95 us (2%)
    unnamed x2, waiting for transfers between devices  57.1 us
    ppermute x4, waiting for transfers between devices, shifted(): return lax.ppermute(block, axis, route)  47.2 us
    pallas_call x1, Pallas kernels, attention_grads(): pl.pallas_call(attn_kernel, out_shape=[jax.ShapeDtypeStruct((rows, q_widt...  32.1 us
    unnamed x18, local copies, waits for them, and re-layouts  13.3 us
    ppermute x4, starting transfers between devices, shifted(): return lax.ppermute(block, axis, route)  8.05 us
  transfers between devices with their start and end apart: 5, of which 4 were waited for; matrix products, arithmetic and copies ran while one was open for 11% of the time, Pallas kernels for 17%

profile of v5, /device:TPU:0, one launch (start us, length us, event | category | flops | bytes accessed | tf_op | source)
XLA Modules:
  0.0 194.5 jit_solution(6047551398675773227)
XLA Ops:
  7.2 3.1 %collective-permute-start.3 = (bf16[512,1024]{1,0:T(8,128)(2,1)}, bf16[512,1024]{1,0:T(8,128)(2,1)}, u32[]{:S(2)}, u32[]{:S(2)}) collective-permute-start(bf16[512,1024]{1,0:T(8,128)(2,1)} %bitcast.42), channel_id=1, source_target_pairs={{12,0},{0,4},{4,8},{8,12},{13,1},{1,5},{5,9},{9,13},{14,2},{2,6},{... | collective-permute-start | bytes 3145736 | tf_op jit(solution)/shard_map/ppermute | solution.py:18
  10.3 1.8 copy.31
  12.1 1.6 collective-permute-start.1
  13.7 1.1 copy.27
  14.8 1.6 collective-permute-start
  16.4 1.2 copy.34
  17.9 24.4 %collective-permute-done.1 = bf16[512,256]{0,1:T(8,128)(2,1)} collective-permute-done((bf16[512,256]{0,1:T(8,128)(2,1)}, bf16[512,256]{0,1:T(8,128)(2,1)}, u32[]{:S(2)}, u32[]{:S(2)}) %collective-permute-start.1) | collective-permute-done | bytes 262176 | tf_op jit(solution)/shard_map/ppermute | solution.py:18
  42.3 2.0 %copy.33 = bf16[512,4,64]{2,0,1:T(8,128)(2,1)} copy(bf16[512,4,64]{0,2,1:T(8,128)(2,1)} %bitcast.8) | data formatting | bytes 524288 | tf_op jit(solution)/shard_map/concatenate | solution.py:135
  44.3 2.8 %collective-permute-done = bf16[512,256]{0,1:T(8,128)(2,1)} collective-permute-done((bf16[512,256]{0,1:T(8,128)(2,1)S(1)}, bf16[512,256]{0,1:T(8,128)(2,1)}, u32[]{:S(2)}, u32[]{:S(2)}) %collective-permute-start) | collective-permute-done | bytes 262176 | tf_op jit(solution)/shard_map/ppermute | solution.py:18
  47.1 2.0 %copy.29 = bf16[512,4,64]{2,0,1:T(8,128)(2,1)} copy(bf16[512,4,64]{0,2,1:T(8,128)(2,1)} %bitcast.4) | data formatting | bytes 524288 | tf_op jit(solution)/shard_map/concatenate | solution.py:134
  49.0 2.9 %maximum_bitcast_fusion = (bf16[4,1024,64]{2,1,0:T(8,128)(2,1)}, bf16[4,1024,64]{2,1,0:T(8,128)(2,1)}) fusion(bf16[512,4,64]{2,0,1:T(8,128)(2,1)S(1)} %copy.30, bf16[512,4,64]{2,0,1:T(8,128)(2,1)} %copy.29, bf16[512,4,64]{2,0,1:T(8,128)(2,1)S(1)} %copy.34, bf16[512,4,64]{2,0,1:T(8,128)(2,1)} %copy.33), kind=kLoop, calls=%fused_computation.5 | loop fusion | flops 2097152 | bytes 2097152 | tf_op jit(solution)/shard_map/transpose | solution.py:92
  52.0 32.1 %shard_map.130 = (bf16[512,1536]{1,0:T(8,128)(2,1)}, bf16[512,512]{1,0:T(8,128)(2,1)}, f32[2,512,256]{2,1,0:T(8,128)}, f32[2,512,256]{2,1,0:T(8,128)}) custom-call(bf16[512,1024]{1,0:T(8,128)(2,1)} %bitcast.37, bf16[512,1024]{1,0:T(8,128)(2,1)} %bitcast.38, bf16[512,1024]{1,0:T(8,128)(2,1)} %bitcast.39, bf16[4,1024,64]{2,1,0:T(8,128)(2,1)} %get-tuple-element.78.k_ref, ...), custom_call_target="tpu_custom_call" | custom-call | tf_op jit(solution)/shard_map/pallas_call | solution.py:95
  84.1 3.2 %fusion.12 = f32[1536,1024]{1,0:T(8,128)S(1)} fusion(bf16[512,1536]{1,0:T(8,128)(2,1)} %get-tuple-element.60, bf16[1,512,1024]{2,1,0:T(8,128)(2,1)S(1)} %copy-done.5), kind=kOutput, calls=%fused_computation.16 | convolution fusion | flops 1610612736 | bytes 8912896 | tf_op jit(solution)/shard_map/dot_general | solution.py:156
  87.4 2.6 %copy.43 = f32[1024,1536]{0,1:T(8,128)} copy(f32[1024,1536]{0,1:T(8,128)S(1)} %bitcast.36) | data formatting | bytes 12582912
  90.0 3.3 %fusion.1 = f32[1024,1536]{0,1:T(8,128)} fusion(f32[1024,1536]{0,1:T(8,128)} %copy.43, f32[1536,1024]{1,0:T(8,128)S(1)} %fusion.12, bf16[512,512]{1,0:T(8,128)(2,1)S(1)} %copy-done.4, bf16[512,1024]{1,0:T(8,128)(2,1)} %collective-permute-done.3), kind=kOutput, calls=%fused_computation.2 | convolution fusion | flops 537395200 | bytes 5767168 | tf_op jit(solution)/shard_map/dot_general | solution.py:157
  93.3 6.6 %copy.38 = f32[1024,1536]{1,0:T(8,128)} copy(f32[1024,1536]{0,1:T(8,128)} %fusion.1) | data formatting | bytes 12582912
  99.9 1.2 copy-done.6
  101.1 1.7 collective-permute-start.2
  102.9 2.5 %fusion.3 = f32[512,1024]{1,0:T(8,128)S(1)} fusion(bf16[1024,1024]{1,0:T(8,128)(2,1)S(1)} %copy-done, bf16[512,1536]{1,0:T(8,128)(2,1)} %get-tuple-element.60), kind=kOutput, calls=%fused_computation.7 | convolution fusion | flops 1073741824 | bytes 5242880 | tf_op jit(solution)/shard_map/dot_general | solution.py:145
  105.4 20.1 %collective-permute-done.2 = f32[2,512,256]{2,1,0:T(8,128)S(1)} collective-permute-done((f32[2,512,256]{2,1,0:T(8,128)S(1)}, f32[2,512,256]{2,1,0:T(8,128)S(1)}, u32[]{:S(2)}, u32[]{:S(2)}) %collective-permute-start.2) | collective-permute-done | bytes 1048608 | tf_op jit(solution)/shard_map/ppermute | solution.py:18
  125.9 1.5 fusion.2
  127.4 57.1 %reduce-scatter.4.cloned.1.call-done = f32[64,1536]{1,0:T(8,128)} async-done(((f32[1024,1536]{1,0:T(8,128)}), f32[64,1536]{1,0:T(8,128)}) %reduce-scatter.4.cloned.1.call-update) | async-done | bytes 393232
  184.5 1.5 fusion.14
  186.0 1.7 slice.83
  (18 shorter events, 0.8 us)
Async XLA Ops:
  7.2 95.7 %copy-start = (bf16[1024,1024]{1,0:T(8,128)(2,1)S(1)}, bf16[1024,1024]{1,0:T(8,128)(2,1)}, u32[]{:S(2)}) copy-start(bf16[1024,1024]{1,0:T(8,128)(2,1)} %param.25) | copy-start | bytes 6291460
  7.2 177.3 %reduce-scatter.4.cloned.1.call-start = ((), (), s32[]{:S(2)}) async-start(), calls=%async_computation.1 | async-start | bytes 6684672
  7.2 82.8 %collective-permute-start.3 = (bf16[512,1024]{1,0:T(8,128)(2,1)}, bf16[512,1024]{1,0:T(8,128)(2,1)}, u32[]{:S(2)}, u32[]{:S(2)}) collective-permute-start(bf16[512,1024]{1,0:T(8,128)(2,1)} %bitcast.42), channel_id=1, source_target_pairs={{12,0},{0,4},{4,8},{8,12},{13,1},{1,5},{5,9},{9,13},{14,2},{2,6},{... | collective-permute-start | bytes 3145736 | tf_op jit(solution)/shard_map/ppermute | solution.py:18
  12.1 30.2 %collective-permute-start.1 = (bf16[512,256]{0,1:T(8,128)(2,1)}, bf16[512,256]{0,1:T(8,128)(2,1)}, u32[]{:S(2)}, u32[]{:S(2)}) collective-permute-start(bf16[512,256]{0,1:T(8,128)(2,1)} %bitcast.7), channel_id=1, source_target_pairs={{12,0},{0,4},{4,8},{8,12},{13,1},{1,5},{5,9},{9,13},{14,2},{2,6},{... | collective-permute-start | bytes 786440 | tf_op jit(solution)/shard_map/ppermute | solution.py:18
  14.8 32.3 %collective-permute-start = (bf16[512,256]{0,1:T(8,128)(2,1)S(1)}, bf16[512,256]{0,1:T(8,128)(2,1)}, u32[]{:S(2)}, u32[]{:S(2)}) collective-permute-start(bf16[512,256]{0,1:T(8,128)(2,1)S(1)} %bitcast.40), channel_id=1, source_target_pairs={{12,0},{0,4},{4,8},{8,12},{13,1},{1,5},{5,9},{9,13},{14,2},{2,6},{... | collective-permute-start | bytes 786440 | tf_op jit(solution)/shard_map/ppermute | solution.py:18
  52.0 32.1 %copy-start.5 = (bf16[1,512,1024]{2,1,0:T(8,128)(2,1)S(1)}, bf16[1,512,1024]{2,1,0:T(8,128)(2,1)}, u32[]{:S(2)}) copy-start(bf16[1,512,1024]{2,1,0:T(8,128)(2,1)} %param.19) | copy-start | bytes 3145732
  87.4 2.7 %copy-start.4 = (bf16[512,512]{1,0:T(8,128)(2,1)S(1)}, bf16[512,512]{1,0:T(8,128)(2,1)}, u32[]{:S(2)}) copy-start(bf16[512,512]{1,0:T(8,128)(2,1)} %get-tuple-element.63) | copy-start | bytes 1572868
  99.9 1.2 copy-start.6
  101.1 24.3 %copy-start.1 = (f32[2,512,256]{2,1,0:T(8,128)S(1)}, f32[2,512,256]{2,1,0:T(8,128)}, u32[]{:S(2)}) copy-start(f32[2,512,256]{2,1,0:T(8,128)} %get-tuple-element.61) | copy-start | bytes 3145732
  101.1 24.3 %copy-start.2 = (bf16[1024,256]{1,0:T(8,128)(2,1)S(1)}, bf16[1024,256]{1,0:T(8,128)(2,1)}, u32[]{:S(2)}) copy-start(bf16[1024,256]{1,0:T(8,128)(2,1)} %param.26) | copy-start | bytes 1572868
  101.1 24.3 %collective-permute-start.2 = (f32[2,512,256]{2,1,0:T(8,128)S(1)}, f32[2,512,256]{2,1,0:T(8,128)S(1)}, u32[]{:S(2)}, u32[]{:S(2)}) collective-permute-start(f32[2,512,256]{2,1,0:T(8,128)S(1)} %copy-done.6), channel_id=1, source_target_pairs={{4,0},{8,4},{12,8},{0,12},{5,1},{9,5},{13,9},{1,13},{6,2},{10,6},{... | collective-permute-start | bytes 3145736 | tf_op jit(solution)/shard_map/ppermute | solution.py:18
  105.4 20.6 %copy-start.3 = (bf16[1024,256]{1,0:T(8,128)(2,1)S(1)}, bf16[1024,256]{1,0:T(8,128)(2,1)}, u32[]{:S(2)}) copy-start(bf16[1024,256]{1,0:T(8,128)(2,1)} %param.27) | copy-start | bytes 1572868
Sparse Core Ops, SparseCore 0:
  100.0 84.4 reduce-scatter.3

commit v6 on v5

--- a/solution.py
+++ b/solution.py
@@ -38,8 +38,8 @@
 
         def row_step(a, carry):
             top = a * ROW_BLOCK
-            keys = k_ref[c, pl.ds(top, span), :]
-            values = v_ref[c, pl.ds(top, span), :]
+            keys = k_ref[top : top + span, kv_cols]
+            values = v_ref[top : top + span, kv_cols]
             dk = jnp.zeros((HEAD_DIM, span), jnp.float32)
             dv = jnp.zeros((HEAD_DIM, span), jnp.float32)
             for r in range(ratio):
@@ -89,8 +89,6 @@
 def attention_grads(queries, outputs, douts, ext_keys, ext_values):
     rows, q_width = queries.shape
     span, kv_width = ext_keys.shape
-    ext_keys = ext_keys.reshape(span, KV_HEADS, HEAD_DIM).transpose(1, 0, 2)
-    ext_values = ext_values.reshape(span, KV_HEADS, HEAD_DIM).transpose(1, 0, 2)
     vmem = pltpu.MemorySpace.VMEM if hasattr(pltpu, "MemorySpace") else pltpu.VMEM
     return pl.pallas_call(
         attn_kernel,
@@ -105,6 +103,36 @@
             pltpu.VMEM((HEAD_DIM, span), jnp.float32),
         ],
     )(queries, outputs, douts, ext_keys, ext_values)
+
+
+def wgrad_kernel(x_ref, xp_ref, own_ref, front_ref, out_ref):
+    by_rows = (((0,), (0,)), ((), ()))
+    q_width = out_ref.shape[1] - front_ref.shape[1]
+    own_part = lax.dot_general(x_ref[...], own_ref[...], by_rows, preferred_element_type=jnp.float32)
+    front_part = lax.dot_general(
+        xp_ref[...], front_ref[...], by_rows, preferred_element_type=jnp.float32
+    )
+    out_ref[:, :q_width] = own_part[:, :q_width]
+    out_ref[:, q_width:] = own_part[:, q_width:] + front_part
+
+
+def weight_partial(inputs, prior_inputs, own_grads, front_grads):
+    tokens, model = inputs.shape
+    width = own_grads.shape[1]
+    cols = 256 if model % 256 == 0 else model
+    x_block = pl.BlockSpec((tokens, cols), lambda i: (0, i))
+    return pl.pallas_call(
+        wgrad_kernel,
+        grid=(model // cols,),
+        in_specs=[
+            x_block,
+            x_block,
+            pl.BlockSpec(own_grads.shape, lambda i: (0, 0)),
+            pl.BlockSpec(front_grads.shape, lambda i: (0, 0)),
+        ],
+        out_specs=pl.BlockSpec((cols, width), lambda i: (i, 0)),
+        out_shape=jax.ShapeDtypeStruct((model, width), jnp.float32),
+    )(inputs, prior_inputs, own_grads, front_grads)
 
 
 def body(
@@ -126,11 +154,12 @@
     douts = output_grad[0]
     tokens = queries.shape[0]
     kv_width = keys_own.shape[1]
-    width = HEADS // KV_HEADS * HEAD_DIM
-    block = min(512, tokens)
     prior_keys = shifted(keys_own, "seq", 1)
     prior_values = shifted(values_own, "seq", 1)
-    prior_inputs = shifted(inputs, "seq", 1)
+    inputs_after, prior_keys, prior_values = lax.optimization_barrier(
+        (inputs, prior_keys, prior_values)
+    )
+    prior_inputs = shifted(inputs_after, "seq", 1)
     ext_keys = jnp.concatenate([prior_keys, keys_own], axis=0)
     ext_values = jnp.concatenate([prior_values, values_own], axis=0)
     own_grads, front_grads, own32, front32 = attention_grads(
@@ -152,12 +181,7 @@
         value_grad, weight_value, contract_cols, preferred_element_type=jnp.float32
     )
     input_grad = summed.astype(jnp.bfloat16)[None]
-    by_tokens = (((0,), (0,)), ((), ()))
-    partial = lax.dot_general(inputs, own_grads, by_tokens, preferred_element_type=jnp.float32)
-    front_part = lax.dot_general(
-        prior_inputs[tokens - WINDOW :], front_grads, by_tokens, preferred_element_type=jnp.float32
-    )
-    partial = partial.at[:, q_span:].add(front_part)
+    partial = weight_partial(inputs, prior_inputs[tokens - WINDOW :], own_grads, front_grads)
     owned = lax.psum_scatter(partial, ("seq", "lat"), scatter_dimension=0, tiled=True)
     q_width = HEADS * HEAD_DIM
     query_weight_grad = owned[:, :q_width]

time: 195 us -> 162 us (0.83)
  local copies, waits for them, and re-layouts: 21.9 us -> 5.4 us
  waiting for transfers between devices: 104 us -> 89.8 us
  matrix products: 11 us -> 4.43 us
  Pallas kernels: 32.1 us -> 37.3 us
    reduce_scatter x0 -> x1, waiting for transfers between devices: none -> 58.2 us  [body(): lax.psum_scatter(partial, ('seq', 'lat'), scatter_dimension=0, tiled=True)]
    unnamed x2 -> x1, waiting for transfers between devices: 57.1 us -> 0.02 us
    ppermute x4, waiting for transfers between devices: 47.2 us -> 31.6 us  [shifted(): return lax.ppermute(block, axis, route)]
    unnamed x18 -> x12, local copies, waits for them, and re-layouts: 13.3 us -> 2.2 us
    pallas_call x0 -> x1, Pallas kernels: none -> 6.75 us  [weight_partial(): pl.pallas_call(wgrad_kernel, grid=(model // cols,), in_specs=[x_block, x_...]
    dot_general x2 -> x0, matrix products: 6.52 us -> none  [the longest x1 3.28 us: body(): lax.dot_general(prior_inputs[tokens - WINDOW:], front_grads, by_tokens, p...]
    concatenate x4 -> x0, local copies, waits for them, and re-layouts: 5.41 us -> none  [the longest x2 3.18 us: body(): ext_values = jnp.concatenate([prior_values, values_own], axis=0)]
    transpose x1 -> x0, other arithmetic: 2.95 us -> none  [attention_grads(): ext_keys = ext_keys.reshape(span, KV_HEADS, HEAD_DIM).transpose(1, 0, 2)]
  transfers between devices with their start and end apart: 5 -> 5, of which waited for: 4 -> 4; matrix products, arithmetic and copies ran while one was open for 11% -> 4% of each run, Pallas kernels for 17% -> 19%
where the time goes in v6:
time: 162 us
  waiting for transfers between devices  89.8 us (55%)
  Pallas kernels  37.3 us (23%)
  between operations  14.1 us (9%)
  starting transfers between devices  8.53 us (5%)
  local copies, waits for them, and re-layouts  5.4 us (3%)
  matrix products  4.43 us (3%)
  other arithmetic  2.08 us (1%)
    reduce_scatter x1, waiting for transfers between devices, body(): lax.psum_scatter(partial, ('seq', 'lat'), scatter_dimension=0, tiled=True)  58.2 us
    ppermute x4, waiting for transfers between devices, shifted(): return lax.ppermute(block, axis, route)  31.6 us
    pallas_call x1, Pallas kernels, attention_grads(): pl.pallas_call(attn_kernel, out_shape=[jax.ShapeDtypeStruct((rows, q_widt...  30.6 us
    ppermute x4, starting transfers between devices, shifted(): return lax.ppermute(block, axis, route)  8.49 us
    pallas_call x1, Pallas kernels, weight_partial(): pl.pallas_call(wgrad_kernel, grid=(model // cols,), in_specs=[x_block, x_...  6.75 us
  transfers between devices with their start and end apart: 5, of which 4 were waited for; matrix products, arithmetic and copies ran while one was open for 4% of the time, Pallas kernels for 19%

profile of v6, /device:TPU:0, one launch (start us, length us, event | category | flops | bytes accessed | tf_op | source)
XLA Modules:
  0.0 161.6 jit_solution(4362318573764750190)
XLA Ops:
  7.2 0.0 copy-start
  7.2 0.0 reduce-scatter.2.cloned.1.call-start
  7.2 3.1 %collective-permute-start = (bf16[512,256]{1,0:T(8,128)(2,1)}, bf16[512,256]{1,0:T(8,128)(2,1)S(1)}, u32[]{:S(2)}, u32[]{:S(2)}) collective-permute-start(bf16[512,256]{1,0:T(8,128)(2,1)} %bitcast.22), channel_id=1, source_target_pairs={{12,0},{0,4},{4,8},{8,12},{13,1},{1,5},{5,9},{9,13},{14,2},{2,6},{... | collective-permute-start | bytes 786440 | tf_op jit(solution)/shard_map/ppermute | solution.py:18
  10.3 1.6 collective-permute-start.1
  11.9 7.8 %collective-permute-done = bf16[512,256]{1,0:T(8,128)(2,1)S(1)} collective-permute-done((bf16[512,256]{1,0:T(8,128)(2,1)}, bf16[512,256]{1,0:T(8,128)(2,1)S(1)}, u32[]{:S(2)}, u32[]{:S(2)}) %collective-permute-start) | collective-permute-done | bytes 262176 | tf_op jit(solution)/shard_map/ppermute | solution.py:18
  19.7 4.8 %collective-permute-done.1 = bf16[512,256]{1,0:T(8,128)(2,1)S(1)} collective-permute-done((bf16[512,256]{1,0:T(8,128)(2,1)}, bf16[512,256]{1,0:T(8,128)(2,1)S(1)}, u32[]{:S(2)}, u32[]{:S(2)}) %collective-permute-start.1) | collective-permute-done | bytes 262176 | tf_op jit(solution)/shard_map/ppermute | solution.py:18
  24.5 0.0 collective-permute-start.3
  24.5 2.1 %pad_maximum_fusion = (bf16[1024,256]{1,0:T(8,128)(2,1)}, bf16[1024,256]{1,0:T(8,128)(2,1)}) fusion(bf16[512,256]{1,0:T(8,128)(2,1)} %bitcast.23, bf16[512,256]{1,0:T(8,128)(2,1)S(1)} %collective-permute-done, bf16[512,256]{1,0:T(8,128)(2,1)} %bitcast.25, bf16[512,256]{1,0:T(8,128)(2,1)S(1)} %collective-permute-done.1), kind=kLoop, calls=%fused_computation.8 | loop fusion | flops 2097152 | bytes 2097152 | tf_op jit(solution)/shard_map/concatenate | solution.py:163
  26.6 30.6 %shard_map.130 = (bf16[512,1536]{1,0:T(8,128)(2,1)}, bf16[512,512]{1,0:T(8,128)(2,1)}, f32[2,512,256]{2,1,0:T(8,128)}, f32[2,512,256]{2,1,0:T(8,128)}) custom-call(bf16[512,1024]{1,0:T(8,128)(2,1)} %bitcast.19, bf16[512,1024]{1,0:T(8,128)(2,1)} %bitcast.20, bf16[512,1024]{1,0:T(8,128)(2,1)} %bitcast.21, bf16[1024,256]{1,0:T(8,128)(2,1)} %get-tuple-element.60.k_ref, ...), custom_call_target="tpu_custom_call" | custom-call | tf_op jit(solution)/shard_map/pallas_call | solution.py:93
  57.1 0.0 collective-permute-done.3.xp_ref
  57.1 1.0 copy-done.1
  58.1 6.8 %shard_map.131 = f32[1024,1536]{1,0:T(8,128)} custom-call(bf16[512,1024]{1,0:T(8,128)(2,1)} %bitcast.18, bf16[512,1024]{1,0:T(8,128)(2,1)} %copy-done.1, bf16[512,1536]{1,0:T(8,128)(2,1)} %get-tuple-element.53.own_ref, bf16[512,512]{1,0:T(8,128)(2,1)} %get-tuple-element.57.front_ref), custom_call_target="tpu_custom_call" | custom-call | tf_op jit(solution)/shard_map/pallas_call | solution.py:124
  64.9 0.0 reduce-scatter.2.cloned.1.call-update
  64.9 1.2 copy-done.5
  66.1 3.8 %collective-permute-start.2 = (f32[2,512,256]{2,1,0:T(8,128)S(1)}, f32[2,512,256]{2,1,0:T(8,128)S(1)}, u32[]{:S(2)}, u32[]{:S(2)}) collective-permute-start(f32[2,512,256]{2,1,0:T(8,128)S(1)} %copy-done.5), channel_id=1, source_target_pairs={{4,0},{8,4},{12,8},{0,12},{5,1},{9,5},{13,9},{1,13},{6,2},{10,6},{... | collective-permute-start | bytes 3145736 | tf_op jit(solution)/shard_map/ppermute | solution.py:18
  69.9 2.5 %fusion.1 = f32[512,1024]{1,0:T(8,128)S(1)} fusion(bf16[1024,1024]{1,0:T(8,128)(2,1)S(1)} %copy-done, bf16[512,1536]{1,0:T(8,128)(2,1)} %get-tuple-element.53.own_ref), kind=kOutput, calls=%fused_computation.2 | convolution fusion | flops 1073741824 | bytes 5242880 | tf_op jit(solution)/shard_map/dot_general | solution.py:174
  72.4 0.0 copy-start.4
  72.4 19.0 %collective-permute-done.2 = f32[2,512,256]{2,1,0:T(8,128)S(1)} collective-permute-done((f32[2,512,256]{2,1,0:T(8,128)S(1)}, f32[2,512,256]{2,1,0:T(8,128)S(1)}, u32[]{:S(2)}, u32[]{:S(2)}) %collective-permute-start.2) | collective-permute-done | bytes 1048608 | tf_op jit(solution)/shard_map/ppermute | solution.py:18
  91.5 0.0 copy-done.3
  91.5 0.5 fusion.6
  92.0 1.5 fusion
  93.4 58.2 %reduce-scatter.2.cloned.1.call-done = f32[64,1536]{1,0:T(8,128)} async-done(((f32[1024,1536]{1,0:T(8,128)}), f32[64,1536]{1,0:T(8,128)}) %reduce-scatter.2.cloned.1.call-update) | async-done | bytes 393232 | tf_op jit(solution)/shard_map/reduce_scatter | solution.py:185
  151.6 1.5 fusion.10
  153.1 1.7 %slice.62 = f32[64,1024]{1,0:T(8,128)} slice(f32[64,1536]{1,0:T(8,128)} %reduce-scatter.2.cloned.1.call-done), slice={[0:64], [0:1024]} | slice | bytes 524288 | tf_op jit(solution)/shard_map/slice | solution.py:187
  (7 shorter events, 0.0 us)
Async XLA Ops:
  7.2 62.7 %copy-start = (bf16[1024,1024]{1,0:T(8,128)(2,1)S(1)}, bf16[1024,1024]{1,0:T(8,128)(2,1)}, u32[]{:S(2)}) copy-start(bf16[1024,1024]{1,0:T(8,128)(2,1)} %param.23) | copy-start | bytes 6291460
  7.2 144.4 %reduce-scatter.2.cloned.1.call-start = ((), (), s32[]{:S(2)}) async-start(), calls=%async_computation.1 | async-start | bytes 6684672 | tf_op jit(solution)/shard_map/reduce_scatter | solution.py:185
  7.2 12.5 %collective-permute-start = (bf16[512,256]{1,0:T(8,128)(2,1)}, bf16[512,256]{1,0:T(8,128)(2,1)S(1)}, u32[]{:S(2)}, u32[]{:S(2)}) collective-permute-start(bf16[512,256]{1,0:T(8,128)(2,1)} %bitcast.22), channel_id=1, source_target_pairs={{12,0},{0,4},{4,8},{8,12},{13,1},{1,5},{5,9},{9,13},{14,2},{2,6},{... | collective-permute-start | bytes 786440 | tf_op jit(solution)/shard_map/ppermute | solution.py:18
  10.3 14.2 %collective-permute-start.1 = (bf16[512,256]{1,0:T(8,128)(2,1)}, bf16[512,256]{1,0:T(8,128)(2,1)S(1)}, u32[]{:S(2)}, u32[]{:S(2)}) collective-permute-start(bf16[512,256]{1,0:T(8,128)(2,1)} %bitcast.24), channel_id=1, source_target_pairs={{12,0},{0,4},{4,8},{8,12},{13,1},{1,5},{5,9},{9,13},{14,2},{2,6},{... | collective-permute-start | bytes 786440 | tf_op jit(solution)/shard_map/ppermute | solution.py:18
  24.5 32.6 %collective-permute-start.3 = (bf16[512,1024]{1,0:T(8,128)(2,1)}, bf16[512,1024]{1,0:T(8,128)(2,1)S(1)}, u32[]{:S(2)}, u32[]{:S(2)}) collective-permute-start(bf16[512,1024]{1,0:T(8,128)(2,1)} %bitcast.17), channel_id=1, source_target_pairs={{12,0},{0,4},{4,8},{8,12},{13,1},{1,5},{5,9},{9,13},{14,2},{2,6},{... | collective-permute-start | bytes 3145736 | tf_op jit(solution)/shard_map/ppermute | solution.py:18
  57.1 1.0 copy-start.1
  64.9 1.2 copy-start.5
  66.1 25.4 %copy-start.2 = (f32[2,512,256]{2,1,0:T(8,128)S(1)}, f32[2,512,256]{2,1,0:T(8,128)}, u32[]{:S(2)}) copy-start(f32[2,512,256]{2,1,0:T(8,128)} %get-tuple-element.54) | copy-start | bytes 3145732
  66.1 25.4 %copy-start.3 = (bf16[1024,256]{1,0:T(8,128)(2,1)S(1)}, bf16[1024,256]{1,0:T(8,128)(2,1)}, u32[]{:S(2)}) copy-start(bf16[1024,256]{1,0:T(8,128)(2,1)} %param.24) | copy-start | bytes 1572868
  66.1 25.4 %collective-permute-start.2 = (f32[2,512,256]{2,1,0:T(8,128)S(1)}, f32[2,512,256]{2,1,0:T(8,128)S(1)}, u32[]{:S(2)}, u32[]{:S(2)}) collective-permute-start(f32[2,512,256]{2,1,0:T(8,128)S(1)} %copy-done.5), channel_id=1, source_target_pairs={{4,0},{8,4},{12,8},{0,12},{5,1},{9,5},{13,9},{1,13},{6,2},{10,6},{... | collective-permute-start | bytes 3145736 | tf_op jit(solution)/shard_map/ppermute | solution.py:18
  72.4 19.5 %copy-start.4 = (bf16[1024,256]{1,0:T(8,128)(2,1)S(1)}, bf16[1024,256]{1,0:T(8,128)(2,1)}, u32[]{:S(2)}) copy-start(bf16[1024,256]{1,0:T(8,128)(2,1)} %param.25) | copy-start | bytes 1572868
Sparse Core Ops, SparseCore 0:
  65.0 86.5 reduce-scatter.1

commit v7 on v6

--- a/solution.py
+++ b/solution.py
@@ -26,8 +26,9 @@
     span = ROW_BLOCK + WINDOW
     q_width = HEADS * HEAD_DIM
     kv_width = KV_HEADS * HEAD_DIM
-    row = lax.broadcasted_iota(jnp.int32, (ROW_BLOCK, span), 0)
-    col = lax.broadcasted_iota(jnp.int32, (ROW_BLOCK, span), 1)
+    stacked = ratio * ROW_BLOCK
+    row = lax.broadcasted_iota(jnp.int32, (stacked, span), 0) % ROW_BLOCK
+    col = lax.broadcasted_iota(jnp.int32, (stacked, span), 1)
     linked = (col > row) & (col <= row + WINDOW)
     by_rows = (((0,), (0,)), ((), ()))
     by_cols = (((1,), (1,)), ((), ()))
@@ -35,41 +36,30 @@
         kv_cols = slice(c * HEAD_DIM, (c + 1) * HEAD_DIM)
         dk_scr[...] = jnp.zeros(dk_scr.shape, jnp.float32)
         dv_scr[...] = jnp.zeros(dv_scr.shape, jnp.float32)
-
-        def row_step(a, carry):
+        for a in range(rows // ROW_BLOCK):
             top = a * ROW_BLOCK
             keys = k_ref[top : top + span, kv_cols]
             values = v_ref[top : top + span, kv_cols]
-            dk = jnp.zeros((HEAD_DIM, span), jnp.float32)
-            dv = jnp.zeros((HEAD_DIM, span), jnp.float32)
-            for r in range(ratio):
-                sl = slice((c * ratio + r) * HEAD_DIM, (c * ratio + r + 1) * HEAD_DIM)
-                q = q_ref[pl.ds(top, ROW_BLOCK), sl]
-                q_scaled = q * jnp.asarray(scale, q.dtype)
-                dout = do_ref[pl.ds(top, ROW_BLOCK), sl]
-                out = o_ref[pl.ds(top, ROW_BLOCK), sl]
-                s = lax.dot_general(q_scaled, keys, by_cols, preferred_element_type=jnp.float32)
-                s = jnp.where(linked, s, -jnp.inf)
-                peak = jnp.max(s, axis=1, keepdims=True)
-                raised = jnp.exp(s - peak)
-                probs = raised * (1.0 / jnp.sum(raised, axis=1, keepdims=True))
-                dp = lax.dot_general(dout, values, by_cols, preferred_element_type=jnp.float32)
-                delta = jnp.sum(
-                    dout.astype(jnp.float32) * out.astype(jnp.float32), axis=1, keepdims=True
-                )
-                ds = (probs * (dp - delta)).astype(jnp.bfloat16)
-                dq = jnp.dot(ds, keys, preferred_element_type=jnp.float32) * scale
-                own_ref[pl.ds(top, ROW_BLOCK), sl] = dq.astype(own_ref.dtype)
-                dk = dk + lax.dot_general(q, ds, by_rows, preferred_element_type=jnp.float32)
-                dv = dv + lax.dot_general(
-                    dout, probs.astype(jnp.bfloat16), by_rows, preferred_element_type=jnp.float32
-                )
-            dk_scr[:, top : top + span] += dk
-            dv_scr[:, top : top + span] += dv
-            return carry
-
-        for a in range(rows // ROW_BLOCK):
-            row_step(a, 0)
+            heads = [slice((c * ratio + r) * HEAD_DIM, (c * ratio + r + 1) * HEAD_DIM) for r in range(ratio)]
+            q = jnp.concatenate([q_ref[top : top + ROW_BLOCK, sl] for sl in heads], axis=0)
+            dout = jnp.concatenate([do_ref[top : top + ROW_BLOCK, sl] for sl in heads], axis=0)
+            out = jnp.concatenate([o_ref[top : top + ROW_BLOCK, sl] for sl in heads], axis=0)
+            q_scaled = q * jnp.asarray(scale, q.dtype)
+            s = lax.dot_general(q_scaled, keys, by_cols, preferred_element_type=jnp.float32)
+            s = jnp.where(linked, s, -jnp.inf)
+            peak = jnp.max(s, axis=1, keepdims=True)
+            raised = jnp.exp(s - peak)
+            probs = raised * (1.0 / jnp.sum(raised, axis=1, keepdims=True))
+            dp = lax.dot_general(dout, values, by_cols, preferred_element_type=jnp.float32)
+            delta = jnp.sum(dout.astype(jnp.float32) * out.astype(jnp.float32), axis=1, keepdims=True)
+            ds = (probs * (dp - delta)).astype(jnp.bfloat16)
+            dq = jnp.dot(ds, keys, preferred_element_type=jnp.float32) * scale
+            for r, sl in enumerate(heads):
+                own_ref[top : top + ROW_BLOCK, sl] = dq[r * ROW_BLOCK : (r + 1) * ROW_BLOCK].astype(own_ref.dtype)
+            dk_scr[:, top : top + span] += lax.dot_general(q, ds, by_rows, preferred_element_type=jnp.float32)
+            dv_scr[:, top : top + span] += lax.dot_general(
+                dout, probs.astype(jnp.bfloat16), by_rows, preferred_element_type=jnp.float32
+            )
         dk_all = dk_scr[...].T * scale
         dv_all = dv_scr[...].T
         k_cols = slice(q_width + c * HEAD_DIM, q_width + (c + 1) * HEAD_DIM)

time: 162 us -> 155 us (0.957)
  Pallas kernels: 37.3 us -> 30.5 us
    pallas_call x1, Pallas kernels: 30.6 us -> 23.8 us  [attention_grads(): pl.pallas_call(attn_kernel, out_shape=[jax.ShapeDtypeStruct((rows, q_widt...]
  transfers between devices with their start and end apart: 5 -> 5, of which waited for: 4 -> 5; matrix products, arithmetic and copies ran while one was open for 4% -> 4% of each run, Pallas kernels for 19% -> 15%
where the time goes in v7:
time: 155 us
  waiting for transfers between devices  90.3 us (58%)
  Pallas kernels  30.5 us (20%)
  between operations  14.1 us (9%)
  starting transfers between devices  8.07 us (5%)
  local copies, waits for them, and re-layouts  5.4 us (3%)
  matrix products  4.44 us (3%)
  other arithmetic  2.08 us (1%)
    reduce_scatter x1, waiting for transfers between devices, body(): lax.psum_scatter(partial, ('seq', 'lat'), scatter_dimension=0, tiled=True)  58.2 us
    ppermute x4, waiting for transfers between devices, shifted(): return lax.ppermute(block, axis, route)  32.1 us
    pallas_call x1, Pallas kernels, attention_grads(): pl.pallas_call(attn_kernel, out_shape=[jax.ShapeDtypeStruct((rows, q_widt...  23.8 us
    ppermute x4, starting transfers between devices, shifted(): return lax.ppermute(block, axis, route)  8.04 us
    pallas_call x1, Pallas kernels, weight_partial(): pl.pallas_call(wgrad_kernel, grid=(model // cols,), in_specs=[x_block, x_...  6.75 us
  transfers between devices with their start and end apart: 5, of which 5 were waited for; matrix products, arithmetic and copies ran while one was open for 4% of the time, Pallas kernels for 15%

profile of v7, /device:TPU:0, one launch (start us, length us, event | category | flops | bytes accessed | tf_op | source)
XLA Modules:
  0.0 154.8 jit_solution(3188590231613821504)
XLA Ops:
  7.2 0.0 copy-start
  7.2 0.0 reduce-scatter.2.cloned.1.call-start
  7.2 3.1 %collective-permute-start = (bf16[512,256]{1,0:T(8,128)(2,1)}, bf16[512,256]{1,0:T(8,128)(2,1)S(1)}, u32[]{:S(2)}, u32[]{:S(2)}) collective-permute-start(bf16[512,256]{1,0:T(8,128)(2,1)} %bitcast.22), channel_id=1, source_target_pairs={{12,0},{0,4},{4,8},{8,12},{13,1},{1,5},{5,9},{9,13},{14,2},{2,6},{... | collective-permute-start | bytes 786440 | tf_op jit(solution)/shard_map/ppermute | solution.py:18
  10.3 1.6 %collective-permute-start.1 = (bf16[512,256]{1,0:T(8,128)(2,1)}, bf16[512,256]{1,0:T(8,128)(2,1)S(1)}, u32[]{:S(2)}, u32[]{:S(2)}) collective-permute-start(bf16[512,256]{1,0:T(8,128)(2,1)} %bitcast.24), channel_id=1, source_target_pairs={{12,0},{0,4},{4,8},{8,12},{13,1},{1,5},{5,9},{9,13},{14,2},{2,6},{... | collective-permute-start | bytes 786440 | tf_op jit(solution)/shard_map/ppermute | solution.py:18
  11.9 7.8 %collective-permute-done = bf16[512,256]{1,0:T(8,128)(2,1)S(1)} collective-permute-done((bf16[512,256]{1,0:T(8,128)(2,1)}, bf16[512,256]{1,0:T(8,128)(2,1)S(1)}, u32[]{:S(2)}, u32[]{:S(2)}) %collective-permute-start) | collective-permute-done | bytes 262176 | tf_op jit(solution)/shard_map/ppermute | solution.py:18
  19.7 4.8 %collective-permute-done.1 = bf16[512,256]{1,0:T(8,128)(2,1)S(1)} collective-permute-done((bf16[512,256]{1,0:T(8,128)(2,1)}, bf16[512,256]{1,0:T(8,128)(2,1)S(1)}, u32[]{:S(2)}, u32[]{:S(2)}) %collective-permute-start.1) | collective-permute-done | bytes 262176 | tf_op jit(solution)/shard_map/ppermute | solution.py:18
  24.5 0.0 collective-permute-start.3
  24.5 2.1 %pad_maximum_fusion = (bf16[1024,256]{1,0:T(8,128)(2,1)}, bf16[1024,256]{1,0:T(8,128)(2,1)}) fusion(bf16[512,256]{1,0:T(8,128)(2,1)} %bitcast.23, bf16[512,256]{1,0:T(8,128)(2,1)S(1)} %collective-permute-done, bf16[512,256]{1,0:T(8,128)(2,1)} %bitcast.25, bf16[512,256]{1,0:T(8,128)(2,1)S(1)} %collective-permute-done.1), kind=kLoop, calls=%fused_computation.8 | loop fusion | flops 2097152 | bytes 2097152 | tf_op jit(solution)/shard_map/concatenate | solution.py:153
  26.6 23.8 %shard_map.130 = (bf16[512,1536]{1,0:T(8,128)(2,1)}, bf16[512,512]{1,0:T(8,128)(2,1)}, f32[2,512,256]{2,1,0:T(8,128)}, f32[2,512,256]{2,1,0:T(8,128)}) custom-call(bf16[512,1024]{1,0:T(8,128)(2,1)} %bitcast.19, bf16[512,1024]{1,0:T(8,128)(2,1)} %bitcast.20, bf16[512,1024]{1,0:T(8,128)(2,1)} %bitcast.21, bf16[1024,256]{1,0:T(8,128)(2,1)} %get-tuple-element.60.k_ref, ...), custom_call_target="tpu_custom_call" | custom-call | tf_op jit(solution)/shard_map/pallas_call | solution.py:83
  50.3 0.5 collective-permute-done.3.xp_ref
  50.8 1.0 copy-done.1
  51.8 6.8 %shard_map.131 = f32[1024,1536]{1,0:T(8,128)} custom-call(bf16[512,1024]{1,0:T(8,128)(2,1)} %bitcast.18, bf16[512,1024]{1,0:T(8,128)(2,1)} %copy-done.1, bf16[512,1536]{1,0:T(8,128)(2,1)} %get-tuple-element.53.own_ref, bf16[512,512]{1,0:T(8,128)(2,1)} %get-tuple-element.57.front_ref), custom_call_target="tpu_custom_call" | custom-call | tf_op jit(solution)/shard_map/pallas_call | solution.py:114
  58.6 0.0 reduce-scatter.2.cloned.1.call-update
  58.6 1.2 copy-done.5
  59.8 3.4 %collective-permute-start.2 = (f32[2,512,256]{2,1,0:T(8,128)S(1)}, f32[2,512,256]{2,1,0:T(8,128)S(1)}, u32[]{:S(2)}, u32[]{:S(2)}) collective-permute-start(f32[2,512,256]{2,1,0:T(8,128)S(1)} %copy-done.5), channel_id=1, source_target_pairs={{4,0},{8,4},{12,8},{0,12},{5,1},{9,5},{13,9},{1,13},{6,2},{10,6},{... | collective-permute-start | bytes 3145736 | tf_op jit(solution)/shard_map/ppermute | solution.py:18
  63.1 0.0 copy-done
  63.1 2.5 %fusion.1 = f32[512,1024]{1,0:T(8,128)S(1)} fusion(bf16[1024,1024]{1,0:T(8,128)(2,1)S(1)} %copy-done, bf16[512,1536]{1,0:T(8,128)(2,1)} %get-tuple-element.53.own_ref), kind=kOutput, calls=%fused_computation.2 | convolution fusion | flops 1073741824 | bytes 5242880 | tf_op jit(solution)/shard_map/dot_general | solution.py:164
  65.7 0.0 copy-start.4
  65.7 19.0 %collective-permute-done.2 = f32[2,512,256]{2,1,0:T(8,128)S(1)} collective-permute-done((f32[2,512,256]{2,1,0:T(8,128)S(1)}, f32[2,512,256]{2,1,0:T(8,128)S(1)}, u32[]{:S(2)}, u32[]{:S(2)}) %collective-permute-start.2) | collective-permute-done | bytes 1048608 | tf_op jit(solution)/shard_map/ppermute | solution.py:18
  84.7 0.5 fusion.6
  85.2 1.5 fusion
  86.6 58.2 %reduce-scatter.2.cloned.1.call-done = f32[64,1536]{1,0:T(8,128)} async-done(((f32[1024,1536]{1,0:T(8,128)}), f32[64,1536]{1,0:T(8,128)}) %reduce-scatter.2.cloned.1.call-update) | async-done | bytes 393232 | tf_op jit(solution)/shard_map/reduce_scatter | solution.py:175
  144.8 1.5 fusion.10
  146.3 1.7 %slice.62 = f32[64,1024]{1,0:T(8,128)} slice(f32[64,1536]{1,0:T(8,128)} %reduce-scatter.2.cloned.1.call-done), slice={[0:64], [0:1024]} | slice | bytes 524288 | tf_op jit(solution)/shard_map/slice | solution.py:177
  (7 shorter events, 0.0 us)
Async XLA Ops:
  7.2 56.0 %copy-start = (bf16[1024,1024]{1,0:T(8,128)(2,1)S(1)}, bf16[1024,1024]{1,0:T(8,128)(2,1)}, u32[]{:S(2)}) copy-start(bf16[1024,1024]{1,0:T(8,128)(2,1)} %param.23) | copy-start | bytes 6291460
  7.2 137.6 %reduce-scatter.2.cloned.1.call-start = ((), (), s32[]{:S(2)}) async-start(), calls=%async_computation.1 | async-start | bytes 6684672 | tf_op jit(solution)/shard_map/reduce_scatter | solution.py:175
  7.2 12.5 %collective-permute-start = (bf16[512,256]{1,0:T(8,128)(2,1)}, bf16[512,256]{1,0:T(8,128)(2,1)S(1)}, u32[]{:S(2)}, u32[]{:S(2)}) collective-permute-start(bf16[512,256]{1,0:T(8,128)(2,1)} %bitcast.22), channel_id=1, source_target_pairs={{12,0},{0,4},{4,8},{8,12},{13,1},{1,5},{5,9},{9,13},{14,2},{2,6},{... | collective-permute-start | bytes 786440 | tf_op jit(solution)/shard_map/ppermute | solution.py:18
  10.3 14.2 %collective-permute-start.1 = (bf16[512,256]{1,0:T(8,128)(2,1)}, bf16[512,256]{1,0:T(8,128)(2,1)S(1)}, u32[]{:S(2)}, u32[]{:S(2)}) collective-permute-start(bf16[512,256]{1,0:T(8,128)(2,1)} %bitcast.24), channel_id=1, source_target_pairs={{12,0},{0,4},{4,8},{8,12},{13,1},{1,5},{5,9},{9,13},{14,2},{2,6},{... | collective-permute-start | bytes 786440 | tf_op jit(solution)/shard_map/ppermute | solution.py:18
  24.5 26.3 %collective-permute-start.3 = (bf16[512,1024]{1,0:T(8,128)(2,1)}, bf16[512,1024]{1,0:T(8,128)(2,1)S(1)}, u32[]{:S(2)}, u32[]{:S(2)}) collective-permute-start(bf16[512,1024]{1,0:T(8,128)(2,1)} %bitcast.17), channel_id=1, source_target_pairs={{12,0},{0,4},{4,8},{8,12},{13,1},{1,5},{5,9},{9,13},{14,2},{2,6},{... | collective-permute-start | bytes 3145736 | tf_op jit(solution)/shard_map/ppermute | solution.py:18
  50.8 1.0 copy-start.1
  58.6 1.2 copy-start.5
  59.8 24.9 %copy-start.2 = (f32[2,512,256]{2,1,0:T(8,128)S(1)}, f32[2,512,256]{2,1,0:T(8,128)}, u32[]{:S(2)}) copy-start(f32[2,512,256]{2,1,0:T(8,128)} %get-tuple-element.54) | copy-start | bytes 3145732
  59.8 24.9 %copy-start.3 = (bf16[1024,256]{1,0:T(8,128)(2,1)S(1)}, bf16[1024,256]{1,0:T(8,128)(2,1)}, u32[]{:S(2)}) copy-start(bf16[1024,256]{1,0:T(8,128)(2,1)} %param.24) | copy-start | bytes 1572868
  59.8 24.9 %collective-permute-start.2 = (f32[2,512,256]{2,1,0:T(8,128)S(1)}, f32[2,512,256]{2,1,0:T(8,128)S(1)}, u32[]{:S(2)}, u32[]{:S(2)}) collective-permute-start(f32[2,512,256]{2,1,0:T(8,128)S(1)} %copy-done.5), channel_id=1, source_target_pairs={{4,0},{8,4},{12,8},{0,12},{5,1},{9,5},{13,9},{1,13},{6,2},{10,6},{... | collective-permute-start | bytes 3145736 | tf_op jit(solution)/shard_map/ppermute | solution.py:18
  65.7 19.5 %copy-start.4 = (bf16[1024,256]{1,0:T(8,128)(2,1)S(1)}, bf16[1024,256]{1,0:T(8,128)(2,1)}, u32[]{:S(2)}) copy-start(bf16[1024,256]{1,0:T(8,128)(2,1)} %param.25) | copy-start | bytes 1572868
Sparse Core Ops, SparseCore 0:
  58.7 86.0 reduce-scatter.1

commit v8 on v7

--- a/solution.py
+++ b/solution.py
@@ -96,21 +96,18 @@
 
 
 def wgrad_kernel(x_ref, xp_ref, own_ref, front_ref, out_ref):
-    by_rows = (((0,), (0,)), ((), ()))
     q_width = out_ref.shape[1] - front_ref.shape[1]
-    own_part = lax.dot_general(x_ref[...], own_ref[...], by_rows, preferred_element_type=jnp.float32)
-    front_part = lax.dot_general(
-        xp_ref[...], front_ref[...], by_rows, preferred_element_type=jnp.float32
-    )
+    own_part = jnp.dot(x_ref[...], own_ref[...], preferred_element_type=jnp.float32)
+    front_part = jnp.dot(xp_ref[...], front_ref[...], preferred_element_type=jnp.float32)
     out_ref[:, :q_width] = own_part[:, :q_width]
     out_ref[:, q_width:] = own_part[:, q_width:] + front_part
 
 
-def weight_partial(inputs, prior_inputs, own_grads, front_grads):
-    tokens, model = inputs.shape
+def weight_partial(inputs_t, prior_inputs_t, own_grads, front_grads):
+    model, tokens = inputs_t.shape
     width = own_grads.shape[1]
     cols = 256 if model % 256 == 0 else model
-    x_block = pl.BlockSpec((tokens, cols), lambda i: (0, i))
+    x_block = pl.BlockSpec((cols, tokens), lambda i: (i, 0))
     return pl.pallas_call(
         wgrad_kernel,
         grid=(model // cols,),
@@ -122,7 +119,7 @@
         ],
         out_specs=pl.BlockSpec((cols, width), lambda i: (i, 0)),
         out_shape=jax.ShapeDtypeStruct((model, width), jnp.float32),
-    )(inputs, prior_inputs, own_grads, front_grads)
+    )(inputs_t, prior_inputs_t, own_grads, front_grads)
 
 
 def body(
@@ -146,10 +143,11 @@
     kv_width = keys_own.shape[1]
     prior_keys = shifted(keys_own, "seq", 1)
     prior_values = shifted(values_own, "seq", 1)
+    inputs_t = inputs.T
     inputs_after, prior_keys, prior_values = lax.optimization_barrier(
-        (inputs, prior_keys, prior_values)
-    )
-    prior_inputs = shifted(inputs_after, "seq", 1)
+        (inputs_t, prior_keys, prior_values)
+    )
+    prior_inputs_t = shifted(inputs_after, "seq", 1)
     ext_keys = jnp.concatenate([prior_keys, keys_own], axis=0)
     ext_values = jnp.concatenate([prior_values, values_own], axis=0)
     own_grads, front_grads, own32, front32 = attention_grads(
@@ -171,7 +169,7 @@
         value_grad, weight_value, contract_cols, preferred_element_type=jnp.float32
     )
     input_grad = summed.astype(jnp.bfloat16)[None]
-    partial = weight_partial(inputs, prior_inputs[tokens - WINDOW :], own_grads, front_grads)
+    partial = weight_partial(inputs_t, prior_inputs_t[:, tokens - WINDOW :], own_grads, front_grads)
     owned = lax.psum_scatter(partial, ("seq", "lat"), scatter_dimension=0, tiled=True)
     q_width = HEADS * HEAD_DIM
     query_weight_grad = owned[:, :q_width]

time: 155 us -> 154 us (level)
  transfers between devices with their start and end apart: 5 -> 5, of which waited for: 5 -> 5; matrix products, arithmetic and copies ran while one was open for 4% -> 5% of each run, Pallas kernels for 15% -> 15%
where the time goes in v8:
time: 154 us
  waiting for transfers between devices  88.8 us (58%)
  Pallas kernels  30.3 us (20%)
  between operations  14.1 us (9%)
  starting transfers between devices  8.2 us (5%)
  local copies, waits for them, and re-layouts  5.92 us (4%)
  matrix products  4.44 us (3%)
  other arithmetic  2.16 us (1%)
    reduce_scatter x1, waiting for transfers between devices, body(): lax.psum_scatter(partial, ('seq', 'lat'), scatter_dimension=0, tiled=True)  58.2 us
    ppermute x4, waiting for transfers between devices, shifted(): return lax.ppermute(block, axis, route)  30.6 us
    pallas_call x1, Pallas kernels, attention_grads(): pl.pallas_call(attn_kernel, out_shape=[jax.ShapeDtypeStruct((rows, q_widt...  23.7 us
    ppermute x4, starting transfers between devices, shifted(): return lax.ppermute(block, axis, route)  8.16 us
    pallas_call x1, Pallas kernels, weight_partial(): pl.pallas_call(wgrad_kernel, grid=(model // cols,), in_specs=[x_block, x_...  6.61 us
  transfers between devices with their start and end apart: 5, of which 5 were waited for; matrix products, arithmetic and copies ran while one was open for 5% of the time, Pallas kernels for 15%

profile of v8, /device:TPU:0, one launch (start us, length us, event | category | flops | bytes accessed | tf_op | source)
XLA Modules:
  0.0 153.9 jit_solution(10216664947906844514)
XLA Ops:
  7.2 0.0 copy-start
  7.2 0.0 copy-start.5
  7.2 0.0 reduce-scatter.2.cloned.1.call-start
  7.2 3.1 %collective-permute-start = (bf16[512,256]{1,0:T(8,128)(2,1)}, bf16[512,256]{1,0:T(8,128)(2,1)}, u32[]{:S(2)}, u32[]{:S(2)}) collective-permute-start(bf16[512,256]{1,0:T(8,128)(2,1)} %bitcast.24), channel_id=1, source_target_pairs={{12,0},{0,4},{4,8},{8,12},{13,1},{1,5},{5,9},{9,13},{14,2},{2,6},{... | collective-permute-start | bytes 786440 | tf_op jit(solution)/shard_map/ppermute | solution.py:18
  10.3 1.6 %collective-permute-start.1 = (bf16[512,256]{1,0:T(8,128)(2,1)}, bf16[512,256]{1,0:T(8,128)(2,1)}, u32[]{:S(2)}, u32[]{:S(2)}) collective-permute-start(bf16[512,256]{1,0:T(8,128)(2,1)} %bitcast.26), channel_id=1, source_target_pairs={{12,0},{0,4},{4,8},{8,12},{13,1},{1,5},{5,9},{9,13},{14,2},{2,6},{... | collective-permute-start | bytes 786440 | tf_op jit(solution)/shard_map/ppermute | solution.py:18
  11.9 1.5 copy.13
  13.4 6.4 %collective-permute-done = bf16[512,256]{1,0:T(8,128)(2,1)} collective-permute-done((bf16[512,256]{1,0:T(8,128)(2,1)}, bf16[512,256]{1,0:T(8,128)(2,1)}, u32[]{:S(2)}, u32[]{:S(2)}) %collective-permute-start) | collective-permute-done | bytes 262176 | tf_op jit(solution)/shard_map/ppermute | solution.py:18
  19.8 4.8 %collective-permute-done.1 = bf16[512,256]{1,0:T(8,128)(2,1)} collective-permute-done((bf16[512,256]{1,0:T(8,128)(2,1)}, bf16[512,256]{1,0:T(8,128)(2,1)}, u32[]{:S(2)}, u32[]{:S(2)}) %collective-permute-start.1) | collective-permute-done | bytes 262176 | tf_op jit(solution)/shard_map/ppermute | solution.py:18
  24.6 0.0 collective-permute-start.3
  24.6 2.2 %pad_maximum_fusion = (bf16[1024,256]{1,0:T(8,128)(2,1)}, bf16[1024,256]{1,0:T(8,128)(2,1)}) fusion(bf16[512,256]{1,0:T(8,128)(2,1)S(1)} %bitcast.25, bf16[512,256]{1,0:T(8,128)(2,1)} %collective-permute-done, bf16[512,256]{1,0:T(8,128)(2,1)} %bitcast.27, bf16[512,256]{1,0:T(8,128)(2,1)} %collective-permute-done.1), kind=kLoop, calls=%fused_computation.8 | loop fusion | flops 2097152 | bytes 2097152 | tf_op jit(solution)/shard_map/concatenate | solution.py:151
  26.8 23.7 %shard_map.130 = (bf16[512,1536]{1,0:T(8,128)(2,1)}, bf16[512,512]{1,0:T(8,128)(2,1)}, f32[2,512,256]{2,1,0:T(8,128)}, f32[2,512,256]{2,1,0:T(8,128)}) custom-call(bf16[512,1024]{1,0:T(8,128)(2,1)} %bitcast.21, bf16[512,1024]{1,0:T(8,128)(2,1)} %bitcast.22, bf16[512,1024]{1,0:T(8,128)(2,1)} %bitcast.23, bf16[1024,256]{1,0:T(8,128)(2,1)} %get-tuple-element.60.k_ref, ...), custom_call_target="tpu_custom_call" | custom-call | tf_op jit(solution)/shard_map/pallas_call | solution.py:83
  50.5 0.4 collective-permute-done.3.xp_ref
  50.8 6.6 %shard_map.131 = f32[1024,1536]{1,0:T(8,128)} custom-call(bf16[1024,512]{1,0:T(8,128)(2,1)} %bitcast.20, bf16[1024,512]{1,0:T(8,128)(2,1)} %collective-permute-done.3.xp_ref, bf16[512,1536]{1,0:T(8,128)(2,1)} %get-tuple-element.53.own_ref, bf16[512,512]{1,0:T(8,128)(2,1)} %get-tuple-element.57.front_ref), custom_call_target="tpu_custom_call" | custom-call | tf_op jit(solution)/shard_map/pallas_call | solution.py:111
  57.4 0.0 reduce-scatter.2.cloned.1.call-update
  57.5 1.2 copy-done.6
  58.7 3.5 %collective-permute-start.2 = (f32[2,512,256]{2,1,0:T(8,128)S(1)}, f32[2,512,256]{2,1,0:T(8,128)S(1)}, u32[]{:S(2)}, u32[]{:S(2)}) collective-permute-start(f32[2,512,256]{2,1,0:T(8,128)S(1)} %copy-done.6), channel_id=1, source_target_pairs={{4,0},{8,4},{12,8},{0,12},{5,1},{9,5},{13,9},{1,13},{6,2},{10,6},{... | collective-permute-start | bytes 3145736 | tf_op jit(solution)/shard_map/ppermute | solution.py:18
  62.2 2.5 %fusion.1 = f32[512,1024]{1,0:T(8,128)S(1)} fusion(bf16[1024,1024]{1,0:T(8,128)(2,1)S(1)} %copy-done, bf16[512,1536]{1,0:T(8,128)(2,1)} %get-tuple-element.53.own_ref), kind=kOutput, calls=%fused_computation.2 | convolution fusion | flops 1073741824 | bytes 5242880 | tf_op jit(solution)/shard_map/dot_general | solution.py:162
  64.7 0.0 copy-start.4
  64.7 19.0 %collective-permute-done.2 = f32[2,512,256]{2,1,0:T(8,128)S(1)} collective-permute-done((f32[2,512,256]{2,1,0:T(8,128)S(1)}, f32[2,512,256]{2,1,0:T(8,128)S(1)}, u32[]{:S(2)}, u32[]{:S(2)}) %collective-permute-start.2) | collective-permute-done | bytes 1048608 | tf_op jit(solution)/shard_map/ppermute | solution.py:18
  83.7 0.5 fusion.6
  84.2 1.5 fusion
  85.7 58.2 %reduce-scatter.2.cloned.1.call-done = f32[64,1536]{1,0:T(8,128)} async-done(((f32[1024,1536]{1,0:T(8,128)}), f32[64,1536]{1,0:T(8,128)}) %reduce-scatter.2.cloned.1.call-update) | async-done | bytes 393232 | tf_op jit(solution)/shard_map/reduce_scatter | solution.py:173
  143.8 1.5 fusion.10
  145.4 1.7 %slice.62 = f32[64,1024]{1,0:T(8,128)} slice(f32[64,1536]{1,0:T(8,128)} %reduce-scatter.2.cloned.1.call-done), slice={[0:64], [0:1024]} | slice | bytes 524288 | tf_op jit(solution)/shard_map/slice | solution.py:175
  (10 shorter events, 0.0 us)
Async XLA Ops:
  7.2 55.0 %copy-start = (bf16[1024,1024]{1,0:T(8,128)(2,1)S(1)}, bf16[1024,1024]{1,0:T(8,128)(2,1)}, u32[]{:S(2)}) copy-start(bf16[1024,1024]{1,0:T(8,128)(2,1)} %param.23) | copy-start | bytes 6291460
  7.2 17.4 %copy-start.5 = (bf16[1,512,256]{2,1,0:T(8,128)(2,1)S(1)}, bf16[1,512,256]{2,1,0:T(8,128)(2,1)}, u32[]{:S(2)}) copy-start(bf16[1,512,256]{2,1,0:T(8,128)(2,1)} %param.19) | copy-start | bytes 786436
  7.2 136.6 %reduce-scatter.2.cloned.1.call-start = ((), (), s32[]{:S(2)}) async-start(), calls=%async_computation.1 | async-start | bytes 6684672 | tf_op jit(solution)/shard_map/reduce_scatter | solution.py:173
  7.2 12.6 %collective-permute-start = (bf16[512,256]{1,0:T(8,128)(2,1)}, bf16[512,256]{1,0:T(8,128)(2,1)}, u32[]{:S(2)}, u32[]{:S(2)}) collective-permute-start(bf16[512,256]{1,0:T(8,128)(2,1)} %bitcast.24), channel_id=1, source_target_pairs={{12,0},{0,4},{4,8},{8,12},{13,1},{1,5},{5,9},{9,13},{14,2},{2,6},{... | collective-permute-start | bytes 786440 | tf_op jit(solution)/shard_map/ppermute | solution.py:18
  10.3 14.3 %collective-permute-start.1 = (bf16[512,256]{1,0:T(8,128)(2,1)}, bf16[512,256]{1,0:T(8,128)(2,1)}, u32[]{:S(2)}, u32[]{:S(2)}) collective-permute-start(bf16[512,256]{1,0:T(8,128)(2,1)} %bitcast.26), channel_id=1, source_target_pairs={{12,0},{0,4},{4,8},{8,12},{13,1},{1,5},{5,9},{9,13},{14,2},{2,6},{... | collective-permute-start | bytes 786440 | tf_op jit(solution)/shard_map/ppermute | solution.py:18
  13.4 37.0 %copy-start.1 = (bf16[1,512,1024]{1,2,0:T(8,128)(2,1)}, bf16[1,512,1024]{1,2,0:T(8,128)(2,1)S(1)}, u32[]{:S(2)}) copy-start(bf16[1,512,1024]{1,2,0:T(8,128)(2,1)S(1)} %copy.13) | copy-start | bytes 3145732
  24.6 26.2 %collective-permute-start.3 = (bf16[1024,512]{1,0:T(8,128)(2,1)S(1)}, bf16[1024,512]{1,0:T(8,128)(2,1)}, u32[]{:S(2)}, u32[]{:S(2)}) collective-permute-start(bf16[1024,512]{1,0:T(8,128)(2,1)S(1)} %bitcast.19), channel_id=1, source_target_pairs={{12,0},{0,4},{4,8},{8,12},{13,1},{1,5},{5,9},{9,13},{14,2},{2,6},{... | collective-permute-start | bytes 3145736 | tf_op jit(solution)/shard_map/ppermute | solution.py:18
  57.4 1.2 copy-start.6
  58.7 25.0 %copy-start.2 = (f32[2,512,256]{2,1,0:T(8,128)S(1)}, f32[2,512,256]{2,1,0:T(8,128)}, u32[]{:S(2)}) copy-start(f32[2,512,256]{2,1,0:T(8,128)} %get-tuple-element.54) | copy-start | bytes 3145732
  58.7 25.0 %copy-start.3 = (bf16[1024,256]{1,0:T(8,128)(2,1)S(1)}, bf16[1024,256]{1,0:T(8,128)(2,1)}, u32[]{:S(2)}) copy-start(bf16[1024,256]{1,0:T(8,128)(2,1)} %param.24) | copy-start | bytes 1572868
  58.7 25.0 %collective-permute-start.2 = (f32[2,512,256]{2,1,0:T(8,128)S(1)}, f32[2,512,256]{2,1,0:T(8,128)S(1)}, u32[]{:S(2)}, u32[]{:S(2)}) collective-permute-start(f32[2,512,256]{2,1,0:T(8,128)S(1)} %copy-done.6), channel_id=1, source_target_pairs={{4,0},{8,4},{12,8},{0,12},{5,1},{9,5},{13,9},{1,13},{6,2},{10,6},{... | collective-permute-start | bytes 3145736 | tf_op jit(solution)/shard_map/ppermute | solution.py:18
  64.7 19.5 %copy-start.4 = (bf16[1024,256]{1,0:T(8,128)(2,1)S(1)}, bf16[1024,256]{1,0:T(8,128)(2,1)}, u32[]{:S(2)}) copy-start(bf16[1024,256]{1,0:T(8,128)(2,1)} %param.25) | copy-start | bytes 1572868
Sparse Core Ops, SparseCore 0:
  57.6 86.1 reduce-scatter.1

commit v9 on v8

--- a/solution.py
+++ b/solution.py
@@ -18,8 +18,13 @@
     return lax.ppermute(block, axis, route)
 
 
-def attn_kernel(q_ref, o_ref, do_ref, k_ref, v_ref, own_ref, front_ref, own32_ref, front32_ref,
-                dk_scr, dv_scr):
+def attn_kernel(q_ref, o_ref, do_ref, kp_ref, ko_ref, vp_ref, vo_ref, own_ref, front_ref,
+                own32_ref, front32_ref, dk_scr, dv_scr, k_ref, v_ref):
+    prior = kp_ref.shape[0]
+    k_ref[:prior, :] = kp_ref[...]
+    k_ref[prior:, :] = ko_ref[...]
+    v_ref[:prior, :] = vp_ref[...]
+    v_ref[prior:, :] = vo_ref[...]
     rows = q_ref.shape[0]
     ratio = HEADS // KV_HEADS
     scale = HEAD_DIM ** (-0.5)
@@ -76,23 +81,25 @@
         front32_ref[1, :, kv_cols] = dv_all[:WINDOW]
 
 
-def attention_grads(queries, outputs, douts, ext_keys, ext_values):
+def attention_grads(queries, outputs, douts, prior_keys, keys_own, prior_values, values_own):
     rows, q_width = queries.shape
-    span, kv_width = ext_keys.shape
-    vmem = pltpu.MemorySpace.VMEM if hasattr(pltpu, "MemorySpace") else pltpu.VMEM
+    prior, kv_width = prior_keys.shape
+    span = prior + keys_own.shape[0]
     return pl.pallas_call(
         attn_kernel,
         out_shape=[
             jax.ShapeDtypeStruct((rows, q_width + 2 * kv_width), jnp.bfloat16),
-            jax.ShapeDtypeStruct((span - rows, 2 * kv_width), jnp.bfloat16),
+            jax.ShapeDtypeStruct((prior, 2 * kv_width), jnp.bfloat16),
             jax.ShapeDtypeStruct((2, rows, kv_width), jnp.float32),
-            jax.ShapeDtypeStruct((2, span - rows, kv_width), jnp.float32),
+            jax.ShapeDtypeStruct((2, prior, kv_width), jnp.float32),
         ],
         scratch_shapes=[
             pltpu.VMEM((HEAD_DIM, span), jnp.float32),
             pltpu.VMEM((HEAD_DIM, span), jnp.float32),
+            pltpu.VMEM((span, kv_width), prior_keys.dtype),
+            pltpu.VMEM((span, kv_width), prior_values.dtype),
         ],
-    )(queries, outputs, douts, ext_keys, ext_values)
+    )(queries, outputs, douts, prior_keys, keys_own, prior_values, values_own)
 
 
 def wgrad_kernel(x_ref, xp_ref, own_ref, front_ref, out_ref):
@@ -148,10 +155,8 @@
         (inputs_t, prior_keys, prior_values)
     )
     prior_inputs_t = shifted(inputs_after, "seq", 1)
-    ext_keys = jnp.concatenate([prior_keys, keys_own], axis=0)
-    ext_values = jnp.concatenate([prior_values, values_own], axis=0)
     own_grads, front_grads, own32, front32 = attention_grads(
-        queries, outputs_own, douts, ext_keys, ext_values
+        queries, outputs_own, douts, prior_keys, keys_own, prior_values, values_own
     )
     q_span = HEADS * HEAD_DIM
     query_blocks = own_grads[:, :q_span]

time: 154 us -> 152 us (0.987)
  waiting for transfers between devices: 88.8 us -> 91.8 us
  other arithmetic: 2.16 us -> 0 us
  starting transfers between devices: 8.2 us -> 6.24 us
    ppermute x4, waiting for transfers between devices: 30.6 us -> 33.3 us  [shifted(): return lax.ppermute(block, axis, route)]
    concatenate x1 -> x0, other arithmetic: 2.16 us -> none  [body(): ext_keys = jnp.concatenate([prior_keys, keys_own], axis=0)]
    ppermute x4, starting transfers between devices: 8.16 us -> 6.2 us  [shifted(): return lax.ppermute(block, axis, route)]
  transfers between devices with their start and end apart: 5 -> 5, of which waited for: 5 -> 5; matrix products, arithmetic and copies ran while one was open for 5% -> 4% of each run, Pallas kernels for 15% -> 16%
where the time goes in v9:
time: 152 us
  waiting for transfers between devices  91.8 us (60%)
  Pallas kernels  30.4 us (20%)
  between operations  14.1 us (9%)
  starting transfers between devices  6.24 us (4%)
  local copies, waits for them, and re-layouts  4.73 us (3%)
  matrix products  4.46 us (3%)
    reduce_scatter x1, waiting for transfers between devices, body(): lax.psum_scatter(partial, ('seq', 'lat'), scatter_dimension=0, tiled=True)  58.6 us
    ppermute x4, waiting for transfers between devices, shifted(): return lax.ppermute(block, axis, route)  33.3 us
    pallas_call x1, Pallas kernels, attention_grads(): pl.pallas_call(attn_kernel, out_shape=[jax.ShapeDtypeStruct((rows, q_widt...  23.8 us
    pallas_call x1, Pallas kernels, weight_partial(): pl.pallas_call(wgrad_kernel, grid=(model // cols,), in_specs=[x_block, x_...  6.59 us
    ppermute x4, starting transfers between devices, shifted(): return lax.ppermute(block, axis, route)  6.2 us
  transfers between devices with their start and end apart: 5, of which 5 were waited for; matrix products, arithmetic and copies ran while one was open for 4% of the time, Pallas kernels for 16%

profile of v9, /device:TPU:0, one launch (start us, length us, event | category | flops | bytes accessed | tf_op | source)
XLA Modules:
  0.0 151.8 jit_solution(18430463745027376392)
XLA Ops:
  7.2 0.0 copy-start
  7.2 0.0 reduce-scatter.2.cloned.1.call-start
  7.2 3.1 %collective-permute-start = (bf16[512,256]{1,0:T(8,128)(2,1)}, bf16[512,256]{1,0:T(8,128)(2,1)S(1)}, u32[]{:S(2)}, u32[]{:S(2)}) collective-permute-start(bf16[512,256]{1,0:T(8,128)(2,1)} %bitcast.24), channel_id=1, source_target_pairs={{12,0},{0,4},{4,8},{8,12},{13,1},{1,5},{5,9},{9,13},{14,2},{2,6},{... | collective-permute-start | bytes 786440 | tf_op jit(solution)/shard_map/ppermute | solution.py:18
  10.3 1.6 %collective-permute-start.1 = (bf16[512,256]{1,0:T(8,128)(2,1)}, bf16[512,256]{1,0:T(8,128)(2,1)}, u32[]{:S(2)}, u32[]{:S(2)}) collective-permute-start(bf16[512,256]{1,0:T(8,128)(2,1)} %bitcast.26), channel_id=1, source_target_pairs={{12,0},{0,4},{4,8},{8,12},{13,1},{1,5},{5,9},{9,13},{14,2},{2,6},{... | collective-permute-start | bytes 786440 | tf_op jit(solution)/shard_map/ppermute | solution.py:18
  11.9 1.5 copy.13
  13.4 0.0 copy-start.1
  13.4 6.3 %collective-permute-done.kp_ref = bf16[512,256]{1,0:T(8,128)(2,1)S(1)} collective-permute-done((bf16[512,256]{1,0:T(8,128)(2,1)}, bf16[512,256]{1,0:T(8,128)(2,1)S(1)}, u32[]{:S(2)}, u32[]{:S(2)}) %collective-permute-start) | collective-permute-done | bytes 262176 | tf_op jit(solution)/shard_map/ppermute | solution.py:18
  19.7 4.9 %collective-permute-done.1.vp_ref = bf16[512,256]{1,0:T(8,128)(2,1)} collective-permute-done((bf16[512,256]{1,0:T(8,128)(2,1)}, bf16[512,256]{1,0:T(8,128)(2,1)}, u32[]{:S(2)}, u32[]{:S(2)}) %collective-permute-start.1) | collective-permute-done | bytes 262176 | tf_op jit(solution)/shard_map/ppermute | solution.py:18
  24.6 0.0 collective-permute-start.3
  24.6 23.8 %shard_map.130 = (bf16[512,1536]{1,0:T(8,128)(2,1)}, bf16[512,512]{1,0:T(8,128)(2,1)}, f32[2,512,256]{2,1,0:T(8,128)}, f32[2,512,256]{2,1,0:T(8,128)}) custom-call(bf16[512,1024]{1,0:T(8,128)(2,1)} %bitcast.21, bf16[512,1024]{1,0:T(8,128)(2,1)} %bitcast.22, bf16[512,1024]{1,0:T(8,128)(2,1)} %bitcast.23, bf16[512,256]{1,0:T(8,128)(2,1)} %copy-done.5, ...), custom_call_target="tpu_custom_call" | custom-call | tf_op jit(solution)/shard_map/pallas_call | solution.py:88
  48.4 2.4 %collective-permute-done.3.xp_ref = bf16[1024,512]{1,0:T(8,128)(2,1)} collective-permute-done((bf16[1024,512]{1,0:T(8,128)(2,1)S(1)}, bf16[1024,512]{1,0:T(8,128)(2,1)}, u32[]{:S(2)}, u32[]{:S(2)}) %collective-permute-start.3) | collective-permute-done | bytes 1048608 | tf_op jit(solution)/shard_map/ppermute | solution.py:18
  50.8 6.6 %shard_map.131 = f32[1024,1536]{1,0:T(8,128)} custom-call(bf16[1024,512]{1,0:T(8,128)(2,1)} %bitcast.20, bf16[1024,512]{1,0:T(8,128)(2,1)} %collective-permute-done.3.xp_ref, bf16[512,1536]{1,0:T(8,128)(2,1)} %get-tuple-element.53.own_ref, bf16[512,512]{1,0:T(8,128)(2,1)} %get-tuple-element.57.front_ref), custom_call_target="tpu_custom_call" | custom-call | tf_op jit(solution)/shard_map/pallas_call | solution.py:118
  57.4 0.0 reduce-scatter.2.cloned.1.call-update
  57.4 0.0 copy-start.2
  57.4 0.0 copy-start.3
  57.5 1.5 collective-permute-start.2
  59.0 2.5 %fusion.1 = f32[512,1024]{1,0:T(8,128)S(1)} fusion(bf16[1024,1024]{1,0:T(8,128)(2,1)S(1)} %copy-done, bf16[512,1536]{1,0:T(8,128)(2,1)} %get-tuple-element.53.own_ref), kind=kOutput, calls=%fused_computation.2 | convolution fusion | flops 1073741824 | bytes 5242880 | tf_op jit(solution)/shard_map/dot_general | solution.py:167
  61.5 0.0 copy-start.4
  61.5 19.7 %collective-permute-done.2 = f32[2,512,256]{2,1,0:T(8,128)S(1)} collective-permute-done((f32[2,512,256]{2,1,0:T(8,128)}, f32[2,512,256]{2,1,0:T(8,128)S(1)}, u32[]{:S(2)}, u32[]{:S(2)}) %collective-permute-start.2) | collective-permute-done | bytes 1048608 | tf_op jit(solution)/shard_map/ppermute | solution.py:18
  81.2 0.5 fusion.6
  81.7 1.5 fusion
  83.2 58.6 %reduce-scatter.2.cloned.1.call-done = f32[64,1536]{1,0:T(8,128)} async-done(((f32[1024,1536]{1,0:T(8,128)}), f32[64,1536]{1,0:T(8,128)}) %reduce-scatter.2.cloned.1.call-update) | async-done | bytes 393232 | tf_op jit(solution)/shard_map/reduce_scatter | solution.py:178
  141.7 1.5 %fusion.10 = (f32[64,256]{1,0:T(8,128)}, f32[64,256]{1,0:T(8,128)}) fusion(f32[64,1536]{1,0:T(8,128)} %reduce-scatter.2.cloned.1.call-done), kind=kLoop, calls=%fused_computation.11 | loop fusion | bytes 262144 | tf_op jit(solution)/shard_map/slice | solution.py:182
  143.3 1.7 %slice.62 = f32[64,1024]{1,0:T(8,128)} slice(f32[64,1536]{1,0:T(8,128)} %reduce-scatter.2.cloned.1.call-done), slice={[0:64], [0:1024]} | slice | bytes 524288 | tf_op jit(solution)/shard_map/slice | solution.py:180
  (7 shorter events, 0.0 us)
Async XLA Ops:
  7.2 51.8 %copy-start = (bf16[1024,1024]{1,0:T(8,128)(2,1)S(1)}, bf16[1024,1024]{1,0:T(8,128)(2,1)}, u32[]{:S(2)}) copy-start(bf16[1024,1024]{1,0:T(8,128)(2,1)} %param.23) | copy-start | bytes 6291460
  7.2 134.5 %reduce-scatter.2.cloned.1.call-start = ((), (), s32[]{:S(2)}) async-start(), calls=%async_computation.1 | async-start | bytes 6684672 | tf_op jit(solution)/shard_map/reduce_scatter | solution.py:178
  7.2 12.5 %collective-permute-start = (bf16[512,256]{1,0:T(8,128)(2,1)}, bf16[512,256]{1,0:T(8,128)(2,1)S(1)}, u32[]{:S(2)}, u32[]{:S(2)}) collective-permute-start(bf16[512,256]{1,0:T(8,128)(2,1)} %bitcast.24), channel_id=1, source_target_pairs={{12,0},{0,4},{4,8},{8,12},{13,1},{1,5},{5,9},{9,13},{14,2},{2,6},{... | collective-permute-start | bytes 786440 | tf_op jit(solution)/shard_map/ppermute | solution.py:18
  10.3 14.3 %collective-permute-start.1 = (bf16[512,256]{1,0:T(8,128)(2,1)}, bf16[512,256]{1,0:T(8,128)(2,1)}, u32[]{:S(2)}, u32[]{:S(2)}) collective-permute-start(bf16[512,256]{1,0:T(8,128)(2,1)} %bitcast.26), channel_id=1, source_target_pairs={{12,0},{0,4},{4,8},{8,12},{13,1},{1,5},{5,9},{9,13},{14,2},{2,6},{... | collective-permute-start | bytes 786440 | tf_op jit(solution)/shard_map/ppermute | solution.py:18
  13.4 35.0 %copy-start.1 = (bf16[1,512,1024]{1,2,0:T(8,128)(2,1)}, bf16[1,512,1024]{1,2,0:T(8,128)(2,1)S(1)}, u32[]{:S(2)}) copy-start(bf16[1,512,1024]{1,2,0:T(8,128)(2,1)S(1)} %copy.13) | copy-start | bytes 3145732
  19.7 4.9 %copy-start.5 = (bf16[512,256]{1,0:T(8,128)(2,1)}, bf16[512,256]{1,0:T(8,128)(2,1)S(1)}, u32[]{:S(2)}) copy-start(bf16[512,256]{1,0:T(8,128)(2,1)S(1)} %collective-permute-done.kp_ref) | copy-start | bytes 786436
  24.6 26.2 %collective-permute-start.3 = (bf16[1024,512]{1,0:T(8,128)(2,1)S(1)}, bf16[1024,512]{1,0:T(8,128)(2,1)}, u32[]{:S(2)}, u32[]{:S(2)}) collective-permute-start(bf16[1024,512]{1,0:T(8,128)(2,1)S(1)} %bitcast.19), channel_id=1, source_target_pairs={{12,0},{0,4},{4,8},{8,12},{13,1},{1,5},{5,9},{9,13},{14,2},{2,6},{... | collective-permute-start | bytes 3145736 | tf_op jit(solution)/shard_map/ppermute | solution.py:18
  57.4 23.8 %copy-start.2 = (f32[2,512,256]{2,1,0:T(8,128)S(1)}, f32[2,512,256]{2,1,0:T(8,128)}, u32[]{:S(2)}) copy-start(f32[2,512,256]{2,1,0:T(8,128)} %get-tuple-element.54) | copy-start | bytes 3145732
  57.4 23.7 %copy-start.3 = (bf16[1024,256]{1,0:T(8,128)(2,1)S(1)}, bf16[1024,256]{1,0:T(8,128)(2,1)}, u32[]{:S(2)}) copy-start(bf16[1024,256]{1,0:T(8,128)(2,1)} %param.24) | copy-start | bytes 1572868
  57.5 23.7 %collective-permute-start.2 = (f32[2,512,256]{2,1,0:T(8,128)}, f32[2,512,256]{2,1,0:T(8,128)S(1)}, u32[]{:S(2)}, u32[]{:S(2)}) collective-permute-start(f32[2,512,256]{2,1,0:T(8,128)} %get-tuple-element.55), channel_id=1, source_target_pairs={{4,0},{8,4},{12,8},{0,12},{5,1},{9,5},{13,9},{1,13},{6,2},{10,6},{... | collective-permute-start | bytes 3145736 | tf_op jit(solution)/shard_map/ppermute | solution.py:18
  61.5 20.2 %copy-start.4 = (bf16[1024,256]{1,0:T(8,128)(2,1)S(1)}, bf16[1024,256]{1,0:T(8,128)(2,1)}, u32[]{:S(2)}) copy-start(bf16[1024,256]{1,0:T(8,128)(2,1)} %param.25) | copy-start | bytes 1572868
Sparse Core Ops, SparseCore 0:
  57.6 84.1 reduce-scatter.1

commit v10 on v9

--- a/solution.py
+++ b/solution.py
@@ -129,6 +129,26 @@
     )(inputs_t, prior_inputs_t, own_grads, front_grads)
 
 
+def split_kernel(src_ref, q_out, k_out, v_out):
+    q_width = q_out.shape[1]
+    kv_width = k_out.shape[1]
+    q_out[...] = src_ref[:, :q_width]
+    k_out[...] = src_ref[:, q_width : q_width + kv_width]
+    v_out[...] = src_ref[:, q_width + kv_width :]
+
+
+def split_columns(owned, q_width, kv_width):
+    rows = owned.shape[0]
+    return pl.pallas_call(
+        split_kernel,
+        out_shape=[
+            jax.ShapeDtypeStruct((rows, q_width), owned.dtype),
+            jax.ShapeDtypeStruct((rows, kv_width), owned.dtype),
+            jax.ShapeDtypeStruct((rows, kv_width), owned.dtype),
+        ],
+    )(owned)
+
+
 def body(
     layer_input,
     query_rows,
@@ -176,10 +196,9 @@
     input_grad = summed.astype(jnp.bfloat16)[None]
     partial = weight_partial(inputs_t, prior_inputs_t[:, tokens - WINDOW :], own_grads, front_grads)
     owned = lax.psum_scatter(partial, ("seq", "lat"), scatter_dimension=0, tiled=True)
-    q_width = HEADS * HEAD_DIM
-    query_weight_grad = owned[:, :q_width]
-    key_weight_grad = owned[:, q_width : q_width + kv_width]
-    value_weight_grad = owned[:, q_width + kv_width :]
+    query_weight_grad, key_weight_grad, value_weight_grad = split_columns(
+        owned, HEADS * HEAD_DIM, kv_width
+    )
     return (input_grad, query_weight_grad, key_weight_grad, value_weight_grad)
 
 

time: 152 us -> 151 us (level)
  local copies, waits for them, and re-layouts: 4.73 us -> 1.53 us
  Pallas kernels: 30.4 us -> 32.2 us
    slice x2 -> x0, local copies, waits for them, and re-layouts: 3.2 us -> none  [the longest x1 1.67 us: body(): query_weight_grad = owned[:, :q_width]]
    pallas_call x0 -> x1, Pallas kernels: none -> 1.74 us  [split_columns(): pl.pallas_call(split_kernel, out_shape=[jax.ShapeDtypeStruct((rows, q_wid...]
where the time goes in v10:
time: 151 us; the launch traced here: 150 us
  waiting for transfers between devices  91.8 us (61%)
  Pallas kernels  32.2 us (21%)
  between operations  14.1 us (9%)
  starting transfers between devices  6.24 us (4%)
  matrix products  4.46 us (3%)
  local copies, waits for them, and re-layouts  1.53 us (1%)
    reduce_scatter x1, waiting for transfers between devices, body(): lax.psum_scatter(partial, ('seq', 'lat'), scatter_dimension=0, tiled=True)  58.6 us
    ppermute x4, waiting for transfers between devices, shifted(): return lax.ppermute(block, axis, route)  33.3 us
    pallas_call x1, Pallas kernels, attention_grads(): pl.pallas_call(attn_kernel, out_shape=[jax.ShapeDtypeStruct((rows, q_widt...  23.8 us
    pallas_call x1, Pallas kernels, weight_partial(): pl.pallas_call(wgrad_kernel, grid=(model // cols,), in_specs=[x_block, x_...  6.59 us
    ppermute x4, starting transfers between devices, shifted(): return lax.ppermute(block, axis, route)  6.2 us
  transfers between devices with their start and end apart: 5, of which 5 were waited for; matrix products, arithmetic and copies ran while one was open for 4% of the time, Pallas kernels for 16%

profile of v10, /device:TPU:0, one launch (start us, length us, event | category | flops | bytes accessed | tf_op | source)
XLA Modules:
  0.0 150.3 jit_solution(1102521771122807087)
XLA Ops:
  7.2 0.0 copy-start
  7.2 0.0 reduce-scatter.2.cloned.1.call-start
  7.2 3.1 %collective-permute-start = (bf16[512,256]{1,0:T(8,128)(2,1)}, bf16[512,256]{1,0:T(8,128)(2,1)S(1)}, u32[]{:S(2)}, u32[]{:S(2)}) collective-permute-start(bf16[512,256]{1,0:T(8,128)(2,1)} %bitcast.24), channel_id=1, source_target_pairs={{12,0},{0,4},{4,8},{8,12},{13,1},{1,5},{5,9},{9,13},{14,2},{2,6},{... | collective-permute-start | bytes 786440 | tf_op jit(solution)/shard_map/ppermute | solution.py:18
  10.3 1.6 %collective-permute-start.1 = (bf16[512,256]{1,0:T(8,128)(2,1)}, bf16[512,256]{1,0:T(8,128)(2,1)}, u32[]{:S(2)}, u32[]{:S(2)}) collective-permute-start(bf16[512,256]{1,0:T(8,128)(2,1)} %bitcast.26), channel_id=1, source_target_pairs={{12,0},{0,4},{4,8},{8,12},{13,1},{1,5},{5,9},{9,13},{14,2},{2,6},{... | collective-permute-start | bytes 786440 | tf_op jit(solution)/shard_map/ppermute | solution.py:18
  11.9 1.5 copy.13
  13.4 0.0 copy-start.1
  13.4 6.3 %collective-permute-done.kp_ref = bf16[512,256]{1,0:T(8,128)(2,1)S(1)} collective-permute-done((bf16[512,256]{1,0:T(8,128)(2,1)}, bf16[512,256]{1,0:T(8,128)(2,1)S(1)}, u32[]{:S(2)}, u32[]{:S(2)}) %collective-permute-start) | collective-permute-done | bytes 262176 | tf_op jit(solution)/shard_map/ppermute | solution.py:18
  19.7 4.9 %collective-permute-done.1.vp_ref = bf16[512,256]{1,0:T(8,128)(2,1)} collective-permute-done((bf16[512,256]{1,0:T(8,128)(2,1)}, bf16[512,256]{1,0:T(8,128)(2,1)}, u32[]{:S(2)}, u32[]{:S(2)}) %collective-permute-start.1) | collective-permute-done | bytes 262176 | tf_op jit(solution)/shard_map/ppermute | solution.py:18
  24.6 0.0 collective-permute-start.3
  24.6 23.8 %shard_map.130 = (bf16[512,1536]{1,0:T(8,128)(2,1)}, bf16[512,512]{1,0:T(8,128)(2,1)}, f32[2,512,256]{2,1,0:T(8,128)}, f32[2,512,256]{2,1,0:T(8,128)}) custom-call(bf16[512,1024]{1,0:T(8,128)(2,1)} %bitcast.21, bf16[512,1024]{1,0:T(8,128)(2,1)} %bitcast.22, bf16[512,1024]{1,0:T(8,128)(2,1)} %bitcast.23, bf16[512,256]{1,0:T(8,128)(2,1)} %copy-done.5, ...), custom_call_target="tpu_custom_call" | custom-call | tf_op jit(solution)/shard_map/pallas_call | solution.py:88
  48.4 2.4 %collective-permute-done.3.xp_ref = bf16[1024,512]{1,0:T(8,128)(2,1)} collective-permute-done((bf16[1024,512]{1,0:T(8,128)(2,1)S(1)}, bf16[1024,512]{1,0:T(8,128)(2,1)}, u32[]{:S(2)}, u32[]{:S(2)}) %collective-permute-start.3) | collective-permute-done | bytes 1048608 | tf_op jit(solution)/shard_map/ppermute | solution.py:18
  50.8 6.6 %shard_map.131 = f32[1024,1536]{1,0:T(8,128)} custom-call(bf16[1024,512]{1,0:T(8,128)(2,1)} %bitcast.20, bf16[1024,512]{1,0:T(8,128)(2,1)} %collective-permute-done.3.xp_ref, bf16[512,1536]{1,0:T(8,128)(2,1)} %get-tuple-element.56.own_ref, bf16[512,512]{1,0:T(8,128)(2,1)} %get-tuple-element.60.front_ref), custom_call_target="tpu_custom_call" | custom-call | tf_op jit(solution)/shard_map/pallas_call | solution.py:118
  57.4 0.0 reduce-scatter.2.cloned.1.call-update
  57.4 0.0 copy-start.2
  57.4 0.0 copy-start.3
  57.5 1.5 %collective-permute-start.2 = (f32[2,512,256]{2,1,0:T(8,128)}, f32[2,512,256]{2,1,0:T(8,128)S(1)}, u32[]{:S(2)}, u32[]{:S(2)}) collective-permute-start(f32[2,512,256]{2,1,0:T(8,128)} %get-tuple-element.58), channel_id=1, source_target_pairs={{4,0},{8,4},{12,8},{0,12},{5,1},{9,5},{13,9},{1,13},{6,2},{10,6},{... | collective-permute-start | bytes 3145736 | tf_op jit(solution)/shard_map/ppermute | solution.py:18
  59.0 2.5 %fusion.1 = f32[512,1024]{1,0:T(8,128)S(1)} fusion(bf16[1024,1024]{1,0:T(8,128)(2,1)S(1)} %copy-done, bf16[512,1536]{1,0:T(8,128)(2,1)} %get-tuple-element.56.own_ref), kind=kOutput, calls=%fused_computation.2 | convolution fusion | flops 1073741824 | bytes 5242880 | tf_op jit(solution)/shard_map/dot_general | solution.py:187
  61.5 0.0 copy-start.4
  61.5 19.7 %collective-permute-done.2 = f32[2,512,256]{2,1,0:T(8,128)S(1)} collective-permute-done((f32[2,512,256]{2,1,0:T(8,128)}, f32[2,512,256]{2,1,0:T(8,128)S(1)}, u32[]{:S(2)}, u32[]{:S(2)}) %collective-permute-start.2) | collective-permute-done | bytes 1048608 | tf_op jit(solution)/shard_map/ppermute | solution.py:18
  81.2 0.0 copy-done.3
  81.2 0.5 fusion.6
  81.7 1.5 fusion
  83.2 58.6 %reduce-scatter.2.cloned.1.call-done.src_ref = f32[64,1536]{1,0:T(8,128)} async-done(((f32[1024,1536]{1,0:T(8,128)}), f32[64,1536]{1,0:T(8,128)}) %reduce-scatter.2.cloned.1.call-update) | async-done | bytes 393232 | tf_op jit(solution)/shard_map/reduce_scatter | solution.py:198
  141.7 1.7 %shard_map.132 = (f32[64,1024]{1,0:T(8,128)}, f32[64,256]{1,0:T(8,128)}, f32[64,256]{1,0:T(8,128)}) custom-call(f32[64,1536]{1,0:T(8,128)} %reduce-scatter.2.cloned.1.call-done.src_ref), custom_call_target="tpu_custom_call" | custom-call | tf_op jit(solution)/shard_map/pallas_call | solution.py:142
  (6 shorter events, 0.0 us)
Async XLA Ops:
  7.2 51.8 %copy-start = (bf16[1024,1024]{1,0:T(8,128)(2,1)S(1)}, bf16[1024,1024]{1,0:T(8,128)(2,1)}, u32[]{:S(2)}) copy-start(bf16[1024,1024]{1,0:T(8,128)(2,1)} %param.23) | copy-start | bytes 6291460
  7.2 134.5 %reduce-scatter.2.cloned.1.call-start = ((), (), s32[]{:S(2)}) async-start(), calls=%async_computation.1 | async-start | bytes 6684672 | tf_op jit(solution)/shard_map/reduce_scatter | solution.py:198
  7.2 12.5 %collective-permute-start = (bf16[512,256]{1,0:T(8,128)(2,1)}, bf16[512,256]{1,0:T(8,128)(2,1)S(1)}, u32[]{:S(2)}, u32[]{:S(2)}) collective-permute-start(bf16[512,256]{1,0:T(8,128)(2,1)} %bitcast.24), channel_id=1, source_target_pairs={{12,0},{0,4},{4,8},{8,12},{13,1},{1,5},{5,9},{9,13},{14,2},{2,6},{... | collective-permute-start | bytes 786440 | tf_op jit(solution)/shard_map/ppermute | solution.py:18
  10.3 14.3 %collective-permute-start.1 = (bf16[512,256]{1,0:T(8,128)(2,1)}, bf16[512,256]{1,0:T(8,128)(2,1)}, u32[]{:S(2)}, u32[]{:S(2)}) collective-permute-start(bf16[512,256]{1,0:T(8,128)(2,1)} %bitcast.26), channel_id=1, source_target_pairs={{12,0},{0,4},{4,8},{8,12},{13,1},{1,5},{5,9},{9,13},{14,2},{2,6},{... | collective-permute-start | bytes 786440 | tf_op jit(solution)/shard_map/ppermute | solution.py:18
  13.4 35.0 %copy-start.1 = (bf16[1,512,1024]{1,2,0:T(8,128)(2,1)}, bf16[1,512,1024]{1,2,0:T(8,128)(2,1)S(1)}, u32[]{:S(2)}) copy-start(bf16[1,512,1024]{1,2,0:T(8,128)(2,1)S(1)} %copy.13) | copy-start | bytes 3145732
  19.7 4.9 %copy-start.5 = (bf16[512,256]{1,0:T(8,128)(2,1)}, bf16[512,256]{1,0:T(8,128)(2,1)S(1)}, u32[]{:S(2)}) copy-start(bf16[512,256]{1,0:T(8,128)(2,1)S(1)} %collective-permute-done.kp_ref) | copy-start | bytes 786436
  24.6 26.2 %collective-permute-start.3 = (bf16[1024,512]{1,0:T(8,128)(2,1)S(1)}, bf16[1024,512]{1,0:T(8,128)(2,1)}, u32[]{:S(2)}, u32[]{:S(2)}) collective-permute-start(bf16[1024,512]{1,0:T(8,128)(2,1)S(1)} %bitcast.19), channel_id=1, source_target_pairs={{12,0},{0,4},{4,8},{8,12},{13,1},{1,5},{5,9},{9,13},{14,2},{2,6},{... | collective-permute-start | bytes 3145736 | tf_op jit(solution)/shard_map/ppermute | solution.py:18
  57.4 23.8 %copy-start.2 = (f32[2,512,256]{2,1,0:T(8,128)S(1)}, f32[2,512,256]{2,1,0:T(8,128)}, u32[]{:S(2)}) copy-start(f32[2,512,256]{2,1,0:T(8,128)} %get-tuple-element.57) | copy-start | bytes 3145732
  57.4 23.7 %copy-start.3 = (bf16[1024,256]{1,0:T(8,128)(2,1)S(1)}, bf16[1024,256]{1,0:T(8,128)(2,1)}, u32[]{:S(2)}) copy-start(bf16[1024,256]{1,0:T(8,128)(2,1)} %param.24) | copy-start | bytes 1572868
  57.5 23.7 %collective-permute-start.2 = (f32[2,512,256]{2,1,0:T(8,128)}, f32[2,512,256]{2,1,0:T(8,128)S(1)}, u32[]{:S(2)}, u32[]{:S(2)}) collective-permute-start(f32[2,512,256]{2,1,0:T(8,128)} %get-tuple-element.58), channel_id=1, source_target_pairs={{4,0},{8,4},{12,8},{0,12},{5,1},{9,5},{13,9},{1,13},{6,2},{10,6},{... | collective-permute-start | bytes 3145736 | tf_op jit(solution)/shard_map/ppermute | solution.py:18
  61.5 20.2 %copy-start.4 = (bf16[1024,256]{1,0:T(8,128)(2,1)S(1)}, bf16[1024,256]{1,0:T(8,128)(2,1)}, u32[]{:S(2)}) copy-start(bf16[1024,256]{1,0:T(8,128)(2,1)} %param.25) | copy-start | bytes 1572868
Sparse Core Ops, SparseCore 0:
  57.6 84.1 reduce-scatter.1

commit v11 on v10

--- a/solution.py
+++ b/solution.py
@@ -113,7 +113,7 @@
 def weight_partial(inputs_t, prior_inputs_t, own_grads, front_grads):
     model, tokens = inputs_t.shape
     width = own_grads.shape[1]
-    cols = 256 if model % 256 == 0 else model
+    cols = 512 if model % 512 == 0 else model
     x_block = pl.BlockSpec((cols, tokens), lambda i: (i, 0))
     return pl.pallas_call(
         wgrad_kernel,

time: 151 us -> 150 us (level)
  no operation moved by 1% of the time
where the time goes in v11:
time: 150 us
  waiting for transfers between devices  91.8 us (61%)
  Pallas kernels  31.6 us (21%)
  between operations  14.1 us (9%)
  starting transfers between devices  6.24 us (4%)
  matrix products  4.47 us (3%)
  local copies, waits for them, and re-layouts  1.53 us (1%)
    reduce_scatter x1, waiting for transfers between devices, body(): lax.psum_scatter(partial, ('seq', 'lat'), scatter_dimension=0, tiled=True)  58.6 us
    ppermute x4, waiting for transfers between devices, shifted(): return lax.ppermute(block, axis, route)  33.3 us
    pallas_call x1, Pallas kernels, attention_grads(): pl.pallas_call(attn_kernel, out_shape=[jax.ShapeDtypeStruct((rows, q_widt...  23.8 us
    ppermute x4, starting transfers between devices, shifted(): return lax.ppermute(block, axis, route)  6.2 us
    pallas_call x1, Pallas kernels, weight_partial(): pl.pallas_call(wgrad_kernel, grid=(model // cols,), in_specs=[x_block, x_...  6.04 us
  transfers between devices with their start and end apart: 5, of which 5 were waited for; matrix products, arithmetic and copies ran while one was open for 4% of the time, Pallas kernels for 16%

profile of v11, /device:TPU:0, one launch (start us, length us, event | category | flops | bytes accessed | tf_op | source)
XLA Modules:
  0.0 149.8 jit_solution(3721262996282733297)
XLA Ops:
  7.2 0.0 copy-start
  7.2 0.0 reduce-scatter.2.cloned.1.call-start
  7.2 3.1 %collective-permute-start = (bf16[512,256]{1,0:T(8,128)(2,1)}, bf16[512,256]{1,0:T(8,128)(2,1)S(1)}, u32[]{:S(2)}, u32[]{:S(2)}) collective-permute-start(bf16[512,256]{1,0:T(8,128)(2,1)} %bitcast.24), channel_id=1, source_target_pairs={{12,0},{0,4},{4,8},{8,12},{13,1},{1,5},{5,9},{9,13},{14,2},{2,6},{... | collective-permute-start | bytes 786440 | tf_op jit(solution)/shard_map/ppermute | solution.py:18
  10.3 1.6 %collective-permute-start.1 = (bf16[512,256]{1,0:T(8,128)(2,1)}, bf16[512,256]{1,0:T(8,128)(2,1)}, u32[]{:S(2)}, u32[]{:S(2)}) collective-permute-start(bf16[512,256]{1,0:T(8,128)(2,1)} %bitcast.26), channel_id=1, source_target_pairs={{12,0},{0,4},{4,8},{8,12},{13,1},{1,5},{5,9},{9,13},{14,2},{2,6},{... | collective-permute-start | bytes 786440 | tf_op jit(solution)/shard_map/ppermute | solution.py:18
  11.9 1.5 copy.13
  13.4 0.0 copy-start.1
  13.4 6.3 %collective-permute-done.kp_ref = bf16[512,256]{1,0:T(8,128)(2,1)S(1)} collective-permute-done((bf16[512,256]{1,0:T(8,128)(2,1)}, bf16[512,256]{1,0:T(8,128)(2,1)S(1)}, u32[]{:S(2)}, u32[]{:S(2)}) %collective-permute-start) | collective-permute-done | bytes 262176 | tf_op jit(solution)/shard_map/ppermute | solution.py:18
  19.7 4.9 %collective-permute-done.1.vp_ref = bf16[512,256]{1,0:T(8,128)(2,1)} collective-permute-done((bf16[512,256]{1,0:T(8,128)(2,1)}, bf16[512,256]{1,0:T(8,128)(2,1)}, u32[]{:S(2)}, u32[]{:S(2)}) %collective-permute-start.1) | collective-permute-done | bytes 262176 | tf_op jit(solution)/shard_map/ppermute | solution.py:18
  24.6 0.0 collective-permute-start.3
  24.6 23.8 %shard_map.130 = (bf16[512,1536]{1,0:T(8,128)(2,1)}, bf16[512,512]{1,0:T(8,128)(2,1)}, f32[2,512,256]{2,1,0:T(8,128)}, f32[2,512,256]{2,1,0:T(8,128)}) custom-call(bf16[512,1024]{1,0:T(8,128)(2,1)} %bitcast.21, bf16[512,1024]{1,0:T(8,128)(2,1)} %bitcast.22, bf16[512,1024]{1,0:T(8,128)(2,1)} %bitcast.23, bf16[512,256]{1,0:T(8,128)(2,1)} %copy-done.5, ...), custom_call_target="tpu_custom_call" | custom-call | tf_op jit(solution)/shard_map/pallas_call | solution.py:88
  48.4 2.4 %collective-permute-done.3.xp_ref = bf16[1024,512]{1,0:T(8,128)(2,1)} collective-permute-done((bf16[1024,512]{1,0:T(8,128)(2,1)S(1)}, bf16[1024,512]{1,0:T(8,128)(2,1)}, u32[]{:S(2)}, u32[]{:S(2)}) %collective-permute-start.3) | collective-permute-done | bytes 1048608 | tf_op jit(solution)/shard_map/ppermute | solution.py:18
  50.8 6.0 %shard_map.131 = f32[1024,1536]{1,0:T(8,128)} custom-call(bf16[1024,512]{1,0:T(8,128)(2,1)} %bitcast.20, bf16[1024,512]{1,0:T(8,128)(2,1)} %collective-permute-done.3.xp_ref, bf16[512,1536]{1,0:T(8,128)(2,1)} %get-tuple-element.56.own_ref, bf16[512,512]{1,0:T(8,128)(2,1)} %get-tuple-element.60.front_ref), custom_call_target="tpu_custom_call" | custom-call | tf_op jit(solution)/shard_map/pallas_call | solution.py:118
  56.9 0.0 reduce-scatter.2.cloned.1.call-update
  56.9 0.0 copy-start.2
  56.9 0.0 copy-start.3
  56.9 1.5 %collective-permute-start.2 = (f32[2,512,256]{2,1,0:T(8,128)}, f32[2,512,256]{2,1,0:T(8,128)S(1)}, u32[]{:S(2)}, u32[]{:S(2)}) collective-permute-start(f32[2,512,256]{2,1,0:T(8,128)} %get-tuple-element.58), channel_id=1, source_target_pairs={{4,0},{8,4},{12,8},{0,12},{5,1},{9,5},{13,9},{1,13},{6,2},{10,6},{... | collective-permute-start | bytes 3145736 | tf_op jit(solution)/shard_map/ppermute | solution.py:18
  58.4 0.0 copy-done
  58.4 2.5 %fusion.1 = f32[512,1024]{1,0:T(8,128)S(1)} fusion(bf16[1024,1024]{1,0:T(8,128)(2,1)S(1)} %copy-done, bf16[512,1536]{1,0:T(8,128)(2,1)} %get-tuple-element.56.own_ref), kind=kOutput, calls=%fused_computation.2 | convolution fusion | flops 1073741824 | bytes 5242880 | tf_op jit(solution)/shard_map/dot_general | solution.py:187
  60.9 0.0 copy-start.4
  61.0 19.7 %collective-permute-done.2 = f32[2,512,256]{2,1,0:T(8,128)S(1)} collective-permute-done((f32[2,512,256]{2,1,0:T(8,128)}, f32[2,512,256]{2,1,0:T(8,128)S(1)}, u32[]{:S(2)}, u32[]{:S(2)}) %collective-permute-start.2) | collective-permute-done | bytes 1048608 | tf_op jit(solution)/shard_map/ppermute | solution.py:18
  80.6 0.5 fusion.6
  81.2 1.5 fusion
  82.6 58.6 %reduce-scatter.2.cloned.1.call-done.src_ref = f32[64,1536]{1,0:T(8,128)} async-done(((f32[1024,1536]{1,0:T(8,128)}), f32[64,1536]{1,0:T(8,128)}) %reduce-scatter.2.cloned.1.call-update) | async-done | bytes 393232 | tf_op jit(solution)/shard_map/reduce_scatter | solution.py:198
  141.2 1.7 %shard_map.132 = (f32[64,1024]{1,0:T(8,128)}, f32[64,256]{1,0:T(8,128)}, f32[64,256]{1,0:T(8,128)}) custom-call(f32[64,1536]{1,0:T(8,128)} %reduce-scatter.2.cloned.1.call-done.src_ref), custom_call_target="tpu_custom_call" | custom-call | tf_op jit(solution)/shard_map/pallas_call | solution.py:142
  (6 shorter events, 0.0 us)
Async XLA Ops:
  7.2 51.3 %copy-start = (bf16[1024,1024]{1,0:T(8,128)(2,1)S(1)}, bf16[1024,1024]{1,0:T(8,128)(2,1)}, u32[]{:S(2)}) copy-start(bf16[1024,1024]{1,0:T(8,128)(2,1)} %param.23) | copy-start | bytes 6291460
  7.2 134.0 %reduce-scatter.2.cloned.1.call-start = ((), (), s32[]{:S(2)}) async-start(), calls=%async_computation.1 | async-start | bytes 6684672 | tf_op jit(solution)/shard_map/reduce_scatter | solution.py:198
  7.2 12.5 %collective-permute-start = (bf16[512,256]{1,0:T(8,128)(2,1)}, bf16[512,256]{1,0:T(8,128)(2,1)S(1)}, u32[]{:S(2)}, u32[]{:S(2)}) collective-permute-start(bf16[512,256]{1,0:T(8,128)(2,1)} %bitcast.24), channel_id=1, source_target_pairs={{12,0},{0,4},{4,8},{8,12},{13,1},{1,5},{5,9},{9,13},{14,2},{2,6},{... | collective-permute-start | bytes 786440 | tf_op jit(solution)/shard_map/ppermute | solution.py:18
  10.3 14.3 %collective-permute-start.1 = (bf16[512,256]{1,0:T(8,128)(2,1)}, bf16[512,256]{1,0:T(8,128)(2,1)}, u32[]{:S(2)}, u32[]{:S(2)}) collective-permute-start(bf16[512,256]{1,0:T(8,128)(2,1)} %bitcast.26), channel_id=1, source_target_pairs={{12,0},{0,4},{4,8},{8,12},{13,1},{1,5},{5,9},{9,13},{14,2},{2,6},{... | collective-permute-start | bytes 786440 | tf_op jit(solution)/shard_map/ppermute | solution.py:18
  13.4 35.0 %copy-start.1 = (bf16[1,512,1024]{1,2,0:T(8,128)(2,1)}, bf16[1,512,1024]{1,2,0:T(8,128)(2,1)S(1)}, u32[]{:S(2)}) copy-start(bf16[1,512,1024]{1,2,0:T(8,128)(2,1)S(1)} %copy.13) | copy-start | bytes 3145732
  19.7 4.9 %copy-start.5 = (bf16[512,256]{1,0:T(8,128)(2,1)}, bf16[512,256]{1,0:T(8,128)(2,1)S(1)}, u32[]{:S(2)}) copy-start(bf16[512,256]{1,0:T(8,128)(2,1)S(1)} %collective-permute-done.kp_ref) | copy-start | bytes 786436
  24.6 26.2 %collective-permute-start.3 = (bf16[1024,512]{1,0:T(8,128)(2,1)S(1)}, bf16[1024,512]{1,0:T(8,128)(2,1)}, u32[]{:S(2)}, u32[]{:S(2)}) collective-permute-start(bf16[1024,512]{1,0:T(8,128)(2,1)S(1)} %bitcast.19), channel_id=1, source_target_pairs={{12,0},{0,4},{4,8},{8,12},{13,1},{1,5},{5,9},{9,13},{14,2},{2,6},{... | collective-permute-start | bytes 3145736 | tf_op jit(solution)/shard_map/ppermute | solution.py:18
  56.9 23.8 %copy-start.2 = (f32[2,512,256]{2,1,0:T(8,128)S(1)}, f32[2,512,256]{2,1,0:T(8,128)}, u32[]{:S(2)}) copy-start(f32[2,512,256]{2,1,0:T(8,128)} %get-tuple-element.57) | copy-start | bytes 3145732
  56.9 23.7 %copy-start.3 = (bf16[1024,256]{1,0:T(8,128)(2,1)S(1)}, bf16[1024,256]{1,0:T(8,128)(2,1)}, u32[]{:S(2)}) copy-start(bf16[1024,256]{1,0:T(8,128)(2,1)} %param.24) | copy-start | bytes 1572868
  56.9 23.7 %collective-permute-start.2 = (f32[2,512,256]{2,1,0:T(8,128)}, f32[2,512,256]{2,1,0:T(8,128)S(1)}, u32[]{:S(2)}, u32[]{:S(2)}) collective-permute-start(f32[2,512,256]{2,1,0:T(8,128)} %get-tuple-element.58), channel_id=1, source_target_pairs={{4,0},{8,4},{12,8},{0,12},{5,1},{9,5},{13,9},{1,13},{6,2},{10,6},{... | collective-permute-start | bytes 3145736 | tf_op jit(solution)/shard_map/ppermute | solution.py:18
  60.9 20.2 %copy-start.4 = (bf16[1024,256]{1,0:T(8,128)(2,1)S(1)}, bf16[1024,256]{1,0:T(8,128)(2,1)}, u32[]{:S(2)}) copy-start(bf16[1024,256]{1,0:T(8,128)(2,1)} %param.25) | copy-start | bytes 1572868
Sparse Core Ops, SparseCore 0:
  57.0 84.1 reduce-scatter.1
